TPU v7x, 128 devices: a whole 4x4x4 slice. The times are simulated.
128 devices in a mesh: fsdp: 16 (over z, x_lo, core), seq: 8 (over x_hi, y).
Axes of the slice: x: 4 (x_hi: 2, x_lo: 2; x = x_hi * 2 + x_lo), y: 4, z: 4, core: 2. Of those that a mesh axis runs over, the one named last changes fastest.
Arguments:
- hidden_in: bfloat16 [64, 5, 1536], P('fsdp'), may hold values from -6 to 6
- norm_gain: float32 [1536], replicated, may hold values from 0.1 to 1.9
- w_qkv: bfloat16 [1536, 3, 24, 64], P(None, None, 'seq', 'fsdp'), may hold values from -0.15625 to 0.15625
- w_forget: bfloat16 [1536, 24], replicated, may hold values from -0.15625 to 0.15625
- forget_bias: float32 [24], replicated, may hold values from 1 to 5
- cache_keys: bfloat16 [64, 4096, 1536], P('fsdp', 'seq')
- cache_values: bfloat16 [64, 4096, 1536], P('fsdp', 'seq'), may hold values from -6 to 6
- cache_forget: float32 [64, 24, 4096], P('fsdp', None, 'seq')
- cache_lengths: int32 [64], P('fsdp'), may hold values from 128 to 4096, as said below
- piece_map: int32 [64, 8], P('fsdp'), may hold values from 0 to 7, each once within a row
- draft_counts: int32 [64], P('fsdp'), may hold values from 1 to 4
Outputs:
- verified: bfloat16 [64, 5, 1536], P('fsdp', None, 'seq')
Inputs may be any that keep to these rules, and one draw needn't show every extreme that they name: `cache_lengths`: 16 requests drawn at random have lengths from 3841 to 4096, one exactly 4096; the others have lengths from 128 to 256, one exactly 128.
All inputs are finite; a program needn't handle non-finite values.
Results may differ from a plain program's by a relative error of at most 0.012.
The roundings to bfloat16 on the way count: a program that leaves them out, or rounds other values in their place, can miss the bound.
Values may be sent and summed in bfloat16 or wider, within the bound.
No kernel may reach another device: no remote copies, remote signals or barrier semaphores. Data moves between devices by JAX's collectives and lax.ppermute only.
A program may use at most 128 MiB of HBM per device.

v0:
```python
import jax
import jax.numpy as jnp
from jax import lax
from jax.sharding import PartitionSpec as P

HEAD_DIM = 64


norm_eps = 1e-06
neg_fill = -1e30


def normalize(rows, gain):
    values = rows.astype(jnp.float32)
    mean_sq = jnp.mean(values * values, axis=-1, keepdims=True)
    return (values * lax.rsqrt(mean_sq + norm_eps) * gain).astype(jnp.bfloat16)


def fold_parts(parts):
    maxima, sums, accums = parts
    joint = jnp.max(maxima, axis=0)
    factor = jnp.exp(maxima - joint[None])
    return (joint, jnp.sum(sums * factor, axis=0), jnp.sum(accums * factor[..., None], axis=0))


def body(
    hidden_in,
    norm_gain,
    w_qkv,
    w_forget,
    forget_bias,
    cache_keys,
    cache_values,
    cache_forget,
    cache_lengths,
    piece_map,
    draft_counts,
):
    req_count, new_count, width = hidden_in.shape
    head_count = w_forget.shape[1]
    seq_count = lax.axis_size("seq")
    own_heads = w_qkv.shape[2]
    own_width = own_heads * HEAD_DIM
    piece_len = cache_forget.shape[2]
    logit_scale = HEAD_DIM ** (-0.5)
    seq_index = lax.axis_index("seq")
    head_start = seq_index * own_heads
    normed = normalize(hidden_in, norm_gain).reshape(req_count * new_count, width)
    gate_logit = (
        jnp.dot(normed, w_forget, preferred_element_type=jnp.float32).reshape(
            req_count, new_count, head_count
        )
        + forget_bias
    )
    prefix = jnp.cumsum(jax.nn.log_sigmoid(gate_logit), axis=1)
    projected = jnp.einsum(
        "nd,dchk->nchk",
        normed,
        lax.all_gather(w_qkv, "fsdp", axis=3, tiled=True),
        preferred_element_type=jnp.float32,
    ).astype(jnp.bfloat16)
    own_part = projected.reshape(req_count * new_count, 3, own_width)
    all_heads = lax.all_gather(own_part, "seq", axis=2, tiled=True).reshape(
        req_count, new_count, 3, head_count, HEAD_DIM
    )
    query_rows_all = all_heads[:, :, 0]
    slot_ids = jnp.arange(seq_count, dtype=jnp.int32)
    holders = piece_map[:, :, None] == slot_ids[None, None, :]
    piece_of_slot = jnp.sum(jnp.where(holders, slot_ids[None, :, None], 0), axis=1)
    own_piece = jnp.sum(jnp.where(piece_map == seq_index, slot_ids[None, :], 0), axis=1)
    positions = own_piece[:, None] * piece_len + jnp.arange(piece_len, dtype=jnp.int32)[None, :]
    live_mask = positions < cache_lengths[:, None]
    masked = jnp.where(live_mask[:, None, :], cache_forget, 0.0)
    piece_total = jnp.sum(masked, axis=-1)
    all_totals = lax.all_gather(piece_total[None], "seq", axis=0, tiled=True)
    later_piece = (piece_of_slot.T > own_piece[None, :])[:, :, None]
    later_sum = jnp.sum(jnp.where(later_piece, all_totals, 0.0), axis=0)
    trailing_part = piece_total[..., None] - jnp.cumsum(masked, axis=-1) + later_sum[..., None]
    key_rows = cache_keys.reshape(req_count, piece_len, head_count, HEAD_DIM)
    value_rows = cache_values.reshape(req_count, piece_len, head_count, HEAD_DIM)
    prefix_transposed = jnp.transpose(prefix, (0, 2, 1))
    scores = (
        jnp.einsum("rmhd,rthd->rhmt", query_rows_all, key_rows, preferred_element_type=jnp.float32)
        * logit_scale
    )
    scores = scores + trailing_part[:, :, None, :] + prefix_transposed[..., None]
    key_live = live_mask[:, None, None, :]
    row_max = jnp.max(jnp.where(key_live, scores, neg_fill), axis=-1)
    attn_weights = jnp.where(key_live, jnp.exp(scores - row_max[..., None]), 0.0)
    weight_sum = jnp.sum(attn_weights, axis=-1)
    accum = jnp.einsum(
        "rhmt,rthd->rhmd",
        attn_weights.astype(jnp.bfloat16),
        value_rows,
        preferred_element_type=jnp.float32,
    )
    gathered = (
        lax.all_gather(row_max[None], "seq", axis=0, tiled=True),
        lax.all_gather(weight_sum[None], "seq", axis=0, tiled=True),
        lax.all_gather(accum[None], "seq", axis=0, tiled=True),
    )
    own_parts = tuple(
        (lax.dynamic_slice_in_dim(member, head_start, own_heads, 2) for member in gathered)
    )
    cache_max, cache_sum, cache_acc = fold_parts(own_parts)
    own_rows = own_part.reshape(req_count, new_count, 3, own_heads, HEAD_DIM)
    own_prefix = jnp.transpose(
        lax.dynamic_slice_in_dim(prefix, head_start, own_heads, 2), (0, 2, 1)
    )
    fresh_logits = (
        jnp.einsum(
            "rmhd,rnhd->rhmn",
            own_rows[:, :, 0],
            own_rows[:, :, 1],
            preferred_element_type=jnp.float32,
        )
        * logit_scale
    )
    fresh_logits = fresh_logits + own_prefix[..., :, None] - own_prefix[..., None, :]
    step_ids = jnp.arange(new_count, dtype=jnp.int32)
    causal = (step_ids[None, :] <= step_ids[:, None])[None, None]
    joint_max = jnp.maximum(cache_max, jnp.max(jnp.where(causal, fresh_logits, neg_fill), axis=-1))
    new_weights = jnp.where(causal, jnp.exp(fresh_logits - joint_max[..., None]), 0.0)
    carried = jnp.exp(cache_max - joint_max)
    total_sum = cache_sum * carried + jnp.sum(new_weights, axis=-1)
    blend_weights = cache_acc * carried[..., None] + jnp.einsum(
        "rhmn,rnhd->rhmd",
        new_weights.astype(jnp.bfloat16),
        own_rows[:, :, 2],
        preferred_element_type=jnp.float32,
    )
    result = blend_weights / total_sum[..., None]
    live_rows = (step_ids[None, :] <= draft_counts[:, None])[:, None, :, None]
    result = jnp.where(live_rows, result, 0.0)
    return (
        jnp.transpose(result, (0, 2, 1, 3))
        .reshape(req_count, new_count, own_heads * HEAD_DIM)
        .astype(jnp.bfloat16)
    )


def solution(mesh):
    in_specs = (
        P("fsdp", None, None),
        P(),
        P(None, None, "seq", "fsdp"),
        P(),
        P(),
        P("fsdp", "seq", None),
        P("fsdp", "seq", None),
        P("fsdp", None, "seq"),
        P("fsdp"),
        P("fsdp", None),
        P("fsdp"),
    )
    out_specs = P("fsdp", None, "seq")
    return jax.shard_map(body, mesh=mesh, in_specs=in_specs, out_specs=out_specs, check_vma=False)
```

profile of v0, /device:TPU:0, one launch (start us, length us, event | category | flops | bytes accessed | tf_op | source)
XLA Modules:
  0.0 235.4 jit_solution(12560561197507895507)
XLA Ops:
  6.5 0.0 copy-start
  6.5 0.0 all-gather.7.cloned.1.call-start
  6.5 1.6 copy.152
  8.2 0.0 all-gather.7.cloned.1.call-update
  8.2 0.9 fusion.14
  9.2 0.9 fusion.16
  10.1 0.0 copy-done
  10.1 0.8 fusion.34
  11.0 0.1 dynamic-slice_bitcast_fusion
  11.1 0.1 copy.171
  11.2 0.1 copy.172
  11.4 0.8 select_reduce_fusion.5
  12.2 0.8 select_reduce_fusion.4
  12.9 0.1 compare_bitcast_fusion
  13.0 0.1 copy.161
  13.1 0.7 add_compare_fusion
  13.8 1.0 select_reduce_fusion.1
  14.9 4.6 %reduce-window.6 = f32[4,24,4,128]{3,1,2,0:T(8,128)S(1)} reduce-window(f32[4,24,4,128]{3,1,2,0:T(8,128)S(1)} %bitcast.84, f32[]{:T(128)} %constant.8.clone.1), window={size=1x1x1x128 pad=0_0x0_0x0_0x127_0}, to_apply=%region_3.4 | reduce-window | flops 6242304 | bytes 393220 | tf_op jit(solution)/shard_map/reduce-window
  19.5 0.2 slice_reduce_fusion
  19.8 0.1 copy.162
  19.9 8.8 %copy.158 = bf16[4,512,1536]{1,2,0:T(8,128)(2,1)} copy(bf16[4,512,1536]{2,1,0:T(8,128)(2,1)} %param.16) | data formatting | bytes 12582912 | tf_op args[5]
  28.7 0.0 copy-start.1
  28.7 8.7 %copy.163 = bf16[4,512,1536]{1,2,0:T(8,128)(2,1)} copy(bf16[4,512,1536]{2,1,0:T(8,128)(2,1)} %param.17) | data formatting | bytes 12582912 | tf_op args[6]
  37.4 30.2 %all-gather.4 = f32[8,4,24]{2,1,0:T(4,128)S(1)} all-gather(f32[1,4,24]{2,1,0:T(4,128)S(1)} %bitcast.88), channel_id=2, replica_groups=mesh['fsdp'=16,'seq'=8] {'seq'}, dimensions={0}, use_global_device_ids=true | all-gather | bytes 3456 | tf_op jit(solution)/shard_map/all_gather | solution.py:75
  67.6 0.1 select_reduce_fusion.3
  67.7 0.0 copy-done.1
  67.8 0.1 fusion.13
  67.9 0.0 all-gather.7.cloned.1.call-done
  67.9 2.4 %fusion.4 = bf16[20,3,3,64]{3,0,2,1:T(8,128)(2,1)S(1)} fusion(bf16[1536,3,3,64]{0,2,1,3:T(4,128)(2,1)} %all-gather.7.cloned.1.call-done, bf16[20,1536,1,1]{1,0,2,3:T(8,128)(2,1)S(1)} %reshape.189), kind=kOutput, calls=%fused_computation.7 | convolution fusion | flops 35400960 | bytes 1853952 | tf_op jit(solution)/shard_map/nd,dchk->nchk/dot_general | solution.py:56
  70.4 0.2 copy.188
  70.6 0.1 fusion.21
  70.8 0.2 copy.170
  70.9 0.2 select_reduce_fusion.2
  71.1 0.1 copy.177
  71.2 0.1 copy.174
  71.3 38.0 %all_gather.19 = bf16[20,3,1536]{0,1,2:T(4,128)(2,1)S(1)} all-gather(bf16[20,3,192]{0,1,2:T(4,128)(2,1)S(1)} %bitcast.83), channel_id=1, replica_groups=mesh['fsdp'=16,'seq'=8] {'seq'}, dimensions={2}, use_global_device_ids=true | all-gather | bytes 207360 | tf_op jit(solution)/shard_map/all_gather | solution.py:63
  109.3 0.9 copy.156
  110.2 0.2 reshape.177
  110.5 3.9 %select_reduce_fusion = (f32[4,24,5]{2,1,0:T(8,128)S(1)}, f32[4,24,5,512]{3,2,1,0:T(8,128)S(1)}) fusion(pred[4,512]{1,0:T(4,128)(4,1)S(1)} %add_compare_fusion, f32[4,24,5]{2,1,0:T(8,128)S(1)} %copy.162, f32[4,24,512]{2,1,0:T(8,128)S(1)} %fusion.13, bf16[4,512,24,64]{1,3,2,0:T(8,128)(2,1)} %bitcast.78, bf16[4,5,1,24,64]{4,3,1,0,2:T(8,128)(2,1)S(1)} %slice.24), kind=kOutput, calls=%fused_computation.3 | convolution fusion | flops 32685600 | bytes 7538432 | tf_op jit(solution)/shard_map/rmhd,rthd->rhmt/dot_general | solution.py:83
  114.3 0.1 copy.165
  114.4 0.5 fusion.2
  114.9 0.1 copy.182
  115.0 34.2 %all-gather.3 = f32[32,24,5]{1,2,0:T(8,128)S(1)} all-gather(f32[4,24,5]{1,2,0:T(8,128)S(1)} %copy.182), channel_id=5, replica_groups=mesh['fsdp'=16,'seq'=8] {'seq'}, dimensions={0}, use_global_device_ids=true | all-gather | bytes 17280 | tf_op jit(solution)/shard_map/all_gather | solution.py:99
  149.2 34.2 %all-gather.2 = f32[32,24,5]{1,2,0:T(8,128)S(1)} all-gather(f32[4,24,5]{1,2,0:T(8,128)S(1)} %copy.165), channel_id=4, replica_groups=mesh['fsdp'=16,'seq'=8] {'seq'}, dimensions={0}, use_global_device_ids=true | all-gather | bytes 17280 | tf_op jit(solution)/shard_map/all_gather | solution.py:98
  183.4 0.1 dynamic-slice_reduce_fusion
  183.6 0.1 copy.176
  183.7 0.1 multiply_reduce_fusion.1
  183.8 0.1 copy.178
  183.9 0.2 fusion.37
  184.1 0.1 copy.184
  184.3 0.1 copy.175
  184.4 0.1 copy.185
  184.5 4.6 %fusion.8 = f32[4,24,5,64]{3,2,1,0:T(8,128)S(1)} fusion(bf16[4,512,24,64]{1,3,2,0:T(8,128)(2,1)} %bitcast.79, f32[4,24,5,512]{3,2,1,0:T(8,128)S(1)} %get-tuple-element.19, f32[4,24,5]{2,1,0:T(8,128)S(1)} %get-tuple-element.18, pred[4,512]{1,0:T(4,128)(4,1)S(1)} %add_compare_fusion), kind=kOutput, calls=%fused_computation.10 | convolution fusion | flops 32194560 | bytes 7401344 | tf_op jit(solution)/shard_map/rhmt,rthd->rhmd/dot_general | solution.py:91
  189.1 0.1 copy.164
  189.1 38.2 %all-gather.1 = f32[32,24,5,64]{3,1,2,0:T(8,128)S(1)} all-gather(f32[4,24,5,64]{3,1,2,0:T(8,128)S(1)} %copy.164), channel_id=3, replica_groups=mesh['fsdp'=16,'seq'=8] {'seq'}, dimensions={0}, use_global_device_ids=true | all-gather | bytes 1105920 | tf_op jit(solution)/shard_map/all_gather | solution.py:100
  227.4 0.3 multiply_reduce_fusion
  227.6 0.1 fusion.20
  227.8 0.1 select_convert_fusion
  227.9 0.7 convert_element_type.27
  (17 shorter events, 0.3 us)
Async XLA Ops:
  6.5 3.6 %copy-start = (bf16[1536,24]{0,1:T(8,128)(2,1)S(1)}, bf16[1536,24]{0,1:T(8,128)(2,1)}, u32[]{:S(2)}) copy-start(bf16[1536,24]{0,1:T(8,128)(2,1)} %param.14) | copy-start | bytes 221188
  6.5 61.4 %all-gather.7.cloned.1.call-start = ((), (), s32[]{:S(2)}) async-start(), calls=%async_computation | async-start | bytes 2506752 | tf_op jit(solution)/shard_map/all_gather | solution.py:59
  28.7 39.0 %copy-start.1 = (s32[4]{0:T(128)S(1)}, s32[4]{0:T(128)}, u32[]{:S(2)}) copy-start(s32[4]{0:T(128)} %param.21) | copy-start | bytes 52
Sparse Core Ops, SparseCore 0:
  9.1 37.0 all-gather.6
where the time goes:
time: 236 us; the launch traced here: 235 us
  blocking collectives  175 us (74%)
  local copies, waits for them, and re-layouts  23.3 us (10%)
  between operations  13.6 us (6%)
  matrix products  12 us (5%)
  other arithmetic  11.7 us (5%)
    all_gather x1, blocking collectives, body(): lax.all_gather(accum[None], 'seq', axis=0, tiled=True)  38.2 us
    all_gather x1, blocking collectives, body(): lax.all_gather(own_part, 'seq', axis=2, tiled=True)  38 us
    all_gather x1, blocking collectives, body(): lax.all_gather(row_max[None], 'seq', axis=0, tiled=True)  34.2 us
    all_gather x1, blocking collectives, body(): lax.all_gather(weight_sum[None], 'seq', axis=0, tiled=True)  34.2 us
    all_gather x1, blocking collectives, body(): all_totals = lax.all_gather(piece_total[None], 'seq', axis=0, tiled=True)  30.2 us
    unnamed x7, local copies, waits for them, and re-layouts  19.1 us
  transfers between devices with their start and end apart: 1, of which 0 were waited for; matrix products, arithmetic and copies ran while one was open for 12% of the time, Pallas kernels for 0%

commit v1 on v0

--- a/solution.py
+++ b/solution.py
@@ -14,13 +14,6 @@
     values = rows.astype(jnp.float32)
     mean_sq = jnp.mean(values * values, axis=-1, keepdims=True)
     return (values * lax.rsqrt(mean_sq + norm_eps) * gain).astype(jnp.bfloat16)
-
-
-def fold_parts(parts):
-    maxima, sums, accums = parts
-    joint = jnp.max(maxima, axis=0)
-    factor = jnp.exp(maxima - joint[None])
-    return (joint, jnp.sum(sums * factor, axis=0), jnp.sum(accums * factor[..., None], axis=0))
 
 
 def body(
@@ -60,10 +53,13 @@
         preferred_element_type=jnp.float32,
     ).astype(jnp.bfloat16)
     own_part = projected.reshape(req_count * new_count, 3, own_width)
-    all_heads = lax.all_gather(own_part, "seq", axis=2, tiled=True).reshape(
-        req_count, new_count, 3, head_count, HEAD_DIM
+    own_query = jnp.broadcast_to(own_part[None, :, 0], (seq_count, req_count * new_count, own_width))
+    query_blocks = lax.all_to_all(own_query, "seq", 0, 0, tiled=True)
+    query_rows_all = (
+        query_blocks.reshape(seq_count, req_count, new_count, own_heads, HEAD_DIM)
+        .transpose(1, 2, 0, 3, 4)
+        .reshape(req_count, new_count, head_count, HEAD_DIM)
     )
-    query_rows_all = all_heads[:, :, 0]
     slot_ids = jnp.arange(seq_count, dtype=jnp.int32)
     holders = piece_map[:, :, None] == slot_ids[None, None, :]
     piece_of_slot = jnp.sum(jnp.where(holders, slot_ids[None, :, None], 0), axis=1)
@@ -72,10 +68,7 @@
     live_mask = positions < cache_lengths[:, None]
     masked = jnp.where(live_mask[:, None, :], cache_forget, 0.0)
     piece_total = jnp.sum(masked, axis=-1)
-    all_totals = lax.all_gather(piece_total[None], "seq", axis=0, tiled=True)
-    later_piece = (piece_of_slot.T > own_piece[None, :])[:, :, None]
-    later_sum = jnp.sum(jnp.where(later_piece, all_totals, 0.0), axis=0)
-    trailing_part = piece_total[..., None] - jnp.cumsum(masked, axis=-1) + later_sum[..., None]
+    trailing_part = piece_total[..., None] - jnp.cumsum(masked, axis=-1)
     key_rows = cache_keys.reshape(req_count, piece_len, head_count, HEAD_DIM)
     value_rows = cache_values.reshape(req_count, piece_len, head_count, HEAD_DIM)
     prefix_transposed = jnp.transpose(prefix, (0, 2, 1))
@@ -94,15 +87,30 @@
         value_rows,
         preferred_element_type=jnp.float32,
     )
-    gathered = (
-        lax.all_gather(row_max[None], "seq", axis=0, tiled=True),
-        lax.all_gather(weight_sum[None], "seq", axis=0, tiled=True),
-        lax.all_gather(accum[None], "seq", axis=0, tiled=True),
+    packed = jnp.concatenate(
+        [
+            accum,
+            row_max[..., None],
+            weight_sum[..., None],
+            jnp.broadcast_to(piece_total[:, :, None, None], (req_count, head_count, new_count, 1)),
+        ],
+        axis=-1,
     )
-    own_parts = tuple(
-        (lax.dynamic_slice_in_dim(member, head_start, own_heads, 2) for member in gathered)
+    packed = packed.reshape(req_count, seq_count, own_heads, new_count, HEAD_DIM + 3).transpose(
+        1, 0, 2, 3, 4
     )
-    cache_max, cache_sum, cache_acc = fold_parts(own_parts)
+    parts = lax.all_to_all(packed, "seq", 0, 0, tiled=True)
+    part_acc = parts[..., :HEAD_DIM]
+    part_max = parts[..., HEAD_DIM]
+    part_sum = parts[..., HEAD_DIM + 1]
+    part_total = parts[..., 0, HEAD_DIM + 2]
+    later_piece = (piece_of_slot.T[None, :, :] > piece_of_slot.T[:, None, :])[..., None]
+    later_sum = jnp.sum(jnp.where(later_piece, part_total[None], 0.0), axis=1)
+    part_max = part_max + later_sum[..., None]
+    cache_max = jnp.max(part_max, axis=0)
+    factor = jnp.exp(part_max - cache_max[None])
+    cache_sum = jnp.sum(part_sum * factor, axis=0)
+    cache_acc = jnp.sum(part_acc * factor[..., None], axis=0)
     own_rows = own_part.reshape(req_count, new_count, 3, own_heads, HEAD_DIM)
     own_prefix = jnp.transpose(
         lax.dynamic_slice_in_dim(prefix, head_start, own_heads, 2), (0, 2, 1)

time: 236 us -> 99.1 us (0.42)
  blocking collectives: 175 us -> 0 us
  waiting for transfers between devices: 0.04 us -> 25.1 us
  starting transfers between devices: 0.01 us -> 9.94 us
    all_gather x5 -> x0, blocking collectives: 175 us -> none  [the longest x1 38.2 us: body(): lax.all_gather(accum[None], 'seq', axis=0, tiled=True)]
    all_to_all x0 -> x2, waiting for transfers between devices: none -> 16 us  [the longest x1 8.42 us: body(): parts = lax.all_to_all(packed, 'seq', 0, 0, tiled=True)]
    all_to_all x0 -> x2, starting transfers between devices: none -> 9.94 us  [the longest x1 6.53 us: body(): query_blocks = lax.all_to_all(own_query, 'seq', 0, 0, tiled=True)]
    all_gather x1, waiting for transfers between devices: 0.02 us -> 9.07 us  [body(): lax.all_gather(w_qkv, 'fsdp', axis=3, tiled=True)]
    unnamed x7 -> x10, local copies, waits for them, and re-layouts: 19.1 us -> 19.5 us
  transfers between devices with their start and end apart: 1 -> 3, of which waited for: 0 -> 3; matrix products, arithmetic and copies ran while one was open for 12% -> 30% of each run, Pallas kernels for 0% -> 0%
where the time goes in v1:
time: 99.1 us; the launch traced here: 98.2 us
  local copies, waits for them, and re-layouts  25.3 us (26%)
  waiting for transfers between devices  25.1 us (25%)
  between operations  13.7 us (14%)
  other arithmetic  12.2 us (12%)
  matrix products  12 us (12%)
  starting transfers between devices  9.94 us (10%)
    unnamed x10, local copies, waits for them, and re-layouts  19.5 us
    all_gather x1, waiting for transfers between devices, body(): lax.all_gather(w_qkv, 'fsdp', axis=3, tiled=True)  9.07 us
    all_to_all x1, waiting for transfers between devices, body(): parts = lax.all_to_all(packed, 'seq', 0, 0, tiled=True)  8.42 us
    all_to_all x1, waiting for transfers between devices, body(): query_blocks = lax.all_to_all(own_query, 'seq', 0, 0, tiled=True)  7.63 us
    all_to_all x1, starting transfers between devices, body(): query_blocks = lax.all_to_all(own_query, 'seq', 0, 0, tiled=True)  6.53 us
    another operation x2, other arithmetic  4.65 us
    dot_general x1, matrix products, body(): jnp.einsum('rhmt,rthd->rhmd', attn_weights.astype(jnp.bfloat16), value_ro...  4.56 us
    dot_general x1, matrix products, body(): jnp.einsum('rmhd,rthd->rhmt', query_rows_all, key_rows, preferred_element...  3.88 us
  transfers between devices with their start and end apart: 3, of which 3 were waited for; matrix products, arithmetic and copies ran while one was open for 30% of the time, Pallas kernels for 0%

profile of v1, /device:TPU:0, one launch (start us, length us, event | category | flops | bytes accessed | tf_op | source)
XLA Modules:
  0.0 98.2 jit_solution(2293794967212627305)
XLA Ops:
  6.5 0.0 copy-start
  6.5 0.0 all-gather.2.cloned.1.call-start
  6.5 1.6 %copy.217 = bf16[1536,3,3,4]{0,2,1,3:T(4,128)(2,1)} copy(bf16[1536,3,3,4]{0,3,2,1:T(4,128)(2,1)} %param.13) | data formatting | bytes 221184 | tf_op args[2]
  8.2 0.0 all-gather.2.cloned.1.call-update
  8.2 0.9 fusion.14
  9.2 0.9 fusion.16
  10.1 0.0 copy-done
  10.1 0.8 fusion.38
  11.0 0.1 dynamic-slice_bitcast_fusion
  11.1 0.1 copy.245
  11.2 0.1 copy.246
  11.4 0.8 select_reduce_fusion.5
  12.2 0.7 add_compare_fusion
  12.9 1.0 %select_bitcast_fusion = (f32[4,3,4,8,128]{4,3,2,1,0:T(8,128)S(1)}, f32[4,24]{1,0:T(4,128)S(1)}) fusion(f32[4,24,512]{2,1,0:T(8,128)} %param.18, pred[4,512]{1,0:T(4,128)(4,1)S(1)} %add_compare_fusion), kind=kLoop, calls=%fused_computation.21 | loop fusion | flops 98208 | bytes 395648
  13.9 4.6 %reduce-window.6 = f32[4,24,4,128]{3,1,2,0:T(8,128)S(1)} reduce-window(f32[4,24,4,128]{3,1,2,0:T(8,128)S(1)} %bitcast.95, f32[]{:T(128)} %constant.8.clone.1), window={size=1x1x1x128 pad=0_0x0_0x0_0x127_0}, to_apply=%region_3.4 | reduce-window | flops 6242304 | bytes 393220 | tf_op jit(solution)/shard_map/reduce-window
  18.6 0.2 slice_reduce_fusion
  18.8 0.1 copy.225
  19.0 8.7 %copy.222 = bf16[4,512,1536]{1,2,0:T(8,128)(2,1)} copy(bf16[4,512,1536]{2,1,0:T(8,128)(2,1)} %param.16) | data formatting | bytes 12582912 | tf_op args[5]
  27.7 0.0 copy-start.1
  27.7 0.0 copy-start.2
  27.7 8.7 %copy.226 = bf16[4,512,1536]{1,2,0:T(8,128)(2,1)} copy(bf16[4,512,1536]{2,1,0:T(8,128)(2,1)} %param.17) | data formatting | bytes 12582912 | tf_op args[6]
  36.4 0.1 broadcast_in_dim.168
  36.5 0.1 copy.229
  36.6 0.0 copy-done.1
  36.6 0.1 select_reduce_fusion.4
  36.7 0.0 copy-done.2
  36.7 0.1 broadcast_compare_fusion
  36.8 0.1 bitcast_subtract_fusion
  36.9 9.1 %all-gather.2.cloned.1.call-done = bf16[1536,3,3,64]{0,2,1,3:T(4,128)(2,1)} async-done(((bf16[1536,3,3,4]{0,2,1,3:T(4,128)(2,1)}), bf16[1536,3,3,64]{0,2,1,3:T(4,128)(2,1)}) %all-gather.2.cloned.1.call-update) | async-done | bytes 1769488 | tf_op jit(solution)/shard_map/all_gather | solution.py:52
  46.0 2.4 %fusion.4 = bf16[20,3,3,64]{3,0,2,1:T(8,128)(2,1)S(1)} fusion(bf16[1536,3,3,64]{0,2,1,3:T(4,128)(2,1)} %all-gather.2.cloned.1.call-done, bf16[20,1536,1,1]{1,0,2,3:T(8,128)(2,1)S(1)} %reshape.201), kind=kOutput, calls=%fused_computation.7 | convolution fusion | flops 35400960 | bytes 1853952 | tf_op jit(solution)/shard_map/nd,dchk->nchk/dot_general | solution.py:49
  48.5 0.1 reshape.194
  48.6 0.6 broadcast_in_dim.163
  49.3 6.5 %all-to-all-start = ((bf16[8,20,192]{2,1,0:T(8,128)(2,1)}), bf16[8,20,192]{2,1,0:T(8,128)(2,1)S(1)}, u32[]{:S(2)}, u32[]{:S(2)}) async-start(bf16[8,20,192]{2,1,0:T(8,128)(2,1)} %broadcast_in_dim.163), calls=%async_computation | async-start | bytes 196608 | tf_op jit(solution)/shard_map/all_to_all | solution.py:57
  55.8 0.1 fusion.25
  55.9 0.2 copy.244
  56.1 7.6 %all-to-all-done = bf16[8,20,192]{2,1,0:T(8,128)(2,1)S(1)} async-done(((bf16[8,20,192]{2,1,0:T(8,128)(2,1)}), bf16[8,20,192]{2,1,0:T(8,128)(2,1)S(1)}, u32[]{:S(2)}, u32[]{:S(2)}) %all-to-all-start) | async-done | bytes 61472 | tf_op jit(solution)/shard_map/all_to_all | solution.py:57
  63.8 0.1 reshape.195
  63.9 0.1 copy.221
  63.9 3.9 %select_reduce_fusion = (f32[4,24,5]{2,1,0:T(8,128)S(1)}, f32[4,24,5,512]{3,2,1,0:T(8,128)S(1)}) fusion(pred[4,512]{1,0:T(4,128)(4,1)S(1)} %add_compare_fusion, f32[4,24,5]{2,1,0:T(8,128)S(1)} %copy.225, f32[4,24,512]{2,1,0:T(8,128)S(1)} %bitcast_subtract_fusion, bf16[4,5,24,64]{3,1,2,0:T(8,128)(2,1)S(1)} %bitcast.94, bf16[4,512,24,64]{1,3,2,0:T(8,128)(2,1)} %bitcast.91), kind=kOutput, calls=%fused_computation.3 | convolution fusion | flops 32685600 | bytes 7538432 | tf_op jit(solution)/shard_map/rmhd,rthd->rhmt/dot_general | solution.py:76
  67.9 0.5 fusion.2
  68.4 4.6 %fusion.8 = f32[4,24,5,64]{3,2,1,0:T(8,128)S(1)} fusion(bf16[4,512,24,64]{1,3,2,0:T(8,128)(2,1)} %bitcast.92, f32[4,24,5,512]{3,2,1,0:T(8,128)S(1)} %get-tuple-element.19, f32[4,24,5]{2,1,0:T(8,128)S(1)} %get-tuple-element.18, pred[4,512]{1,0:T(4,128)(4,1)S(1)} %add_compare_fusion), kind=kOutput, calls=%fused_computation.10 | convolution fusion | flops 32194560 | bytes 7401344 | tf_op jit(solution)/shard_map/rhmt,rthd->rhmd/dot_general | solution.py:84
  72.9 0.2 copy.230
  73.1 0.7 copy.232
  73.8 0.7 copy.231
  74.5 0.1 broadcast_in_dim.169
  74.7 1.1 %maximum_bitcast_fusion = f32[8,4,3,5,67]{4,1,3,2,0:T(4,128)} fusion(f32[4,8,3,5,1]{4,0,3,2,1:T(4,128)S(1)} %broadcast_in_dim.169, f32[4,8,3,5,1]{4,0,3,2,1:T(4,128)S(1)} %copy.232, f32[4,8,3,5,1]{4,0,3,2,1:T(4,128)S(1)} %copy.231, f32[4,8,3,5,64]{4,0,3,2,1:T(4,128)S(1)} %copy.230), kind=kLoop, calls=%fused_computation.16 | loop fusion | flops 96480 | bytes 257280 | tf_op jit(solution)/shard_map/transpose | solution.py:99
  75.8 3.4 %all-to-all-start.1 = ((f32[8,4,3,5,67]{4,1,3,2,0:T(4,128)}), f32[8,4,3,5,67]{4,1,3,2,0:T(4,128)S(1)}, u32[]{:S(2)}, u32[]{:S(2)}) async-start(f32[8,4,3,5,67]{4,1,3,2,0:T(4,128)} %maximum_bitcast_fusion), calls=%async_computation.1 | async-start | bytes 491520 | tf_op jit(solution)/shard_map/all_to_all | solution.py:102
  79.2 0.2 select_reduce_fusion.3
  79.4 8.4 %all-to-all-done.1 = f32[8,4,3,5,67]{4,1,3,2,0:T(4,128)S(1)} async-done(((f32[8,4,3,5,67]{4,1,3,2,0:T(4,128)}), f32[8,4,3,5,67]{4,1,3,2,0:T(4,128)S(1)}, u32[]{:S(2)}, u32[]{:S(2)}) %all-to-all-start.1) | async-done | bytes 128672 | tf_op jit(solution)/shard_map/all_to_all | solution.py:102
  87.8 0.3 fusion.44
  88.1 0.4 copy.268
  88.5 0.1 slice.45
  88.7 0.2 copy.264
  88.8 0.1 select_reduce_fusion.2
  88.9 0.4 copy.254
  89.4 0.1 fusion.23
  89.5 0.1 exponential_bitcast_fusion
  89.6 0.2 fusion.22
  89.8 0.2 fusion.41
  90.0 0.2 copy.238
  90.2 0.1 fusion.24
  90.3 0.2 fusion.13
  90.5 0.1 select_convert_fusion
  90.7 0.7 convert_element_type.27
  (24 shorter events, 0.4 us)
Async XLA Ops:
  6.5 3.6 %copy-start = (bf16[1536,24]{0,1:T(8,128)(2,1)S(1)}, bf16[1536,24]{0,1:T(8,128)(2,1)}, u32[]{:S(2)}) copy-start(bf16[1536,24]{0,1:T(8,128)(2,1)} %param.14) | copy-start | bytes 221188
  6.5 39.4 %all-gather.2.cloned.1.call-start = ((), (), s32[]{:S(2)}) async-start(), calls=%async_computation.2 | async-start | bytes 2506752 | tf_op jit(solution)/shard_map/all_gather | solution.py:52
  27.7 8.9 %copy-start.1 = (s32[4,8]{1,0:T(4,128)S(1)}, s32[4,8]{1,0:T(4,128)}, u32[]{:S(2)}) copy-start(s32[4,8]{1,0:T(4,128)} %param.20) | copy-start | bytes 388
  27.7 9.0 %copy-start.2 = (s32[4]{0:T(128)S(1)}, s32[4]{0:T(128)}, u32[]{:S(2)}) copy-start(s32[4]{0:T(128)} %param.21) | copy-start | bytes 52
  49.3 14.5 %all-to-all-start = ((bf16[8,20,192]{2,1,0:T(8,128)(2,1)}), bf16[8,20,192]{2,1,0:T(8,128)(2,1)S(1)}, u32[]{:S(2)}, u32[]{:S(2)}) async-start(bf16[8,20,192]{2,1,0:T(8,128)(2,1)} %broadcast_in_dim.163), calls=%async_computation | async-start | bytes 196608 | tf_op jit(solution)/shard_map/all_to_all | solution.py:57
  75.8 12.0 %all-to-all-start.1 = ((f32[8,4,3,5,67]{4,1,3,2,0:T(4,128)}), f32[8,4,3,5,67]{4,1,3,2,0:T(4,128)S(1)}, u32[]{:S(2)}, u32[]{:S(2)}) async-start(f32[8,4,3,5,67]{4,1,3,2,0:T(4,128)} %maximum_bitcast_fusion), calls=%async_computation.1 | async-start | bytes 491520 | tf_op jit(solution)/shard_map/all_to_all | solution.py:102
Sparse Core Ops, SparseCore 0:
  9.1 36.8 all-gather.1

commit v2 on v1

--- a/solution.py
+++ b/solution.py
@@ -32,12 +32,34 @@
     req_count, new_count, width = hidden_in.shape
     head_count = w_forget.shape[1]
     seq_count = lax.axis_size("seq")
+    fsdp_count = lax.axis_size("fsdp")
     own_heads = w_qkv.shape[2]
-    own_width = own_heads * HEAD_DIM
+    own_dims = w_qkv.shape[3]
     piece_len = cache_forget.shape[2]
     logit_scale = HEAD_DIM ** (-0.5)
     seq_index = lax.axis_index("seq")
     head_start = seq_index * own_heads
+    hidden_all = lax.all_to_all(
+        jnp.broadcast_to(hidden_in[None], (fsdp_count, req_count, new_count, width)),
+        "fsdp",
+        0,
+        0,
+        tiled=True,
+    )
+    normed_all = normalize(hidden_all, norm_gain).reshape(fsdp_count * req_count * new_count, width)
+    projected = jnp.einsum(
+        "nd,dchk->nchk", normed_all, w_qkv, preferred_element_type=jnp.float32
+    ).astype(jnp.bfloat16)
+    projected = projected.reshape(fsdp_count, 1, req_count, new_count, 3, own_heads, own_dims)
+    outgoing = jnp.broadcast_to(
+        projected, (fsdp_count, seq_count, req_count, new_count, 3, own_heads, own_dims)
+    ).reshape(fsdp_count * seq_count, req_count, new_count, 3, own_heads, own_dims)
+    incoming = lax.all_to_all(outgoing, ("fsdp", "seq"), 0, 0, tiled=True)
+    all_heads = (
+        incoming.reshape(fsdp_count, seq_count, req_count, new_count, 3, own_heads, own_dims)
+        .transpose(2, 3, 4, 1, 5, 0, 6)
+        .reshape(req_count, new_count, 3, head_count, HEAD_DIM)
+    )
     normed = normalize(hidden_in, norm_gain).reshape(req_count * new_count, width)
     gate_logit = (
         jnp.dot(normed, w_forget, preferred_element_type=jnp.float32).reshape(
@@ -46,46 +68,43 @@
         + forget_bias
     )
     prefix = jnp.cumsum(jax.nn.log_sigmoid(gate_logit), axis=1)
-    projected = jnp.einsum(
-        "nd,dchk->nchk",
-        normed,
-        lax.all_gather(w_qkv, "fsdp", axis=3, tiled=True),
-        preferred_element_type=jnp.float32,
-    ).astype(jnp.bfloat16)
-    own_part = projected.reshape(req_count * new_count, 3, own_width)
-    own_query = jnp.broadcast_to(own_part[None, :, 0], (seq_count, req_count * new_count, own_width))
-    query_blocks = lax.all_to_all(own_query, "seq", 0, 0, tiled=True)
-    query_rows_all = (
-        query_blocks.reshape(seq_count, req_count, new_count, own_heads, HEAD_DIM)
-        .transpose(1, 2, 0, 3, 4)
-        .reshape(req_count, new_count, head_count, HEAD_DIM)
-    )
     slot_ids = jnp.arange(seq_count, dtype=jnp.int32)
     holders = piece_map[:, :, None] == slot_ids[None, None, :]
     piece_of_slot = jnp.sum(jnp.where(holders, slot_ids[None, :, None], 0), axis=1)
     own_piece = jnp.sum(jnp.where(piece_map == seq_index, slot_ids[None, :], 0), axis=1)
-    positions = own_piece[:, None] * piece_len + jnp.arange(piece_len, dtype=jnp.int32)[None, :]
+    steps = jnp.arange(piece_len, dtype=jnp.int32)
+    positions = own_piece[:, None] * piece_len + steps[None, :]
     live_mask = positions < cache_lengths[:, None]
     masked = jnp.where(live_mask[:, None, :], cache_forget, 0.0)
     piece_total = jnp.sum(masked, axis=-1)
-    trailing_part = piece_total[..., None] - jnp.cumsum(masked, axis=-1)
-    key_rows = cache_keys.reshape(req_count, piece_len, head_count, HEAD_DIM)
-    value_rows = cache_values.reshape(req_count, piece_len, head_count, HEAD_DIM)
+    later_step = (steps[:, None] > steps[None, :]).astype(jnp.float32)
+    trailing_part = jnp.einsum(
+        "rhl,lj->rhj", masked, later_step, precision=lax.Precision.HIGHEST,
+        preferred_element_type=jnp.float32,
+    )
     prefix_transposed = jnp.transpose(prefix, (0, 2, 1))
+    head_eye = jnp.eye(head_count, dtype=jnp.bfloat16)
+    query_rows = jnp.transpose(all_heads[:, :, 0], (0, 2, 1, 3))
+    query_blocks = (
+        query_rows[:, :, :, None, :] * head_eye[None, :, None, :, None]
+    ).reshape(req_count, head_count * new_count, head_count * HEAD_DIM)
     scores = (
-        jnp.einsum("rmhd,rthd->rhmt", query_rows_all, key_rows, preferred_element_type=jnp.float32)
+        jnp.einsum("rnc,rtc->rnt", query_blocks, cache_keys, preferred_element_type=jnp.float32)
         * logit_scale
-    )
+    ).reshape(req_count, head_count, new_count, piece_len)
     scores = scores + trailing_part[:, :, None, :] + prefix_transposed[..., None]
     key_live = live_mask[:, None, None, :]
     row_max = jnp.max(jnp.where(key_live, scores, neg_fill), axis=-1)
     attn_weights = jnp.where(key_live, jnp.exp(scores - row_max[..., None]), 0.0)
     weight_sum = jnp.sum(attn_weights, axis=-1)
-    accum = jnp.einsum(
-        "rhmt,rthd->rhmd",
-        attn_weights.astype(jnp.bfloat16),
-        value_rows,
+    accum_blocks = jnp.einsum(
+        "rnt,rtc->rnc",
+        attn_weights.astype(jnp.bfloat16).reshape(req_count, head_count * new_count, piece_len),
+        cache_values,
         preferred_element_type=jnp.float32,
+    ).reshape(req_count, head_count, new_count, head_count, HEAD_DIM)
+    accum = jnp.sum(
+        accum_blocks * head_eye.astype(jnp.float32)[None, :, None, :, None], axis=3
     )
     packed = jnp.concatenate(
         [
@@ -111,7 +130,7 @@
     factor = jnp.exp(part_max - cache_max[None])
     cache_sum = jnp.sum(part_sum * factor, axis=0)
     cache_acc = jnp.sum(part_acc * factor[..., None], axis=0)
-    own_rows = own_part.reshape(req_count, new_count, 3, own_heads, HEAD_DIM)
+    own_rows = lax.dynamic_slice_in_dim(all_heads, head_start, own_heads, 3)
     own_prefix = jnp.transpose(
         lax.dynamic_slice_in_dim(prefix, head_start, own_heads, 2), (0, 2, 1)
     )

time: 99.1 us -> 148 us (1.49)
  local copies, waits for them, and re-layouts: 25.3 us -> 82.3 us
  between operations: 13.7 us -> 0.5 us
  starting transfers between devices: 9.94 us -> 17.6 us
  other arithmetic: 12.2 us -> 10.7 us
    transpose x1 -> x3, local copies, waits for them, and re-layouts: 0.08 us -> 37.1 us  [the longest x1 37 us: body(): all_heads = incoming.reshape(fsdp_count, seq_count, req_count, new_count,...]
    reshape x4 -> x3, local copies, waits for them, and re-layouts: 0.26 us -> 11.6 us  [the longest x1 7.68 us: body(): all_heads = incoming.reshape(fsdp_count, seq_count, req_count, new_count,...]
    all_to_all x1 -> x2, waiting for transfers between devices: 7.63 us -> 18 us  [the longest x1 9.15 us: body(): incoming = lax.all_to_all(outgoing, ('fsdp', 'seq'), 0, 0, tiled=True)]
    all_gather x1 -> x0, waiting for transfers between devices: 9.07 us -> none  [body(): lax.all_gather(w_qkv, 'fsdp', axis=3, tiled=True)]
    all_to_all x1 -> x2, starting transfers between devices: 6.53 us -> 14.2 us  [the longest x1 7.76 us: body(): incoming = lax.all_to_all(outgoing, ('fsdp', 'seq'), 0, 0, tiled=True)]
    broadcast_in_dim x2 -> x3, local copies, waits for them, and re-layouts: 0.65 us -> 6.73 us  [the longest x2 4.56 us: body(): jnp.broadcast_to(projected, (fsdp_count, seq_count, req_count, new_count,...]
    unnamed x10 -> x40, local copies, waits for them, and re-layouts: 19.5 us -> 13.5 us
    another operation x2 -> x0, other arithmetic: 4.65 us -> none
  transfers between devices with their start and end apart: 3 -> 3, of which waited for: 3 -> 3; matrix products, arithmetic and copies ran while one was open for 30% -> 6% of each run, Pallas kernels for 0% -> 0%
where the time goes in v2:
time: 148 us
  local copies, waits for them, and re-layouts  82.3 us (56%)
  waiting for transfers between devices  25.4 us (17%)
  starting transfers between devices  17.6 us (12%)
  matrix products  11.2 us (8%)
  other arithmetic  10.7 us (7%)
    transpose x1, local copies, waits for them, and re-layouts, body(): all_heads = incoming.reshape(fsdp_count, seq_count, req_count, new_count,...  37 us
    unnamed x40, local copies, waits for them, and re-layouts  13.5 us
    all_to_all x1, waiting for transfers between devices, body(): incoming = lax.all_to_all(outgoing, ('fsdp', 'seq'), 0, 0, tiled=True)  9.15 us
    all_to_all x1, waiting for transfers between devices, body(): lax.all_to_all(jnp.broadcast_to(hidden_in[None], (fsdp_count, req_count,...  8.84 us
    all_to_all x1, starting transfers between devices, body(): incoming = lax.all_to_all(outgoing, ('fsdp', 'seq'), 0, 0, tiled=True)  7.76 us
    reshape x1, local copies, waits for them, and re-layouts, body(): all_heads = incoming.reshape(fsdp_count, seq_count, req_count, new_count,...  7.68 us
    all_to_all x1, waiting for transfers between devices, body(): parts = lax.all_to_all(packed, 'seq', 0, 0, tiled=True)  7.39 us
    all_to_all x1, starting transfers between devices, body(): lax.all_to_all(jnp.broadcast_to(hidden_in[None], (fsdp_count, req_count,...  6.44 us
  transfers between devices with their start and end apart: 3, of which 3 were waited for; matrix products, arithmetic and copies ran while one was open for 6% of the time, Pallas kernels for 0%

profile of v2, /device:TPU:0, one launch (start us, length us, event | category | flops | bytes accessed | tf_op | source)
XLA Modules:
  0.0 147.6 jit_solution(17209757075584089472)
XLA Ops:
  0.1 2.2 %broadcast_in_dim.174 = bf16[16,4,5,1536]{3,1,2,0:T(4,128)(2,1)} broadcast(bf16[4,5,1536]{2,0,1:T(4,128)(2,1)} %param.11), dimensions={1,2,3} | broadcast | bytes 1044480 | tf_op jit(solution)/shard_map/broadcast_in_dim | solution.py:43
  2.2 6.4 %all-to-all-start = ((bf16[16,4,5,1536]{3,1,2,0:T(4,128)(2,1)}), bf16[16,4,5,1536]{3,1,2,0:T(4,128)(2,1)S(1)}, u32[]{:S(2)}, u32[]{:S(2)}) async-start(bf16[16,4,5,1536]{3,1,2,0:T(4,128)(2,1)} %broadcast_in_dim.174), calls=%async_computation | async-start | bytes 1966080 | tf_op jit(solution)/shard_map/all_to_all | solution.py:42
  8.7 0.1 fusion.29
  8.8 0.1 select_reduce_fusion.5
  9.0 0.3 fusion.56
  9.5 0.7 copy.289
  10.2 0.7 copy.288
  11.0 0.7 copy.276
  12.0 0.4 fusion.16
  12.4 0.8 copy.272
  13.2 0.2 mul.127
  13.4 0.4 mul.128
  13.8 0.5 iota_compare_fusion.3
  14.3 0.6 fusion.57
  15.0 0.7 broadcast_compare_fusion
  15.7 8.8 %all-to-all-done = bf16[16,4,5,1536]{3,1,2,0:T(4,128)(2,1)S(1)} async-done(((bf16[16,4,5,1536]{3,1,2,0:T(4,128)(2,1)}), bf16[16,4,5,1536]{3,1,2,0:T(4,128)(2,1)S(1)}, u32[]{:S(2)}, u32[]{:S(2)}) %all-to-all-start) | async-done | bytes 983072 | tf_op jit(solution)/shard_map/all_to_all | solution.py:42
  24.5 0.6 fusion
  25.1 0.6 fusion.2
  25.7 0.3 copy.266
  26.0 0.5 reshape.221
  26.5 0.4 convolution_convert_fusion
  26.9 1.2 broadcast_in_dim.175
  28.1 0.5 copy.313
  28.6 3.3 %broadcast_in_dim.176.clone = bf16[16,8,4,5,3,3,4]{3,6,5,4,2,1,0:T(4,128)(2,1)} broadcast(bf16[16,4,5,3,3,4]{2,5,4,3,1,0:T(4,128)(2,1)S(1)} %copy.313), dimensions={0,2,3,4,5,6} | broadcast | bytes 207360 | tf_op jit(solution)/shard_map/broadcast_in_dim | solution.py:54
  31.9 7.3 %reshape.225 = bf16[128,2,360]{2,1,0:T(2,128)(2,1)} reshape(bf16[128,4,3,3,4,5]{5,4,3,2,1,0:T(4,128)(2,1)} %bitcast.90) | data formatting | bytes 368640
  39.2 7.8 %all-to-all-start.1 = ((bf16[128,2,360]{2,1,0:T(2,128)(2,1)}), bf16[128,2,360]{2,1,0:T(2,128)(2,1)S(1)}, u32[]{:S(2)}, u32[]{:S(2)}) async-start(bf16[128,2,360]{2,1,0:T(2,128)(2,1)} %reshape.225), calls=%async_computation.1 | async-start | bytes 393216 | tf_op jit(solution)/shard_map/all_to_all | solution.py:57
  47.0 0.6 iota_compare_fusion.4
  47.6 9.1 %all-to-all-done.1 = bf16[128,2,360]{2,1,0:T(2,128)(2,1)S(1)} async-done(((bf16[128,2,360]{2,1,0:T(2,128)(2,1)}), bf16[128,2,360]{2,1,0:T(2,128)(2,1)S(1)}, u32[]{:S(2)}, u32[]{:S(2)}) %all-to-all-start.1) | async-done | bytes 184352 | tf_op jit(solution)/shard_map/all_to_all | solution.py:57
  56.7 4.5 %reshape.226 = bf16[128,4,3,3,4,5]{5,4,3,2,1,0:T(4,128)(2,1)} reshape(bf16[128,2,360]{2,1,0:T(2,128)(2,1)S(1)} %all-to-all-done.1) | data formatting | bytes 368640
  61.3 37.0 %copy.304 = bf16[16,8,4,5,3,3,4]{6,0,5,1,4,3,2:T(8,128)(2,1)} copy(bf16[16,8,4,5,3,3,4]{3,6,5,4,2,1,0:T(4,128)(2,1)} %bitcast.91) | data formatting | bytes 368640 | tf_op jit(solution)/shard_map/transpose | solution.py:60
  98.3 7.7 %reshape.219 = bf16[4,5,3,24,64]{4,3,2,1,0:T(8,128)(2,1)S(1)} reshape(bf16[4,5,3,8,3,16,4]{6,5,4,3,2,1,0:T(8,128)(2,1)} %bitcast.89) | data formatting | bytes 368640 | tf_op jit(solution)/shard_map/reshape | solution.py:61
  106.0 0.7 copy-done.2
  106.8 0.4 mul.125
  107.2 2.8 %mul.126 = bf16[4,120,1536]{2,1,0:T(8,128)(2,1)} reshape(bf16[4,24,5,24,64]{4,3,2,1,0:T(8,128)(2,1)S(1)} %mul.125) | data formatting | bytes 2949120 | tf_op jit(solution)/shard_map/mul | solution.py:89
  110.0 1.1 add.121
  111.0 5.6 %select_reduce_fusion = (f32[4,120]{1,0:T(4,128)S(1)}, f32[4,120,512]{2,1,0:T(8,128)S(1)}) fusion(pred[4,512]{1,0:T(4,128)(4,1)S(1)} %add_compare_fusion, f32[4,120]{1,0:T(4,128)S(1)} %add.128, f32[4,120,512]{2,0,1:T(4,128)S(1)} %bitcast.92, bf16[4,512,1536]{2,1,0:T(8,128)(2,1)} %param.16, bf16[4,120,1536]{2,1,0:T(8,128)(2,1)} %mul.126, ...), kind=kOutput, calls=%fused_computation.19 | convolution fusion | flops 756940288 | bytes 10106624 | tf_op jit(solution)/shard_map/rnc,rtc->rnt/dot_general | solution.py:92
  116.7 0.1 concatenate.11
  116.8 0.3 fusion.19
  117.1 0.1 concatenate.12
  117.3 0.7 copy.278
  118.0 0.7 copy.277
  118.7 4.2 %fusion.22 = f32[4,120,1536]{2,1,0:T(8,128)S(1)} fusion(bf16[4,512,1536]{2,1,0:T(8,128)(2,1)} %param.17, f32[4,120,512]{2,1,0:T(8,128)} %copy-done.1, f32[4,120]{1,0:T(4,128)} %copy-done.6, pred[4,512]{1,0:T(4,128)(4,1)S(1)} %add_compare_fusion), kind=kOutput, calls=%fused_computation.23 | convolution fusion | flops 755712000 | bytes 10227584 | tf_op jit(solution)/shard_map/rnt,rtc->rnc/dot_general | solution.py:100
  122.9 3.4 %reshape.220 = f32[4,24,5,24,64]{4,3,2,1,0:T(8,128)} reshape(f32[4,120,1536]{2,1,0:T(8,128)S(1)} %fusion.22) | data formatting | bytes 5898240 | tf_op jit(solution)/shard_map/reshape | solution.py:105
  126.3 4.0 %multiply_reduce_fusion = f32[4,24,5,64]{3,2,1,0:T(8,128)S(1)} fusion(f32[4,24,5,24,64]{4,3,2,1,0:T(8,128)} %reshape.220, f32[24,24]{1,0:T(8,128)} %fusion.57), kind=kLoop, calls=%fused_computation | loop fusion | flops 1443840 | bytes 3074304 | tf_op jit(solution)/shard_map/reduce_sum | solution.py:106
  130.3 0.2 copy.275
  130.6 1.1 maximum_bitcast_fusion
  131.8 3.4 %all-to-all-start.2 = ((f32[8,4,3,5,67]{4,1,3,2,0:T(4,128)}), f32[8,4,3,5,67]{4,1,3,2,0:T(4,128)S(1)}, u32[]{:S(2)}, u32[]{:S(2)}) async-start(f32[8,4,3,5,67]{4,1,3,2,0:T(4,128)} %maximum_bitcast_fusion), calls=%async_computation.2 | async-start | bytes 491520 | tf_op jit(solution)/shard_map/all_to_all | solution.py:121
  135.2 1.0 constant_dynamic-slice_fusion
  136.2 0.1 fusion.42
  136.3 0.2 copy.287
  136.5 0.2 select_reduce_fusion.3
  136.7 7.4 %all-to-all-done.2 = f32[8,4,3,5,67]{4,1,3,2,0:T(4,128)S(1)} async-done(((f32[8,4,3,5,67]{4,1,3,2,0:T(4,128)}), f32[8,4,3,5,67]{4,1,3,2,0:T(4,128)S(1)}, u32[]{:S(2)}, u32[]{:S(2)}) %all-to-all-start.2) | async-done | bytes 128672 | tf_op jit(solution)/shard_map/all_to_all | solution.py:121
  144.1 0.3 fusion.64
  144.4 0.4 copy.308
  144.9 0.2 copy.305
  145.1 0.1 select_reduce_fusion.2
  145.4 0.2 fusion.61
  145.6 0.2 copy.284
  145.8 0.4 copy.296
  146.2 0.2 fusion.38
  146.5 0.1 fusion.41
  146.6 0.2 fusion.27
  146.8 0.1 select_convert_fusion
  147.0 0.7 convert_element_type.58
  (60 shorter events, 1.2 us)
Async XLA Ops:
  0.0 26.5 %copy-start = (bf16[1536,3,3,4]{0,3,2,1:T(4,128)(2,1)S(1)}, bf16[1536,3,3,4]{0,3,2,1:T(4,128)(2,1)}, u32[]{:S(2)}) copy-start(bf16[1536,3,3,4]{0,3,2,1:T(4,128)(2,1)} %param.13) | copy-start | bytes 331780
  0.0 8.7 %copy-start.3 = (bf16[4,5,1536]{2,0,1:T(4,128)(2,1)S(1)}, bf16[4,5,1536]{2,0,1:T(4,128)(2,1)}, u32[]{:S(2)}) copy-start(bf16[4,5,1536]{2,0,1:T(4,128)(2,1)} %param.11) | copy-start | bytes 184324
  0.0 8.8 %copy-start.11 = (s32[4,8]{1,0:T(4,128)S(1)}, s32[4,8]{1,0:T(4,128)}, u32[]{:S(2)}) copy-start(s32[4,8]{1,0:T(4,128)} %param.20) | copy-start | bytes 388
  0.0 8.9 %copy-start.10 = (f32[1536]{0:T(1024)S(1)}, f32[1536]{0:T(1024)}, u32[]{:S(2)}) copy-start(f32[1536]{0:T(1024)} %param.12) | copy-start | bytes 18436
  0.0 8.9 %copy-start.16 = (f32[24]{0:T(128)S(1)}, f32[24]{0:T(128)}, u32[]{:S(2)}) copy-start(f32[24]{0:T(128)} %param.15) | copy-start | bytes 292
  0.0 8.9 %copy-start.15 = (bf16[1536,24]{0,1:T(8,128)(2,1)S(1)}, bf16[1536,24]{0,1:T(8,128)(2,1)}, u32[]{:S(2)}) copy-start(bf16[1536,24]{0,1:T(8,128)(2,1)} %param.14) | copy-start | bytes 221188
  0.0 9.2 %copy-start.14 = (s32[4]{0:T(128)S(1)}, s32[4]{0:T(128)}, u32[]{:S(2)}) copy-start(s32[4]{0:T(128)} %param.19) | copy-start | bytes 52
  0.0 9.3 %copy-start.4 = (f32[4,24,512]{2,1,0:T(8,128)S(1)}, f32[4,24,512]{2,1,0:T(8,128)}, u32[]{:S(2)}) copy-start(f32[4,24,512]{2,1,0:T(8,128)} %param.18) | copy-start | bytes 589828
  2.2 22.3 %all-to-all-start = ((bf16[16,4,5,1536]{3,1,2,0:T(4,128)(2,1)}), bf16[16,4,5,1536]{3,1,2,0:T(4,128)(2,1)S(1)}, u32[]{:S(2)}, u32[]{:S(2)}) async-start(bf16[16,4,5,1536]{3,1,2,0:T(4,128)(2,1)} %broadcast_in_dim.174), calls=%async_computation | async-start | bytes 1966080 | tf_op jit(solution)/shard_map/all_to_all | solution.py:42
  31.9 15.0 %copy-start.17 = (s32[4]{0:T(128)S(1)}, s32[4]{0:T(128)}, u32[]{:S(2)}) copy-start(s32[4]{0:T(128)} %param.21) | copy-start | bytes 52
  39.2 17.5 %all-to-all-start.1 = ((bf16[128,2,360]{2,1,0:T(2,128)(2,1)}), bf16[128,2,360]{2,1,0:T(2,128)(2,1)S(1)}, u32[]{:S(2)}, u32[]{:S(2)}) async-start(bf16[128,2,360]{2,1,0:T(2,128)(2,1)} %reshape.225), calls=%async_computation.1 | async-start | bytes 393216 | tf_op jit(solution)/shard_map/all_to_all | solution.py:57
  106.0 0.7 copy-start.2
  116.7 0.6 copy-start.6
  116.7 1.3 copy-start.1
  126.3 4.2 %copy-start.7 = (f32[4,8,3]{0,2,1:T(4,128)S(1)}, f32[4,8,3]{0,2,1:T(4,128)}, u32[]{:S(2)}) copy-start(f32[4,8,3]{0,2,1:T(4,128)} %copy.276) | copy-start | bytes 1156
  126.3 10.2 %copy-start.5 = (f32[4,3,5]{0,2,1:T(8,128)S(1)}, f32[4,3,5]{0,2,1:T(8,128)}, u32[]{:S(2)}) copy-start(f32[4,3,5]{0,2,1:T(8,128)} %copy.288) | copy-start | bytes 724
  126.3 10.2 %copy-start.8 = (f32[4,3,5]{2,0,1:T(4,128)S(1)}, f32[4,3,5]{2,0,1:T(4,128)}, u32[]{:S(2)}) copy-start(f32[4,3,5]{2,0,1:T(4,128)} %copy.289) | copy-start | bytes 724
  126.3 10.2 %copy-start.12 = (pred[5,5]{1,0:T(8,128)(4,1)S(1)}, pred[5,5]{1,0:T(8,128)(4,1)}, u32[]{:S(2)}) copy-start(pred[5,5]{1,0:T(8,128)(4,1)} %iota_compare_fusion.3) | copy-start | bytes 79
  130.3 14.8 %copy-start.9 = (pred[8,8,4]{1,0,2:T(8,128)(4,1)S(1)}, pred[8,8,4]{1,0,2:T(8,128)(4,1)}, u32[]{:S(2)}) copy-start(pred[8,8,4]{1,0,2:T(8,128)(4,1)} %broadcast_compare_fusion) | copy-start | bytes 772
  130.3 16.5 %copy-start.13 = (pred[4,5]{0,1:T(8,128)(4,1)S(1)}, pred[4,5]{0,1:T(8,128)(4,1)}, u32[]{:S(2)}) copy-start(pred[4,5]{0,1:T(8,128)(4,1)} %iota_compare_fusion.4) | copy-start | bytes 64
  131.8 12.3 %all-to-all-start.2 = ((f32[8,4,3,5,67]{4,1,3,2,0:T(4,128)}), f32[8,4,3,5,67]{4,1,3,2,0:T(4,128)S(1)}, u32[]{:S(2)}, u32[]{:S(2)}) async-start(f32[8,4,3,5,67]{4,1,3,2,0:T(4,128)} %maximum_bitcast_fusion), calls=%async_computation.2 | async-start | bytes 491520 | tf_op jit(solution)/shard_map/all_to_all | solution.py:121

commit v3 on v2

v3 whole, which is shorter than its diff:
```python
import jax
import jax.numpy as jnp
from jax import lax
from jax.sharding import PartitionSpec as P

HEAD_DIM = 64


norm_eps = 1e-06
neg_fill = -1e30


def normalize(rows, gain):
    values = rows.astype(jnp.float32)
    mean_sq = jnp.mean(values * values, axis=-1, keepdims=True)
    return (values * lax.rsqrt(mean_sq + norm_eps) * gain).astype(jnp.bfloat16)


def body(
    hidden_in,
    norm_gain,
    w_qkv,
    w_forget,
    forget_bias,
    cache_keys,
    cache_values,
    cache_forget,
    cache_lengths,
    piece_map,
    draft_counts,
):
    req_count, new_count, width = hidden_in.shape
    head_count = w_forget.shape[1]
    seq_count = lax.axis_size("seq")
    fsdp_count = lax.axis_size("fsdp")
    own_heads = w_qkv.shape[2]
    own_dims = w_qkv.shape[3]
    own_cols = 3 * own_heads * own_dims
    rows = req_count * new_count
    inner_width = head_count * HEAD_DIM
    piece_len = cache_forget.shape[2]
    logit_scale = HEAD_DIM ** (-0.5)
    seq_index = lax.axis_index("seq")
    head_start = seq_index * own_heads
    hidden_all = lax.all_to_all(
        jnp.broadcast_to(hidden_in[None], (fsdp_count, req_count, new_count, width)),
        "fsdp",
        0,
        0,
        tiled=True,
    )
    normed_all = normalize(hidden_all, norm_gain).reshape(fsdp_count * rows, width)
    projected = jnp.einsum(
        "dk,nd->kn",
        w_qkv.reshape(width, own_cols),
        normed_all,
        preferred_element_type=jnp.float32,
    ).astype(jnp.bfloat16)
    outgoing = (
        projected.reshape(3, own_heads * own_dims, fsdp_count, rows)
        .transpose(2, 1, 0, 3)
        .reshape(fsdp_count, 1, own_heads * own_dims * 3 * rows)
    )
    outgoing = jnp.broadcast_to(
        outgoing, (fsdp_count, seq_count, own_heads * own_dims * 3 * rows)
    ).reshape(fsdp_count * seq_count, own_heads * own_dims * 3 * rows)
    incoming = lax.all_to_all(outgoing, ("fsdp", "seq"), 0, 0, tiled=True)
    incoming = incoming.reshape(fsdp_count * seq_count * own_heads * own_dims, 3 * rows)
    src_row = jnp.arange(fsdp_count * seq_count * own_heads * own_dims, dtype=jnp.int32)
    src_dev = src_row // (own_heads * own_dims)
    src_head = (src_row // own_dims) % own_heads
    src_dim = src_row % own_dims
    target = ((src_dev % seq_count) * own_heads + src_head) * HEAD_DIM + (
        src_dev // seq_count
    ) * own_dims + src_dim
    placement = (target[:, None] == jnp.arange(inner_width, dtype=jnp.int32)[None, :]).astype(
        jnp.bfloat16
    )
    all_heads = jnp.einsum(
        "kx,kj->xj", incoming, placement, preferred_element_type=jnp.float32
    ).astype(jnp.bfloat16).reshape(3, req_count, new_count, inner_width)
    normed = normalize(hidden_in, norm_gain).reshape(rows, width)
    gate_logit = (
        jnp.dot(normed, w_forget, preferred_element_type=jnp.float32).reshape(
            req_count, new_count, head_count
        )
        + forget_bias
    )
    prefix = jnp.cumsum(jax.nn.log_sigmoid(gate_logit), axis=1)
    slot_ids = jnp.arange(seq_count, dtype=jnp.int32)
    holders = piece_map[:, :, None] == slot_ids[None, None, :]
    piece_of_slot = jnp.sum(jnp.where(holders, slot_ids[None, :, None], 0), axis=1)
    own_piece = jnp.sum(jnp.where(piece_map == seq_index, slot_ids[None, :], 0), axis=1)
    steps = jnp.arange(piece_len, dtype=jnp.int32)
    positions = own_piece[:, None] * piece_len + steps[None, :]
    live_mask = positions < cache_lengths[:, None]
    masked = jnp.where(live_mask[:, None, :], cache_forget, 0.0)
    piece_total = jnp.sum(masked, axis=-1)
    later_step = (steps[:, None] > steps[None, :]).astype(jnp.float32)
    trailing_part = jnp.einsum(
        "rhl,lj->rhj", masked, later_step, precision=lax.Precision.HIGHEST,
        preferred_element_type=jnp.float32,
    )
    col_head = jnp.arange(inner_width, dtype=jnp.int32) // HEAD_DIM
    head_mask = col_head[None, :] == jnp.arange(head_count, dtype=jnp.int32)[:, None]
    query_blocks = jnp.where(head_mask[None, None], all_heads[0][:, :, None, :], 0).reshape(
        req_count, new_count * head_count, inner_width
    )
    scores = (
        jnp.einsum("rnc,rtc->rnt", query_blocks, cache_keys, preferred_element_type=jnp.float32)
        * logit_scale
    ).reshape(req_count, new_count, head_count, piece_len)
    scores = scores + trailing_part[:, None, :, :] + prefix[..., None]
    key_live = live_mask[:, None, None, :]
    row_max = jnp.max(jnp.where(key_live, scores, neg_fill), axis=-1)
    attn_weights = jnp.where(key_live, jnp.exp(scores - row_max[..., None]), 0.0)
    weight_sum = jnp.sum(attn_weights, axis=-1)
    accum_blocks = jnp.einsum(
        "rnt,rtc->rnc",
        attn_weights.astype(jnp.bfloat16).reshape(req_count, new_count * head_count, piece_len),
        cache_values,
        preferred_element_type=jnp.float32,
    ).reshape(req_count, new_count, head_count, inner_width)
    fold = (
        (jnp.arange(inner_width, dtype=jnp.int32) % HEAD_DIM)[:, None]
        == jnp.arange(HEAD_DIM, dtype=jnp.int32)[None, :]
    ).astype(jnp.float32)
    accum = jnp.einsum(
        "rmhc,cd->rmhd",
        jnp.where(head_mask[None, None], accum_blocks, 0.0),
        fold,
        precision=lax.Precision.HIGHEST,
        preferred_element_type=jnp.float32,
    )
    packed = jnp.concatenate(
        [
            accum,
            row_max[..., None],
            weight_sum[..., None],
            jnp.broadcast_to(piece_total[:, None, :, None], (req_count, new_count, head_count, 1)),
        ],
        axis=-1,
    )
    packed = packed.reshape(req_count, new_count, seq_count, own_heads, HEAD_DIM + 3).transpose(
        2, 0, 1, 3, 4
    )
    parts = lax.all_to_all(packed, "seq", 0, 0, tiled=True)
    part_acc = parts[..., :HEAD_DIM]
    part_max = parts[..., HEAD_DIM]
    part_sum = parts[..., HEAD_DIM + 1]
    part_total = parts[:, :, 0, :, HEAD_DIM + 2]
    later_piece = (piece_of_slot.T[None, :, :] > piece_of_slot.T[:, None, :])[..., None]
    later_sum = jnp.sum(jnp.where(later_piece, part_total[None], 0.0), axis=1)
    part_max = part_max + later_sum[:, :, None, :]
    cache_max = jnp.max(part_max, axis=0)
    factor = jnp.exp(part_max - cache_max[None])
    cache_sum = jnp.sum(part_sum * factor, axis=0)
    cache_acc = jnp.sum(part_acc * factor[..., None], axis=0)
    own_rows = lax.dynamic_slice_in_dim(
        all_heads, head_start * HEAD_DIM, own_heads * HEAD_DIM, 3
    ).reshape(3, req_count, new_count, own_heads, HEAD_DIM)
    own_prefix = lax.dynamic_slice_in_dim(prefix, head_start, own_heads, 2)
    fresh_logits = (
        jnp.einsum(
            "rmhd,rnhd->rmhn",
            own_rows[0],
            own_rows[1],
            preferred_element_type=jnp.float32,
        )
        * logit_scale
    )
    fresh_logits = (
        fresh_logits + own_prefix[..., None] - jnp.transpose(own_prefix, (0, 2, 1))[:, None, :, :]
    )
    step_ids = jnp.arange(new_count, dtype=jnp.int32)
    causal = (step_ids[None, :] <= step_ids[:, None])[None, :, None, :]
    joint_max = jnp.maximum(cache_max, jnp.max(jnp.where(causal, fresh_logits, neg_fill), axis=-1))
    new_weights = jnp.where(causal, jnp.exp(fresh_logits - joint_max[..., None]), 0.0)
    carried = jnp.exp(cache_max - joint_max)
    total_sum = cache_sum * carried + jnp.sum(new_weights, axis=-1)
    blend_weights = cache_acc * carried[..., None] + jnp.einsum(
        "rmhn,rnhd->rmhd",
        new_weights.astype(jnp.bfloat16),
        own_rows[2],
        preferred_element_type=jnp.float32,
    )
    result = blend_weights / total_sum[..., None]
    live_rows = (step_ids[None, :] <= draft_counts[:, None])[:, :, None, None]
    result = jnp.where(live_rows, result, 0.0)
    return result.reshape(req_count, new_count, own_heads * HEAD_DIM).astype(jnp.bfloat16)


def solution(mesh):
    in_specs = (
        P("fsdp", None, None),
        P(),
        P(None, None, "seq", "fsdp"),
        P(),
        P(),
        P("fsdp", "seq", None),
        P("fsdp", "seq", None),
        P("fsdp", None, "seq"),
        P("fsdp"),
        P("fsdp", None),
        P("fsdp"),
    )
    out_specs = P("fsdp", None, "seq")
    return jax.shard_map(body, mesh=mesh, in_specs=in_specs, out_specs=out_specs, check_vma=False)
```

time: 148 us -> 86.4 us (0.58)
  local copies, waits for them, and re-layouts: 82.3 us -> 15.2 us
  waiting for transfers between devices: 25.4 us -> 31.5 us
  other arithmetic: 10.7 us -> 6.15 us
  matrix products: 11.2 us -> 15 us
    transpose x7 -> x3, local copies, waits for them, and re-layouts: 38.7 us -> 0.89 us  [the longest x1 0.71 us: body(): packed.reshape(req_count, new_count, seq_count, own_heads, HEAD_DIM + 3)]
    unnamed x40 -> x22, local copies, waits for them, and re-layouts: 13.5 us -> 1.85 us
    reshape x3 -> x6, local copies, waits for them, and re-layouts: 11.6 us -> 1.29 us  [the longest x1 0.45 us: body(): normalize(hidden_all, norm_gain).reshape(fsdp_count * rows, width)]
    broadcast_in_dim x5 -> x6, local copies, waits for them, and re-layouts: 5.47 us -> 0.58 us  [the longest x3 0.31 us: body(): jnp.broadcast_to(piece_total[:, None, :, None], (req_count, new_count, he...]
    dot_general x3 -> x5, matrix products: 0.68 us -> 5.49 us  [the longest x1 2.92 us: body(): jnp.einsum('rmhc,cd->rmhd', jnp.where(head_mask[None, None], accum_blocks...]
    all_to_all x1, waiting for transfers between devices: 8.84 us -> 13.6 us  [body(): lax.all_to_all(jnp.broadcast_to(hidden_in[None], (fsdp_count, req_count,...]
    reduce_sum x1 -> x0, other arithmetic: 3.97 us -> none  [body(): jnp.sum(accum_blocks * head_eye.astype(jnp.float32)[None, :, None, :, Non...]
    mul x4 -> x0, local copies, waits for them, and re-layouts: 3.82 us -> none  [body(): query_rows[:, :, :, None, :] * head_eye[None, :, None, :, None]]
  transfers between devices with their start and end apart: 3 -> 3, of which waited for: 3 -> 3; matrix products, arithmetic and copies ran while one was open for 6% -> 3% of each run, Pallas kernels for 0% -> 0%
where the time goes in v3:
time: 86.4 us; the launch traced here: 86 us
  waiting for transfers between devices  31.5 us (36%)
  starting transfers between devices  17.6 us (20%)
  local copies, waits for them, and re-layouts  15.2 us (18%)
  matrix products  15 us (17%)
  other arithmetic  6.15 us (7%)
    all_to_all x1, waiting for transfers between devices, body(): lax.all_to_all(jnp.broadcast_to(hidden_in[None], (fsdp_count, req_count,...  13.6 us
    all_to_all x1, waiting for transfers between devices, body(): incoming = lax.all_to_all(outgoing, ('fsdp', 'seq'), 0, 0, tiled=True)  9.73 us
    all_to_all x1, waiting for transfers between devices, body(): parts = lax.all_to_all(packed, 'seq', 0, 0, tiled=True)  8.15 us
    all_to_all x1, starting transfers between devices, body(): incoming = lax.all_to_all(outgoing, ('fsdp', 'seq'), 0, 0, tiled=True)  7.76 us
    all_to_all x1, starting transfers between devices, body(): lax.all_to_all(jnp.broadcast_to(hidden_in[None], (fsdp_count, req_count,...  6.45 us
    dot_general x1, matrix products, body(): jnp.einsum('rnc,rtc->rnt', query_blocks, cache_keys, preferred_element_ty...  5 us
    dot_general x1, matrix products, body(): jnp.einsum('rnt,rtc->rnc', attn_weights.astype(jnp.bfloat16).reshape(req_...  3.91 us
    all_to_all x1, starting transfers between devices, body(): parts = lax.all_to_all(packed, 'seq', 0, 0, tiled=True)  3.41 us
  transfers between devices with their start and end apart: 3, of which 3 were waited for; matrix products, arithmetic and copies ran while one was open for 3% of the time, Pallas kernels for 0%

profile of v3, /device:TPU:0, one launch (start us, length us, event | category | flops | bytes accessed | tf_op | source)
XLA Modules:
  0.0 86.0 jit_solution(17696701786455221984)
XLA Ops:
  0.1 2.1 %broadcast_in_dim.223 = bf16[16,4,5,1536]{3,1,2,0:T(4,128)(2,1)} broadcast(bf16[4,5,1536]{2,0,1:T(4,128)(2,1)} %param.11), dimensions={1,2,3} | broadcast | bytes 1044480 | tf_op jit(solution)/shard_map/broadcast_in_dim | solution.py:46
  2.2 6.4 %all-to-all-start = ((bf16[16,4,5,1536]{3,1,2,0:T(4,128)(2,1)}), bf16[16,4,5,1536]{3,1,2,0:T(4,128)(2,1)S(1)}, u32[]{:S(2)}, u32[]{:S(2)}) async-start(bf16[16,4,5,1536]{3,1,2,0:T(4,128)(2,1)} %broadcast_in_dim.223), calls=%async_computation | async-start | bytes 1966080 | tf_op jit(solution)/shard_map/all_to_all | solution.py:45
  8.7 0.1 fusion.29
  8.8 0.1 select_reduce_fusion.5
  9.1 0.4 fusion.15
  9.7 0.3 fusion.86
  10.3 0.1 copy.220
  10.6 0.1 copy.237
  10.7 0.1 copy.236
  10.8 0.1 broadcast_compare_fusion
  10.9 13.6 %all-to-all-done = bf16[16,4,5,1536]{3,1,2,0:T(4,128)(2,1)S(1)} async-done(((bf16[16,4,5,1536]{3,1,2,0:T(4,128)(2,1)}), bf16[16,4,5,1536]{3,1,2,0:T(4,128)(2,1)S(1)}, u32[]{:S(2)}, u32[]{:S(2)}) %all-to-all-start) | async-done | bytes 983072 | tf_op jit(solution)/shard_map/all_to_all | solution.py:45
  24.5 0.6 fusion.5
  25.1 0.6 fusion.7
  25.7 0.3 copy.215
  26.0 0.5 reshape.347
  26.4 0.4 fusion.12
  26.8 0.2 reshape.349
  27.1 0.1 copy.281
  27.2 0.2 broadcast_in_dim.224
  27.4 0.5 broadcast.373
  28.0 0.7 reduce.5
  28.7 0.9 %reshape.360 = bf16[128,2,360]{2,1,0:T(2,128)(2,1)} reshape(bf16[128,720]{1,0:T(8,128)(2,1)S(1)} %reduce.5) | data formatting | bytes 368640
  29.5 7.8 %all-to-all-start.1 = ((bf16[128,2,360]{2,1,0:T(2,128)(2,1)}), bf16[128,2,360]{2,1,0:T(2,128)(2,1)S(1)}, u32[]{:S(2)}, u32[]{:S(2)}) async-start(bf16[128,2,360]{2,1,0:T(2,128)(2,1)} %reshape.360), calls=%async_computation.1 | async-start | bytes 393216 | tf_op jit(solution)/shard_map/all_to_all | solution.py:67
  37.3 9.7 %all-to-all-done.1 = bf16[128,2,360]{2,1,0:T(2,128)(2,1)S(1)} async-done(((bf16[128,2,360]{2,1,0:T(2,128)(2,1)}), bf16[128,2,360]{2,1,0:T(2,128)(2,1)S(1)}, u32[]{:S(2)}, u32[]{:S(2)}) %all-to-all-start.1) | async-done | bytes 184352 | tf_op jit(solution)/shard_map/all_to_all | solution.py:67
  47.1 0.3 reshape.361
  47.4 1.3 %reduce.2 = bf16[128,720]{1,0:T(8,128)(2,1)S(1)} reduce(bf16[128,1,720]{2,1,0:T(2,128)(2,1)S(1)} %reshape.361, bf16[]{:T(256)} %constant.136), dimensions={1}, to_apply=%all_to_all.14.reduce_sub_computation | reduce | bytes 368642 | tf_op jit(solution)/shard_map/all_to_all | solution.py:67
  48.7 0.4 reshape.350
  49.1 1.9 %fusion.4 = bf16[60,1536]{1,0:T(8,128)(2,1)S(1)} fusion(bf16[1536,60]{1,0:T(8,128)(2,1)S(1)} %reshape.350, s32[1536]{0:T(1024)S(1)} %fusion.72), kind=kOutput, calls=%fused_computation.7 | convolution fusion | flops 285566976 | bytes 374784 | tf_op jit(solution)/shard_map/kx,kj->xj/dot_general | solution.py:79
  51.4 0.2 bitcast_select_fusion
  51.6 0.1 add.206
  51.7 5.0 %select_reduce_fusion = (f32[4,120]{1,0:T(4,128)S(1)}, f32[4,120,512]{2,1,0:T(8,128)S(1)}) fusion(pred[4,512]{1,0:T(4,128)(4,1)S(1)} %add_compare_fusion, f32[4,120]{1,0:T(4,128)S(1)} %add.213, f32[4,120,512]{2,1,0:T(8,128)S(1)} %bitcast.72, bf16[4,120,1536]{2,1,0:T(8,128)(2,1)S(1)} %bitcast_select_fusion, bf16[4,512,1536]{2,1,0:T(8,128)(2,1)} %param.16), kind=kOutput, calls=%fused_computation.26 | convolution fusion | flops 756203008 | bytes 9737984 | tf_op jit(solution)/shard_map/rnc,rtc->rnt/dot_general | solution.py:110
  56.7 0.1 concatenate.8
  56.8 0.3 fusion.17
  57.2 0.1 concatenate.9
  57.3 1.1 %copy.222 = f32[4,5,8,3,1]{4,0,3,2,1:T(4,128)S(1)} copy(f32[4,5,8,3,1]{3,2,1,0,4:T(8,128)S(1)} %concatenate.9) | data formatting | bytes 3840 | tf_op jit(solution)/shard_map/concatenate | solution.py:135
  58.3 1.1 %copy.221 = f32[4,5,8,3,1]{4,0,3,2,1:T(4,128)S(1)} copy(f32[4,5,8,3,1]{3,2,1,0,4:T(8,128)S(1)} %concatenate.8) | data formatting | bytes 3840 | tf_op jit(solution)/shard_map/concatenate | solution.py:135
  59.4 3.9 %fusion.19 = f32[4,120,1536]{2,1,0:T(8,128)S(1)} fusion(bf16[4,512,1536]{2,1,0:T(8,128)(2,1)} %param.17, f32[4,120,512]{2,1,0:T(8,128)S(1)} %get-tuple-element.17, f32[4,120]{1,0:T(4,128)S(1)} %get-tuple-element.16, pred[4,512]{1,0:T(4,128)(4,1)S(1)} %add_compare_fusion), kind=kOutput, calls=%fused_computation.29 | convolution fusion | flops 755712000 | bytes 10227584 | tf_op jit(solution)/shard_map/rnt,rtc->rnc/dot_general | solution.py:118
  63.3 1.9 %copy.219 = f32[4,120,1536]{2,0,1:T(4,128)S(1)} copy(f32[4,120,1536]{2,1,0:T(8,128)S(1)} %fusion.19) | data formatting | bytes 5898240 | tf_op jit(solution)/shard_map/rnt,rtc->rnc/dot_general | solution.py:118
  65.2 2.9 %fusion.2 = f32[4,5,8,3,64]{4,0,3,2,1:T(4,128)S(1)} fusion(f32[4,5,8,3,1536]{4,0,3,2,1:T(4,128)S(1)} %bitcast.73, pred[8,3,1536]{2,1,0:T(4,128)(4,1)S(1)} %broadcast_compare_fusion, s32[1536]{0:T(1024)S(1)} %fusion.51), kind=kOutput, calls=%fused_computation.3 | convolution fusion | flops 567066624 | bytes 3115008 | tf_op jit(solution)/shard_map/rmhc,cd->rmhd/dot_general | solution.py:128
  68.3 0.5 maximum_bitcast_fusion
  68.7 0.7 copy.223
  69.4 3.4 %all-to-all-start.2 = ((f32[8,4,5,3,67]{4,1,3,2,0:T(4,128)}), f32[8,4,5,3,67]{4,1,3,2,0:T(4,128)S(1)}, u32[]{:S(2)}, u32[]{:S(2)}) async-start(f32[8,4,5,3,67]{4,1,3,2,0:T(4,128)} %copy.223), calls=%async_computation.2 | async-start | bytes 491520 | tf_op jit(solution)/shard_map/all_to_all | solution.py:147
  73.0 0.1 convolution_multiply_fusion.1
  73.2 0.2 copy.268
  73.3 0.2 select_reduce_fusion.3
  73.5 0.1 copy.240
  73.6 8.2 %all-to-all-done.2 = f32[8,4,5,3,67]{4,1,3,2,0:T(4,128)S(1)} async-done(((f32[8,4,5,3,67]{4,1,3,2,0:T(4,128)}), f32[8,4,5,3,67]{4,1,3,2,0:T(4,128)S(1)}, u32[]{:S(2)}, u32[]{:S(2)}) %all-to-all-start.2) | async-done | bytes 128672 | tf_op jit(solution)/shard_map/all_to_all | solution.py:147
  81.8 0.3 fusion.93
  82.1 0.4 copy.265
  82.6 0.2 copy.255
  83.0 0.1 copy.241
  83.2 0.1 copy.244
  83.4 0.2 fusion.91
  83.6 0.2 copy.229
  83.7 0.1 copy.251
  83.8 0.4 copy.248
  84.3 0.2 fusion.38
  84.5 0.1 copy.249
  84.6 0.1 copy.252
  84.7 0.1 copy.242
  84.8 0.1 fusion.42
  84.9 0.2 fusion.26
  85.2 0.1 select_convert_fusion
  85.3 0.7 convert_element_type.49
  (58 shorter events, 1.9 us)
Async XLA Ops:
  0.0 9.6 %copy-start = (bf16[1536,24]{0,1:T(8,128)(2,1)S(1)}, bf16[1536,24]{0,1:T(8,128)(2,1)}, u32[]{:S(2)}) copy-start(bf16[1536,24]{0,1:T(8,128)(2,1)} %param.14) | copy-start | bytes 221188
  0.0 8.7 %copy-start.1 = (bf16[4,5,1536]{2,0,1:T(4,128)(2,1)S(1)}, bf16[4,5,1536]{2,0,1:T(4,128)(2,1)}, u32[]{:S(2)}) copy-start(bf16[4,5,1536]{2,0,1:T(4,128)(2,1)} %param.11) | copy-start | bytes 184324
  0.0 8.8 %copy-start.5 = (s32[4,8]{1,0:T(4,128)S(1)}, s32[4,8]{1,0:T(4,128)}, u32[]{:S(2)}) copy-start(s32[4,8]{1,0:T(4,128)} %param.20) | copy-start | bytes 388
  0.0 8.9 %copy-start.6 = (s32[4]{0:T(128)S(1)}, s32[4]{0:T(128)}, u32[]{:S(2)}) copy-start(s32[4]{0:T(128)} %param.19) | copy-start | bytes 52
  0.0 9.0 %copy-start.2 = (f32[4,24,512]{2,1,0:T(8,128)S(1)}, f32[4,24,512]{2,1,0:T(8,128)}, u32[]{:S(2)}) copy-start(f32[4,24,512]{2,1,0:T(8,128)} %param.18) | copy-start | bytes 589828
  0.0 9.6 %copy-start.4 = (f32[1536]{0:T(1024)S(1)}, f32[1536]{0:T(1024)}, u32[]{:S(2)}) copy-start(f32[1536]{0:T(1024)} %param.12) | copy-start | bytes 18436
  0.0 9.6 %copy-start.7 = (f32[24]{0:T(128)S(1)}, f32[24]{0:T(128)}, u32[]{:S(2)}) copy-start(f32[24]{0:T(128)} %param.15) | copy-start | bytes 292
  0.0 10.2 %copy-start.3 = (bf16[1536,3,3,4]{0,3,2,1:T(4,128)(2,1)S(1)}, bf16[1536,3,3,4]{0,3,2,1:T(4,128)(2,1)}, u32[]{:S(2)}) copy-start(bf16[1536,3,3,4]{0,3,2,1:T(4,128)(2,1)} %param.13) | copy-start | bytes 331780
  2.2 22.3 %all-to-all-start = ((bf16[16,4,5,1536]{3,1,2,0:T(4,128)(2,1)}), bf16[16,4,5,1536]{3,1,2,0:T(4,128)(2,1)S(1)}, u32[]{:S(2)}, u32[]{:S(2)}) async-start(bf16[16,4,5,1536]{3,1,2,0:T(4,128)(2,1)} %broadcast_in_dim.223), calls=%async_computation | async-start | bytes 1966080 | tf_op jit(solution)/shard_map/all_to_all | solution.py:45
  26.0 11.3 %copy-start.8 = (s32[4]{0:T(128)S(1)}, s32[4]{0:T(128)}, u32[]{:S(2)}) copy-start(s32[4]{0:T(128)} %param.21) | copy-start | bytes 52
  29.5 17.5 %all-to-all-start.1 = ((bf16[128,2,360]{2,1,0:T(2,128)(2,1)}), bf16[128,2,360]{2,1,0:T(2,128)(2,1)S(1)}, u32[]{:S(2)}, u32[]{:S(2)}) async-start(bf16[128,2,360]{2,1,0:T(2,128)(2,1)} %reshape.360), calls=%async_computation.1 | async-start | bytes 393216 | tf_op jit(solution)/shard_map/all_to_all | solution.py:67
  69.4 12.3 %all-to-all-start.2 = ((f32[8,4,5,3,67]{4,1,3,2,0:T(4,128)}), f32[8,4,5,3,67]{4,1,3,2,0:T(4,128)S(1)}, u32[]{:S(2)}, u32[]{:S(2)}) async-start(f32[8,4,5,3,67]{4,1,3,2,0:T(4,128)} %copy.223), calls=%async_computation.2 | async-start | bytes 491520 | tf_op jit(solution)/shard_map/all_to_all | solution.py:147

commit v4 on v3

--- a/solution.py
+++ b/solution.py
@@ -1,6 +1,10 @@
+import functools
+
 import jax
 import jax.numpy as jnp
 from jax import lax
+from jax.experimental import pallas as pl
+from jax.experimental.pallas import tpu as pltpu
 from jax.sharding import PartitionSpec as P
 
 HEAD_DIM = 64
@@ -14,6 +18,55 @@
     values = rows.astype(jnp.float32)
     mean_sq = jnp.mean(values * values, axis=-1, keepdims=True)
     return (values * lax.rsqrt(mean_sq + norm_eps) * gain).astype(jnp.bfloat16)
+
+
+def attention_kernel(q_ref, k_ref, v_ref, bias_ref, live_ref, total_ref, out_ref, *, new_count):
+    row_count = q_ref.shape[1]
+    pair_count = v_ref.shape[2] // 128
+    scores = lax.dot_general(
+        q_ref[0], k_ref[0], (((1,), (1,)), ((), ())), preferred_element_type=jnp.float32
+    )
+    scores = scores * (HEAD_DIM ** (-0.5)) + bias_ref[0]
+    live = live_ref[0] > 0.5
+    row_max = jnp.max(jnp.where(live, scores, neg_fill), axis=1, keepdims=True)
+    weights = jnp.where(live, jnp.exp(scores - row_max), 0.0)
+    weight_sum = jnp.sum(weights, axis=1, keepdims=True)
+    blocks = jnp.dot(weights.astype(jnp.bfloat16), v_ref[0], preferred_element_type=jnp.float32)
+    row = lax.broadcasted_iota(jnp.int32, (row_count, 128), 0)
+    picked = jnp.zeros((row_count, 128), jnp.float32)
+    odd = row < 0
+    for pair in range(pair_count):
+        lo = 2 * pair * new_count
+        picked = jnp.where(
+            (row >= lo) & (row < lo + 2 * new_count), blocks[:, pair * 128 : (pair + 1) * 128], picked
+        )
+        odd = odd | ((row >= lo + new_count) & (row < lo + 2 * new_count))
+    accum = jnp.where(odd, pltpu.roll(picked, 64, 1), picked)
+    lane = lax.broadcasted_iota(jnp.int32, (row_count, 128), 1)
+    packed = jnp.where(lane < HEAD_DIM, accum, 0.0)
+    packed = jnp.where(lane == HEAD_DIM, row_max, packed)
+    packed = jnp.where(lane == HEAD_DIM + 1, weight_sum, packed)
+    packed = jnp.where(lane == HEAD_DIM + 2, total_ref[0], packed)
+    out_ref[0] = packed
+
+
+def piece_attention(query_blocks, keys, values, bias, live_row, total_row, new_count):
+    req_count, row_count, inner_width = query_blocks.shape
+    piece_len = keys.shape[1]
+    return pl.pallas_call(
+        functools.partial(attention_kernel, new_count=new_count),
+        grid=(req_count,),
+        in_specs=[
+            pl.BlockSpec((1, row_count, inner_width), lambda r: (r, 0, 0)),
+            pl.BlockSpec((1, piece_len, inner_width), lambda r: (r, 0, 0)),
+            pl.BlockSpec((1, piece_len, inner_width), lambda r: (r, 0, 0)),
+            pl.BlockSpec((1, row_count, piece_len), lambda r: (r, 0, 0)),
+            pl.BlockSpec((1, 1, piece_len), lambda r: (r, 0, 0)),
+            pl.BlockSpec((1, row_count, 1), lambda r: (r, 0, 0)),
+        ],
+        out_specs=pl.BlockSpec((1, row_count, 128), lambda r: (r, 0, 0)),
+        out_shape=jax.ShapeDtypeStruct((req_count, row_count, 128), jnp.float32),
+    )(query_blocks, keys, values, bias, live_row, total_row)
 
 
 def body(
@@ -103,55 +156,26 @@
     )
     col_head = jnp.arange(inner_width, dtype=jnp.int32) // HEAD_DIM
     head_mask = col_head[None, :] == jnp.arange(head_count, dtype=jnp.int32)[:, None]
-    query_blocks = jnp.where(head_mask[None, None], all_heads[0][:, :, None, :], 0).reshape(
-        req_count, new_count * head_count, inner_width
-    )
-    scores = (
-        jnp.einsum("rnc,rtc->rnt", query_blocks, cache_keys, preferred_element_type=jnp.float32)
-        * logit_scale
-    ).reshape(req_count, new_count, head_count, piece_len)
-    scores = scores + trailing_part[:, None, :, :] + prefix[..., None]
-    key_live = live_mask[:, None, None, :]
-    row_max = jnp.max(jnp.where(key_live, scores, neg_fill), axis=-1)
-    attn_weights = jnp.where(key_live, jnp.exp(scores - row_max[..., None]), 0.0)
-    weight_sum = jnp.sum(attn_weights, axis=-1)
-    accum_blocks = jnp.einsum(
-        "rnt,rtc->rnc",
-        attn_weights.astype(jnp.bfloat16).reshape(req_count, new_count * head_count, piece_len),
-        cache_values,
-        preferred_element_type=jnp.float32,
-    ).reshape(req_count, new_count, head_count, inner_width)
-    fold = (
-        (jnp.arange(inner_width, dtype=jnp.int32) % HEAD_DIM)[:, None]
-        == jnp.arange(HEAD_DIM, dtype=jnp.int32)[None, :]
-    ).astype(jnp.float32)
-    accum = jnp.einsum(
-        "rmhc,cd->rmhd",
-        jnp.where(head_mask[None, None], accum_blocks, 0.0),
-        fold,
-        precision=lax.Precision.HIGHEST,
-        preferred_element_type=jnp.float32,
-    )
-    packed = jnp.concatenate(
-        [
-            accum,
-            row_max[..., None],
-            weight_sum[..., None],
-            jnp.broadcast_to(piece_total[:, None, :, None], (req_count, new_count, head_count, 1)),
-        ],
-        axis=-1,
-    )
-    packed = packed.reshape(req_count, new_count, seq_count, own_heads, HEAD_DIM + 3).transpose(
-        2, 0, 1, 3, 4
-    )
+    query_blocks = jnp.where(
+        head_mask[None, :, None, :], all_heads[0][:, None, :, :], 0
+    ).reshape(req_count, head_count * new_count, inner_width)
+    bias = (trailing_part[:, :, None, :] + jnp.transpose(prefix, (0, 2, 1))[..., None]).reshape(
+        req_count, head_count * new_count, piece_len
+    )
+    live_row = live_mask.astype(jnp.float32)[:, None, :]
+    total_row = jnp.broadcast_to(
+        piece_total[:, :, None], (req_count, head_count, new_count)
+    ).reshape(req_count, head_count * new_count, 1)
+    packed = piece_attention(query_blocks, cache_keys, cache_values, bias, live_row, total_row, new_count)
+    packed = packed.reshape(req_count, seq_count, own_heads, new_count, 128).transpose(1, 0, 2, 3, 4)
     parts = lax.all_to_all(packed, "seq", 0, 0, tiled=True)
     part_acc = parts[..., :HEAD_DIM]
     part_max = parts[..., HEAD_DIM]
     part_sum = parts[..., HEAD_DIM + 1]
-    part_total = parts[:, :, 0, :, HEAD_DIM + 2]
+    part_total = parts[:, :, :, 0, HEAD_DIM + 2]
     later_piece = (piece_of_slot.T[None, :, :] > piece_of_slot.T[:, None, :])[..., None]
     later_sum = jnp.sum(jnp.where(later_piece, part_total[None], 0.0), axis=1)
-    part_max = part_max + later_sum[:, :, None, :]
+    part_max = part_max + later_sum[..., None]
     cache_max = jnp.max(part_max, axis=0)
     factor = jnp.exp(part_max - cache_max[None])
     cache_sum = jnp.sum(part_sum * factor, axis=0)
@@ -159,35 +183,39 @@
     own_rows = lax.dynamic_slice_in_dim(
         all_heads, head_start * HEAD_DIM, own_heads * HEAD_DIM, 3
     ).reshape(3, req_count, new_count, own_heads, HEAD_DIM)
-    own_prefix = lax.dynamic_slice_in_dim(prefix, head_start, own_heads, 2)
+    own_prefix = jnp.transpose(
+        lax.dynamic_slice_in_dim(prefix, head_start, own_heads, 2), (0, 2, 1)
+    )
     fresh_logits = (
         jnp.einsum(
-            "rmhd,rnhd->rmhn",
+            "rmhd,rnhd->rhmn",
             own_rows[0],
             own_rows[1],
             preferred_element_type=jnp.float32,
         )
         * logit_scale
     )
-    fresh_logits = (
-        fresh_logits + own_prefix[..., None] - jnp.transpose(own_prefix, (0, 2, 1))[:, None, :, :]
-    )
+    fresh_logits = fresh_logits + own_prefix[..., :, None] - own_prefix[..., None, :]
     step_ids = jnp.arange(new_count, dtype=jnp.int32)
-    causal = (step_ids[None, :] <= step_ids[:, None])[None, :, None, :]
+    causal = (step_ids[None, :] <= step_ids[:, None])[None, None]
     joint_max = jnp.maximum(cache_max, jnp.max(jnp.where(causal, fresh_logits, neg_fill), axis=-1))
     new_weights = jnp.where(causal, jnp.exp(fresh_logits - joint_max[..., None]), 0.0)
     carried = jnp.exp(cache_max - joint_max)
     total_sum = cache_sum * carried + jnp.sum(new_weights, axis=-1)
     blend_weights = cache_acc * carried[..., None] + jnp.einsum(
-        "rmhn,rnhd->rmhd",
+        "rhmn,rnhd->rhmd",
         new_weights.astype(jnp.bfloat16),
         own_rows[2],
         preferred_element_type=jnp.float32,
     )
     result = blend_weights / total_sum[..., None]
-    live_rows = (step_ids[None, :] <= draft_counts[:, None])[:, :, None, None]
+    live_rows = (step_ids[None, :] <= draft_counts[:, None])[:, None, :, None]
     result = jnp.where(live_rows, result, 0.0)
-    return result.reshape(req_count, new_count, own_heads * HEAD_DIM).astype(jnp.bfloat16)
+    return (
+        jnp.transpose(result, (0, 2, 1, 3))
+        .reshape(req_count, new_count, own_heads * HEAD_DIM)
+        .astype(jnp.bfloat16)
+    )
 
 
 def solution(mesh):

time: 86.4 us -> 79.8 us (0.924)
  matrix products: 15 us -> 3.2 us
  Pallas kernels: 0 us -> 8.42 us
  waiting for transfers between devices: 31.5 us -> 28.4 us
  other arithmetic: 6.15 us -> 8.76 us
  local copies, waits for them, and re-layouts: 15.2 us -> 12.8 us
    dot_general x5 -> x2, matrix products: 12.1 us -> 0.25 us  [the longest x1 0.13 us: body(): jnp.einsum('rmhd,rnhd->rhmn', own_rows[0], own_rows[1], preferred_element...]
    pallas_call x0 -> x1, Pallas kernels: none -> 8.42 us  [piece_attention(): pl.pallas_call(functools.partial(attention_kernel, new_count=new_count),...]
    all_to_all x1, waiting for transfers between devices: 13.6 us -> 10.4 us  [body(): lax.all_to_all(jnp.broadcast_to(hidden_in[None], (fsdp_count, req_count,...]
    concatenate x4 -> x0, local copies, waits for them, and re-layouts: 2.38 us -> none  [body(): jnp.concatenate([accum, row_max[..., None], weight_sum[..., None], jnp.br...]
    pallas_call x0 -> x1, local copies, waits for them, and re-layouts: none -> 1.69 us  [piece_attention(): pl.pallas_call(functools.partial(attention_kernel, new_count=new_count),...]
    dot_general x1 -> x2, local copies, waits for them, and re-layouts: 1.9 us -> 0.29 us  [the longest x1 0.16 us: body(): jnp.einsum('rmhd,rnhd->rhmn', own_rows[0], own_rows[1], preferred_element...]
    select_n x2 -> x1, other arithmetic: 0.22 us -> 1.75 us  [body(): jnp.where(head_mask[None, :, None, :], all_heads[0][:, None, :, :], 0)]
    add x0 -> x1, other arithmetic: none -> 1.29 us  [body(): trailing_part[:, :, None, :] + jnp.transpose(prefix, (0, 2, 1))[..., None]]
  transfers between devices with their start and end apart: 3 -> 3, of which waited for: 3 -> 3; matrix products, arithmetic and copies ran while one was open for 3% -> 8% of each run, Pallas kernels for 0% -> 0%
where the time goes in v4:
time: 79.8 us; the launch traced here: 79.4 us
  waiting for transfers between devices  28.4 us (36%)
  starting transfers between devices  17.4 us (22%)
  local copies, waits for them, and re-layouts  12.8 us (16%)
  other arithmetic  8.76 us (11%)
  Pallas kernels  8.42 us (11%)
  matrix products  3.2 us (4%)
    all_to_all x1, waiting for transfers between devices, body(): lax.all_to_all(jnp.broadcast_to(hidden_in[None], (fsdp_count, req_count,...  10.4 us
    all_to_all x1, waiting for transfers between devices, body(): incoming = lax.all_to_all(outgoing, ('fsdp', 'seq'), 0, 0, tiled=True)  9.91 us
    pallas_call x1, Pallas kernels, piece_attention(): pl.pallas_call(functools.partial(attention_kernel, new_count=new_count),...  8.42 us
    all_to_all x1, waiting for transfers between devices, body(): parts = lax.all_to_all(packed, 'seq', 0, 0, tiled=True)  8.06 us
    all_to_all x1, starting transfers between devices, body(): incoming = lax.all_to_all(outgoing, ('fsdp', 'seq'), 0, 0, tiled=True)  7.58 us
    all_to_all x1, starting transfers between devices, body(): lax.all_to_all(jnp.broadcast_to(hidden_in[None], (fsdp_count, req_count,...  6.45 us
    all_to_all x1, starting transfers between devices, body(): parts = lax.all_to_all(packed, 'seq', 0, 0, tiled=True)  3.41 us
    broadcast_in_dim x1, local copies, waits for them, and re-layouts, body(): jnp.broadcast_to(hidden_in[None], (fsdp_count, req_count, new_count, width))  2.14 us
  transfers between devices with their start and end apart: 3, of which 3 were waited for; matrix products, arithmetic and copies ran while one was open for 8% of the time, Pallas kernels for 0%

profile of v4, /device:TPU:0, one launch (start us, length us, event | category | flops | bytes accessed | tf_op | source)
XLA Modules:
  0.0 79.4 jit_solution(10131293355138604785)
XLA Ops:
  0.1 2.1 %broadcast_in_dim.181 = bf16[16,4,5,1536]{3,1,2,0:T(4,128)(2,1)} broadcast(bf16[4,5,1536]{2,0,1:T(4,128)(2,1)} %param.11), dimensions={1,2,3} | broadcast | bytes 1044480 | tf_op jit(solution)/shard_map/broadcast_in_dim | solution.py:99
  2.2 6.4 %all-to-all-start = ((bf16[16,4,5,1536]{3,1,2,0:T(4,128)(2,1)}), bf16[16,4,5,1536]{3,1,2,0:T(4,128)(2,1)S(1)}, u32[]{:S(2)}, u32[]{:S(2)}) async-start(bf16[16,4,5,1536]{3,1,2,0:T(4,128)(2,1)} %broadcast_in_dim.181), calls=%async_computation | async-start | bytes 1966080 | tf_op jit(solution)/shard_map/all_to_all | solution.py:98
  8.7 0.1 fusion.13
  8.8 0.1 select_reduce_fusion.4
  9.0 0.4 fusion.9
  9.4 0.1 select_reduce_fusion
  9.6 0.3 fusion.67
  9.9 0.1 copy.303
  10.0 0.1 copy.302
  10.3 0.1 broadcast_in_dim.178
  10.4 0.2 broadcast_in_dim.179
  10.6 0.1 copy.285
  10.7 0.1 copy.286
  10.8 0.1 add.202
  11.0 0.8 %reshape.327.total_ref = f32[4,120,1]{2,1,0:T(8,128)} reshape(f32[4,24,5]{2,1,0:T(8,128)S(1)} %broadcast_in_dim.192) | data formatting | bytes 3840 | tf_op jit(solution)/shard_map/reshape | solution.py:168
  12.0 0.7 compare_convert_fusion.live_ref
  12.7 0.1 add.196
  12.8 1.3 %copy_add_fusion.bias_ref = f32[4,120,512]{2,1,0:T(8,128)} fusion(f32[4,120,512]{2,0,1:T(4,128)S(1)} %bitcast.70, f32[4,120]{1,0:T(4,128)S(1)} %add.202), kind=kLoop, calls=%fused_computation.17 | loop fusion | flops 245760 | bytes 1968000 | tf_op jit(solution)/shard_map/add | solution.py:162
  14.1 10.4 %all-to-all-done = bf16[16,4,5,1536]{3,1,2,0:T(4,128)(2,1)S(1)} async-done(((bf16[16,4,5,1536]{3,1,2,0:T(4,128)(2,1)}), bf16[16,4,5,1536]{3,1,2,0:T(4,128)(2,1)S(1)}, u32[]{:S(2)}, u32[]{:S(2)}) %all-to-all-start) | async-done | bytes 983072 | tf_op jit(solution)/shard_map/all_to_all | solution.py:98
  24.5 0.6 fusion.3
  25.1 0.6 fusion.5
  25.7 0.3 copy.280
  26.0 0.5 reshape.318
  26.4 0.4 fusion.6
  26.8 0.2 reshape.320
  27.1 0.1 copy.344
  27.2 0.2 broadcast_in_dim.182
  27.4 0.6 broadcast.338
  28.0 0.7 reduce.3
  28.8 0.9 %reshape.332 = bf16[128,2,360]{2,1,0:T(2,128)(2,1)} reshape(bf16[128,720]{1,0:T(8,128)(2,1)S(1)} %reduce.3) | data formatting | bytes 368640
  29.7 7.6 %all-to-all-start.1 = ((bf16[128,2,360]{2,1,0:T(2,128)(2,1)}), bf16[128,2,360]{2,1,0:T(2,128)(2,1)S(1)}, u32[]{:S(2)}, u32[]{:S(2)}) async-start(bf16[128,2,360]{2,1,0:T(2,128)(2,1)} %reshape.332), calls=%async_computation.1 | async-start | bytes 393216 | tf_op jit(solution)/shard_map/all_to_all | solution.py:120
  37.3 9.9 %all-to-all-done.1 = bf16[128,2,360]{2,1,0:T(2,128)(2,1)S(1)} async-done(((bf16[128,2,360]{2,1,0:T(2,128)(2,1)}), bf16[128,2,360]{2,1,0:T(2,128)(2,1)S(1)}, u32[]{:S(2)}, u32[]{:S(2)}) %all-to-all-start.1) | async-done | bytes 184352 | tf_op jit(solution)/shard_map/all_to_all | solution.py:120
  47.2 0.3 reshape.333
  47.5 1.3 %reduce = bf16[128,720]{1,0:T(8,128)(2,1)S(1)} reduce(bf16[128,1,720]{2,1,0:T(2,128)(2,1)S(1)} %reshape.333, bf16[]{:T(256)} %constant.125), dimensions={1}, to_apply=%all_to_all.14.reduce_sub_computation | reduce | bytes 368642 | tf_op jit(solution)/shard_map/all_to_all | solution.py:120
  48.8 0.4 reshape.321
  49.2 1.9 %fusion.2 = bf16[60,1536]{1,0:T(8,128)(2,1)S(1)} fusion(bf16[1536,60]{1,0:T(8,128)(2,1)S(1)} %reshape.321, s32[1536]{0:T(1024)S(1)} %fusion.51), kind=kOutput, calls=%fused_computation.5 | convolution fusion | flops 285566976 | bytes 374784 | tf_op jit(solution)/shard_map/kx,kj->xj/dot_general | solution.py:132
  51.3 0.4 broadcast_in_dim.185
  51.7 1.8 %copy_select_fusion.q_ref = bf16[4,120,1536]{2,1,0:T(8,128)(2,1)} fusion(bf16[4,120,1536]{2,0,1:T(4,128)(2,1)S(1)} %bitcast.69, pred[120,1536]{1,0:T(8,128)(4,1)S(1)} %broadcast_in_dim.179), kind=kLoop, calls=%fused_computation.9 | loop fusion | flops 737280 | bytes 3133440 | tf_op jit(solution)/shard_map/jit(_where)/select_n | solution.py:159
  53.4 8.4 %shard_map.109 = f32[4,120,128]{2,1,0:T(8,128)} custom-call(bf16[4,120,1536]{2,1,0:T(8,128)(2,1)} %copy_select_fusion.q_ref, bf16[4,512,1536]{2,1,0:T(8,128)(2,1)} %k_ref.1, bf16[4,512,1536]{2,1,0:T(8,128)(2,1)} %v_ref.1, f32[4,120,512]{2,1,0:T(8,128)} %copy_add_fusion.bias_ref, f32[4,1,512]{2,1,0:T(1,128)} %compare_convert_fusion.live_ref, ...), custom_call_target="tpu_custom_call" | custom-call | tf_op jit(solution)/shard_map/pallas_call | solution.py:56
  61.9 1.7 %copy.289 = f32[4,120,128]{2,0,1:T(4,128)} copy(f32[4,120,128]{2,1,0:T(8,128)} %shard_map.109) | data formatting | bytes 491520 | tf_op jit(solution)/shard_map/pallas_call | solution.py:56
  63.5 3.4 %all-to-all-start.2 = ((f32[8,4,3,5,128]{4,1,3,2,0:T(4,128)}), f32[8,4,3,5,128]{4,1,3,2,0:T(4,128)S(1)}, u32[]{:S(2)}, u32[]{:S(2)}) async-start(f32[8,4,3,5,128]{4,1,3,2,0:T(4,128)} %bitcast.9), calls=%async_computation.2 | async-start | bytes 491520 | tf_op jit(solution)/shard_map/all_to_all | solution.py:171
  67.0 0.1 constant_dynamic-slice_fusion.1
  67.1 0.1 reshape.329
  67.2 0.1 reshape.328
  67.2 0.1 fusion.27
  67.4 0.1 reshape.330
  67.5 0.2 copy.301
  67.6 0.2 select_reduce_fusion.2
  67.8 8.1 %all-to-all-done.2 = f32[8,4,3,5,128]{4,1,3,2,0:T(4,128)S(1)} async-done(((f32[8,4,3,5,128]{4,1,3,2,0:T(4,128)}), f32[8,4,3,5,128]{4,1,3,2,0:T(4,128)S(1)}, u32[]{:S(2)}, u32[]{:S(2)}) %all-to-all-start.2) | async-done | bytes 245792 | tf_op jit(solution)/shard_map/all_to_all | solution.py:171
  75.9 0.3 fusion.73
  76.2 0.4 copy.326
  76.6 0.1 slice.39
  76.7 0.2 copy.317
  76.9 0.1 select_reduce_fusion.1
  77.0 0.1 fusion.24
  77.1 0.1 exponential_bitcast_fusion
  77.2 0.2 fusion.70
  77.4 0.2 copy.295
  77.6 0.4 copy.312
  78.0 0.2 fusion.22
  78.2 0.1 fusion.25
  78.4 0.2 fusion.11
  78.6 0.1 select_convert_fusion
  78.7 0.7 convert_element_type.54
  (45 shorter events, 0.8 us)
Async XLA Ops:
  0.0 9.5 %copy-start = (bf16[1536,24]{0,1:T(8,128)(2,1)S(1)}, bf16[1536,24]{0,1:T(8,128)(2,1)}, u32[]{:S(2)}) copy-start(bf16[1536,24]{0,1:T(8,128)(2,1)} %param.14) | copy-start | bytes 221188
  0.0 8.7 %copy-start.1 = (bf16[4,5,1536]{2,0,1:T(4,128)(2,1)S(1)}, bf16[4,5,1536]{2,0,1:T(4,128)(2,1)}, u32[]{:S(2)}) copy-start(bf16[4,5,1536]{2,0,1:T(4,128)(2,1)} %param.11) | copy-start | bytes 184324
  0.0 8.8 %copy-start.5 = (s32[4,8]{1,0:T(4,128)S(1)}, s32[4,8]{1,0:T(4,128)}, u32[]{:S(2)}) copy-start(s32[4,8]{1,0:T(4,128)} %param.20) | copy-start | bytes 388
  0.0 8.9 %copy-start.6 = (s32[4]{0:T(128)S(1)}, s32[4]{0:T(128)}, u32[]{:S(2)}) copy-start(s32[4]{0:T(128)} %param.19) | copy-start | bytes 52
  0.0 9.0 %copy-start.2 = (f32[4,24,512]{2,1,0:T(8,128)S(1)}, f32[4,24,512]{2,1,0:T(8,128)}, u32[]{:S(2)}) copy-start(f32[4,24,512]{2,1,0:T(8,128)} %param.18) | copy-start | bytes 589828
  0.0 9.5 %copy-start.4 = (f32[1536]{0:T(1024)S(1)}, f32[1536]{0:T(1024)}, u32[]{:S(2)}) copy-start(f32[1536]{0:T(1024)} %param.12) | copy-start | bytes 18436
  0.0 9.5 %copy-start.7 = (f32[24]{0:T(128)S(1)}, f32[24]{0:T(128)}, u32[]{:S(2)}) copy-start(f32[24]{0:T(128)} %param.15) | copy-start | bytes 292
  0.0 10.1 %copy-start.3 = (bf16[1536,3,3,4]{0,3,2,1:T(4,128)(2,1)S(1)}, bf16[1536,3,3,4]{0,3,2,1:T(4,128)(2,1)}, u32[]{:S(2)}) copy-start(bf16[1536,3,3,4]{0,3,2,1:T(4,128)(2,1)} %param.13) | copy-start | bytes 331780
  2.2 22.3 %all-to-all-start = ((bf16[16,4,5,1536]{3,1,2,0:T(4,128)(2,1)}), bf16[16,4,5,1536]{3,1,2,0:T(4,128)(2,1)S(1)}, u32[]{:S(2)}, u32[]{:S(2)}) async-start(bf16[16,4,5,1536]{3,1,2,0:T(4,128)(2,1)} %broadcast_in_dim.181), calls=%async_computation | async-start | bytes 1966080 | tf_op jit(solution)/shard_map/all_to_all | solution.py:98
  26.4 10.8 %copy-start.8 = (s32[4]{0:T(128)S(1)}, s32[4]{0:T(128)}, u32[]{:S(2)}) copy-start(s32[4]{0:T(128)} %param.21) | copy-start | bytes 52
  29.7 17.5 %all-to-all-start.1 = ((bf16[128,2,360]{2,1,0:T(2,128)(2,1)}), bf16[128,2,360]{2,1,0:T(2,128)(2,1)S(1)}, u32[]{:S(2)}, u32[]{:S(2)}) async-start(bf16[128,2,360]{2,1,0:T(2,128)(2,1)} %reshape.332), calls=%async_computation.1 | async-start | bytes 393216 | tf_op jit(solution)/shard_map/all_to_all | solution.py:120
  63.5 12.3 %all-to-all-start.2 = ((f32[8,4,3,5,128]{4,1,3,2,0:T(4,128)}), f32[8,4,3,5,128]{4,1,3,2,0:T(4,128)S(1)}, u32[]{:S(2)}, u32[]{:S(2)}) async-start(f32[8,4,3,5,128]{4,1,3,2,0:T(4,128)} %bitcast.9), calls=%async_computation.2 | async-start | bytes 491520 | tf_op jit(solution)/shard_map/all_to_all | solution.py:171

commit v5 on v4

--- a/solution.py
+++ b/solution.py
@@ -1,5 +1,3 @@
-import functools
-
 import jax
 import jax.numpy as jnp
 from jax import lax
@@ -20,13 +18,26 @@
     return (values * lax.rsqrt(mean_sq + norm_eps) * gain).astype(jnp.bfloat16)
 
 
-def attention_kernel(q_ref, k_ref, v_ref, bias_ref, live_ref, total_ref, out_ref, *, new_count):
-    row_count = q_ref.shape[1]
-    pair_count = v_ref.shape[2] // 128
+def attention_kernel(q_ref, k_ref, v_ref, trail_ref, prefix_ref, live_ref, total_ref, out_ref):
+    step_rows = q_ref.shape[1]
+    head_count = trail_ref.shape[1]
+    piece_len = trail_ref.shape[2]
+    inner_width = q_ref.shape[2]
+    row_count = head_count * step_rows
+    pair_count = inner_width // 128
+    row_step = lax.broadcasted_iota(jnp.int32, (row_count, step_rows), 0) % step_rows
+    spread = (row_step == lax.broadcasted_iota(jnp.int32, (row_count, step_rows), 1)).astype(jnp.bfloat16)
+    repeated = jnp.dot(spread, q_ref[0], preferred_element_type=jnp.float32)
+    row_head = lax.broadcasted_iota(jnp.int32, (row_count, inner_width), 0) // step_rows
+    col_head = lax.broadcasted_iota(jnp.int32, (row_count, inner_width), 1) // HEAD_DIM
+    query_blocks = jnp.where(row_head == col_head, repeated, 0.0).astype(jnp.bfloat16)
     scores = lax.dot_general(
-        q_ref[0], k_ref[0], (((1,), (1,)), ((), ())), preferred_element_type=jnp.float32
-    )
-    scores = scores * (HEAD_DIM ** (-0.5)) + bias_ref[0]
+        query_blocks, k_ref[0], (((1,), (1,)), ((), ())), preferred_element_type=jnp.float32
+    )
+    trailing = jnp.broadcast_to(
+        trail_ref[0][:, None, :], (head_count, step_rows, piece_len)
+    ).reshape(row_count, piece_len)
+    scores = scores * (HEAD_DIM ** (-0.5)) + (trailing + prefix_ref[0])
     live = live_ref[0] > 0.5
     row_max = jnp.max(jnp.where(live, scores, neg_fill), axis=1, keepdims=True)
     weights = jnp.where(live, jnp.exp(scores - row_max), 0.0)
@@ -34,39 +45,44 @@
     blocks = jnp.dot(weights.astype(jnp.bfloat16), v_ref[0], preferred_element_type=jnp.float32)
     row = lax.broadcasted_iota(jnp.int32, (row_count, 128), 0)
     picked = jnp.zeros((row_count, 128), jnp.float32)
-    odd = row < 0
     for pair in range(pair_count):
-        lo = 2 * pair * new_count
+        lo = 2 * pair * step_rows
         picked = jnp.where(
-            (row >= lo) & (row < lo + 2 * new_count), blocks[:, pair * 128 : (pair + 1) * 128], picked
+            (row >= lo) & (row < lo + 2 * step_rows), blocks[:, pair * 128 : (pair + 1) * 128], picked
         )
-        odd = odd | ((row >= lo + new_count) & (row < lo + 2 * new_count))
+    odd = (row // step_rows) % 2 == 1
     accum = jnp.where(odd, pltpu.roll(picked, 64, 1), picked)
     lane = lax.broadcasted_iota(jnp.int32, (row_count, 128), 1)
     packed = jnp.where(lane < HEAD_DIM, accum, 0.0)
     packed = jnp.where(lane == HEAD_DIM, row_max, packed)
     packed = jnp.where(lane == HEAD_DIM + 1, weight_sum, packed)
     packed = jnp.where(lane == HEAD_DIM + 2, total_ref[0], packed)
-    out_ref[0] = packed
-
-
-def piece_attention(query_blocks, keys, values, bias, live_row, total_row, new_count):
-    req_count, row_count, inner_width = query_blocks.shape
+    own_heads = out_ref.shape[2]
+    for head in range(head_count):
+        out_ref[head // own_heads, 0, head % own_heads] = packed[head * step_rows : (head + 1) * step_rows]
+
+
+def piece_attention(query_rows, keys, values, trailing, prefix_rows, live_row, total_rows, seq_count):
+    req_count, step_rows, inner_width = query_rows.shape
+    head_count = trailing.shape[1]
     piece_len = keys.shape[1]
+    row_count = head_count * step_rows
+    own_heads = head_count // seq_count
     return pl.pallas_call(
-        functools.partial(attention_kernel, new_count=new_count),
+        attention_kernel,
         grid=(req_count,),
         in_specs=[
-            pl.BlockSpec((1, row_count, inner_width), lambda r: (r, 0, 0)),
+            pl.BlockSpec((1, step_rows, inner_width), lambda r: (r, 0, 0)),
             pl.BlockSpec((1, piece_len, inner_width), lambda r: (r, 0, 0)),
             pl.BlockSpec((1, piece_len, inner_width), lambda r: (r, 0, 0)),
-            pl.BlockSpec((1, row_count, piece_len), lambda r: (r, 0, 0)),
+            pl.BlockSpec((1, head_count, piece_len), lambda r: (r, 0, 0)),
+            pl.BlockSpec((1, row_count, 1), lambda r: (r, 0, 0)),
             pl.BlockSpec((1, 1, piece_len), lambda r: (r, 0, 0)),
             pl.BlockSpec((1, row_count, 1), lambda r: (r, 0, 0)),
         ],
-        out_specs=pl.BlockSpec((1, row_count, 128), lambda r: (r, 0, 0)),
-        out_shape=jax.ShapeDtypeStruct((req_count, row_count, 128), jnp.float32),
-    )(query_blocks, keys, values, bias, live_row, total_row)
+        out_specs=pl.BlockSpec((seq_count, 1, own_heads, step_rows, 128), lambda r: (0, r, 0, 0, 0)),
+        out_shape=jax.ShapeDtypeStruct((seq_count, req_count, own_heads, step_rows, 128), jnp.float32),
+    )(query_rows, keys, values, trailing, prefix_rows, live_row, total_rows)
 
 
 def body(
@@ -154,21 +170,20 @@
         "rhl,lj->rhj", masked, later_step, precision=lax.Precision.HIGHEST,
         preferred_element_type=jnp.float32,
     )
-    col_head = jnp.arange(inner_width, dtype=jnp.int32) // HEAD_DIM
-    head_mask = col_head[None, :] == jnp.arange(head_count, dtype=jnp.int32)[:, None]
-    query_blocks = jnp.where(
-        head_mask[None, :, None, :], all_heads[0][:, None, :, :], 0
-    ).reshape(req_count, head_count * new_count, inner_width)
-    bias = (trailing_part[:, :, None, :] + jnp.transpose(prefix, (0, 2, 1))[..., None]).reshape(
-        req_count, head_count * new_count, piece_len
+    step_rows = 8
+    pad_steps = ((0, 0), (0, step_rows - new_count))
+    query_rows = jnp.pad(all_heads[0], pad_steps + ((0, 0),))
+    prefix_rows = jnp.pad(jnp.transpose(prefix, (0, 2, 1)), ((0, 0),) + pad_steps).reshape(
+        req_count, head_count * step_rows, 1
     )
     live_row = live_mask.astype(jnp.float32)[:, None, :]
-    total_row = jnp.broadcast_to(
-        piece_total[:, :, None], (req_count, head_count, new_count)
-    ).reshape(req_count, head_count * new_count, 1)
-    packed = piece_attention(query_blocks, cache_keys, cache_values, bias, live_row, total_row, new_count)
-    packed = packed.reshape(req_count, seq_count, own_heads, new_count, 128).transpose(1, 0, 2, 3, 4)
-    parts = lax.all_to_all(packed, "seq", 0, 0, tiled=True)
+    total_rows = jnp.broadcast_to(
+        piece_total[:, :, None], (req_count, head_count, step_rows)
+    ).reshape(req_count, head_count * step_rows, 1)
+    packed = piece_attention(
+        query_rows, cache_keys, cache_values, trailing_part, prefix_rows, live_row, total_rows, seq_count
+    )
+    parts = lax.all_to_all(packed, "seq", 0, 0, tiled=True)[:, :, :, :new_count]
     part_acc = parts[..., :HEAD_DIM]
     part_max = parts[..., HEAD_DIM]
     part_sum = parts[..., HEAD_DIM + 1]

time: 79.8 us -> 79.6 us (level)
  other arithmetic: 8.76 us -> 5.93 us
  waiting for transfers between devices: 28.4 us -> 30.1 us
    select_n x2 -> x0, other arithmetic: 1.76 us -> none  [the longest x1 1.75 us: body(): jnp.where(head_mask[None, :, None, :], all_heads[0][:, None, :, :], 0)]
    pallas_call x1 -> x0, local copies, waits for them, and re-layouts: 1.69 us -> none  [piece_attention(): pl.pallas_call(functools.partial(attention_kernel, new_count=new_count),...]
    all_to_all x1, waiting for transfers between devices: 8.06 us -> 9.44 us  [body(): parts = lax.all_to_all(packed, 'seq', 0, 0, tiled=True)[:, :, :, :new_count]]
    add x1 -> x0, other arithmetic: 1.29 us -> none  [body(): trailing_part[:, :, None, :] + jnp.transpose(prefix, (0, 2, 1))[..., None]]
    reshape x1 -> x2, local copies, waits for them, and re-layouts: 0.83 us -> 1.86 us  [the longest x1 0.94 us: body(): total_rows = jnp.broadcast_to(piece_total[:, :, None], (req_count, head_c...]
  transfers between devices with their start and end apart: 3 -> 3, of which waited for: 3 -> 3; matrix products, arithmetic and copies ran while one was open for 8% -> 7% of each run, Pallas kernels for 0% -> 0%
where the time goes in v5:
time: 79.6 us; the launch traced here: 79.3 us
  waiting for transfers between devices  30.1 us (38%)
  starting transfers between devices  17.5 us (22%)
  local copies, waits for them, and re-layouts  12.5 us (16%)
  Pallas kernels  8.98 us (11%)
  other arithmetic  5.93 us (7%)
  matrix products  3.87 us (5%)
    all_to_all x1, waiting for transfers between devices, body(): lax.all_to_all(jnp.broadcast_to(hidden_in[None], (fsdp_count, req_count,...  10.7 us
    all_to_all x1, waiting for transfers between devices, body(): incoming = lax.all_to_all(outgoing, ('fsdp', 'seq'), 0, 0, tiled=True)  9.91 us
    all_to_all x1, waiting for transfers between devices, body(): parts = lax.all_to_all(packed, 'seq', 0, 0, tiled=True)[:, :, :, :new_count]  9.44 us
    pallas_call x1, Pallas kernels, piece_attention(): pl.pallas_call(attention_kernel, grid=(req_count,), in_specs=[pl.BlockSpe...  8.98 us
    all_to_all x1, starting transfers between devices, body(): incoming = lax.all_to_all(outgoing, ('fsdp', 'seq'), 0, 0, tiled=True)  7.58 us
    all_to_all x1, starting transfers between devices, body(): lax.all_to_all(jnp.broadcast_to(hidden_in[None], (fsdp_count, req_count,...  6.44 us
    all_to_all x1, starting transfers between devices, body(): parts = lax.all_to_all(packed, 'seq', 0, 0, tiled=True)[:, :, :, :new_count]  3.45 us
    broadcast_in_dim x1, local copies, waits for them, and re-layouts, body(): jnp.broadcast_to(hidden_in[None], (fsdp_count, req_count, new_count, width))  2.08 us
  transfers between devices with their start and end apart: 3, of which 3 were waited for; matrix products, arithmetic and copies ran while one was open for 7% of the time, Pallas kernels for 0%

profile of v5, /device:TPU:0, one launch (start us, length us, event | category | flops | bytes accessed | tf_op | source)
XLA Modules:
  0.0 79.3 jit_solution(16999012226094578989)
XLA Ops:
  0.1 2.1 %broadcast_in_dim.95 = bf16[16,4,5,1536]{3,1,2,0:T(4,128)(2,1)} broadcast(bf16[4,5,1536]{2,0,1:T(4,128)(2,1)} %param.11), dimensions={1,2,3} | broadcast | bytes 1044480 | tf_op jit(solution)/shard_map/broadcast_in_dim | solution.py:115
  2.1 6.4 %all-to-all-start = ((bf16[16,4,5,1536]{3,1,2,0:T(4,128)(2,1)}), bf16[16,4,5,1536]{3,1,2,0:T(4,128)(2,1)S(1)}, u32[]{:S(2)}, u32[]{:S(2)}) async-start(bf16[16,4,5,1536]{3,1,2,0:T(4,128)(2,1)} %broadcast_in_dim.95), calls=%async_computation | async-start | bytes 1966080 | tf_op jit(solution)/shard_map/all_to_all | solution.py:114
  8.6 0.1 fusion.13
  8.7 0.1 select_reduce_fusion.4
  8.9 0.3 fusion.65
  9.2 0.1 add_compare_fusion
  9.3 0.1 select_reduce_fusion
  9.4 0.1 dynamic-slice_bitcast_fusion
  9.5 0.1 copy.245
  9.6 0.1 copy.244
  9.7 0.1 copy.269
  9.9 0.9 %reshape.282.prefix_ref = f32[4,192,1]{2,1,0:T(8,128)} reshape(f32[4,24,8]{2,1,0:T(8,128)S(1)} %pad.9.clone) | data formatting | bytes 6144 | tf_op jit(solution)/shard_map/reshape | solution.py:176
  10.9 0.9 %reshape.283.total_ref = f32[4,192,1]{2,1,0:T(8,128)} reshape(f32[4,24,8]{2,1,0:T(8,128)S(1)} %broadcast_in_dim.152) | data formatting | bytes 6144 | tf_op jit(solution)/shard_map/reshape | solution.py:182
  11.8 0.1 select_reduce_fusion.3
  11.9 0.1 broadcast_compare_fusion
  12.0 0.7 compare_convert_fusion.live_ref
  12.7 1.0 %fusion.9.trail_ref = f32[4,24,512]{2,1,0:T(8,128)} fusion(f32[4,24,512]{2,1,0:T(8,128)S(1)} %copy-done.2, pred[4,512]{1,0:T(4,128)(4,1)S(1)} %add_compare_fusion), kind=kOutput, calls=%fused_computation.15 | convolution fusion | flops 302301184 | bytes 395264 | tf_op jit(solution)/shard_map/rhl,lj->rhj/dot_general | solution.py:169
  13.7 10.7 %all-to-all-done = bf16[16,4,5,1536]{3,1,2,0:T(4,128)(2,1)S(1)} async-done(((bf16[16,4,5,1536]{3,1,2,0:T(4,128)(2,1)}), bf16[16,4,5,1536]{3,1,2,0:T(4,128)(2,1)S(1)}, u32[]{:S(2)}, u32[]{:S(2)}) %all-to-all-start) | async-done | bytes 983072 | tf_op jit(solution)/shard_map/all_to_all | solution.py:114
  24.4 0.6 fusion.3
  25.0 0.6 fusion.5
  25.6 0.3 copy.224
  25.9 0.5 reshape.273
  26.4 0.4 fusion.6
  26.8 0.2 reshape.275
  27.0 0.1 copy.285
  27.2 0.2 broadcast_in_dim.146
  27.4 0.6 broadcast.292
  28.0 0.7 reduce.3
  28.7 0.9 %reshape.288 = bf16[128,2,360]{2,1,0:T(2,128)(2,1)} reshape(bf16[128,720]{1,0:T(8,128)(2,1)S(1)} %reduce.3) | data formatting | bytes 368640
  29.6 7.6 %all-to-all-start.1 = ((bf16[128,2,360]{2,1,0:T(2,128)(2,1)}), bf16[128,2,360]{2,1,0:T(2,128)(2,1)S(1)}, u32[]{:S(2)}, u32[]{:S(2)}) async-start(bf16[128,2,360]{2,1,0:T(2,128)(2,1)} %reshape.288), calls=%async_computation.1 | async-start | bytes 393216 | tf_op jit(solution)/shard_map/all_to_all | solution.py:136
  37.2 9.9 %all-to-all-done.1 = bf16[128,2,360]{2,1,0:T(2,128)(2,1)S(1)} async-done(((bf16[128,2,360]{2,1,0:T(2,128)(2,1)}), bf16[128,2,360]{2,1,0:T(2,128)(2,1)S(1)}, u32[]{:S(2)}, u32[]{:S(2)}) %all-to-all-start.1) | async-done | bytes 184352 | tf_op jit(solution)/shard_map/all_to_all | solution.py:136
  47.1 0.3 reshape.289
  47.5 1.3 %reduce = bf16[128,720]{1,0:T(8,128)(2,1)S(1)} reduce(bf16[128,1,720]{2,1,0:T(2,128)(2,1)S(1)} %reshape.289, bf16[]{:T(256)} %constant.118), dimensions={1}, to_apply=%all_to_all.14.reduce_sub_computation | reduce | bytes 368642 | tf_op jit(solution)/shard_map/all_to_all | solution.py:136
  48.7 0.4 reshape.276
  49.1 1.9 %fusion.2 = bf16[60,1536]{1,0:T(8,128)(2,1)S(1)} fusion(bf16[1536,60]{1,0:T(8,128)(2,1)S(1)} %reshape.276, s32[1536]{0:T(1024)S(1)} %fusion.51), kind=kOutput, calls=%fused_computation.5 | convolution fusion | flops 285566976 | bytes 374784 | tf_op jit(solution)/shard_map/kx,kj->xj/dot_general | solution.py:148
  51.0 0.1 reshape.279
  51.1 0.1 constant_dynamic-slice_fusion
  51.2 0.1 reshape.286
  51.4 0.7 pad.8.q_ref
  52.0 9.0 %shard_map.109 = f32[8,4,3,8,128]{4,3,2,1,0:T(8,128)} custom-call(bf16[4,8,1536]{2,1,0:T(8,128)(2,1)} %pad.8.q_ref, bf16[4,512,1536]{2,1,0:T(8,128)(2,1)} %k_ref.1, bf16[4,512,1536]{2,1,0:T(8,128)(2,1)} %v_ref.1, f32[4,24,512]{2,1,0:T(8,128)} %fusion.9.trail_ref, f32[4,192,1]{2,1,0:T(8,128)} %reshape.282.prefix_ref, ...), custom_call_target="tpu_custom_call" | custom-call | tf_op jit(solution)/shard_map/pallas_call | solution.py:71
  61.0 3.5 %all-to-all-start.2 = ((f32[8,4,3,8,128]{4,3,2,1,0:T(8,128)}), f32[8,4,3,8,128]{4,3,2,1,0:T(8,128)S(1)}, u32[]{:S(2)}, u32[]{:S(2)}) async-start(f32[8,4,3,8,128]{4,3,2,1,0:T(8,128)} %shard_map.109), calls=%async_computation.2 | async-start | bytes 786432 | tf_op jit(solution)/shard_map/all_to_all | solution.py:186
  64.5 0.1 reshape.285
  64.6 0.1 reshape.284
  64.6 0.1 fusion.27
  64.8 0.2 copy.243
  64.9 0.2 select_reduce_fusion.2
  65.1 9.4 %all-to-all-done.2 = f32[8,4,3,8,128]{4,3,2,1,0:T(8,128)S(1)} async-done(((f32[8,4,3,8,128]{4,3,2,1,0:T(8,128)}), f32[8,4,3,8,128]{4,3,2,1,0:T(8,128)S(1)}, u32[]{:S(2)}, u32[]{:S(2)}) %all-to-all-start.2) | async-done | bytes 393248 | tf_op jit(solution)/shard_map/all_to_all | solution.py:186
  74.6 0.2 slice.44
  74.7 0.2 copy.259
  74.9 0.1 select_reduce_fusion.1
  75.0 0.1 copy.232
  75.1 0.2 slice.43
  75.3 0.5 copy.233
  75.7 0.1 fusion.24
  75.8 0.1 copy.235
  76.0 0.2 fusion.68
  76.2 0.4 fusion.71
  76.6 0.9 %copy.260 = f32[8,4,3,5,1]{3,2,1,0,4:T(4,128)S(1)} copy(f32[8,4,3,5,1]{4,3,2,1,0:T(8,128)S(1)} %get-tuple-element.8) | data formatting | bytes 3840 | tf_op jit(solution)/shard_map/mul | solution.py:197
  77.4 0.5 copy.254
  77.9 0.2 fusion.22
  78.1 0.1 fusion.25
  78.3 0.2 fusion.11
  78.4 0.1 select_convert_fusion
  78.6 0.7 convert_element_type.56
  (38 shorter events, 0.3 us)
Async XLA Ops:
  0.0 8.8 %copy-start = (bf16[1536,24]{0,1:T(8,128)(2,1)S(1)}, bf16[1536,24]{0,1:T(8,128)(2,1)}, u32[]{:S(2)}) copy-start(bf16[1536,24]{0,1:T(8,128)(2,1)} %param.14) | copy-start | bytes 221188
  0.0 8.6 %copy-start.1 = (bf16[4,5,1536]{2,0,1:T(4,128)(2,1)S(1)}, bf16[4,5,1536]{2,0,1:T(4,128)(2,1)}, u32[]{:S(2)}) copy-start(bf16[4,5,1536]{2,0,1:T(4,128)(2,1)} %param.11) | copy-start | bytes 184324
  0.0 8.7 %copy-start.5 = (s32[4,8]{1,0:T(4,128)S(1)}, s32[4,8]{1,0:T(4,128)}, u32[]{:S(2)}) copy-start(s32[4,8]{1,0:T(4,128)} %param.20) | copy-start | bytes 388
  0.0 8.9 %copy-start.4 = (f32[1536]{0:T(1024)S(1)}, f32[1536]{0:T(1024)}, u32[]{:S(2)}) copy-start(f32[1536]{0:T(1024)} %param.12) | copy-start | bytes 18436
  0.0 8.9 %copy-start.7 = (f32[24]{0:T(128)S(1)}, f32[24]{0:T(128)}, u32[]{:S(2)}) copy-start(f32[24]{0:T(128)} %param.15) | copy-start | bytes 292
  0.0 9.1 %copy-start.6 = (s32[4]{0:T(128)S(1)}, s32[4]{0:T(128)}, u32[]{:S(2)}) copy-start(s32[4]{0:T(128)} %param.19) | copy-start | bytes 52
  0.0 9.2 %copy-start.2 = (f32[4,24,512]{2,1,0:T(8,128)S(1)}, f32[4,24,512]{2,1,0:T(8,128)}, u32[]{:S(2)}) copy-start(f32[4,24,512]{2,1,0:T(8,128)} %param.18) | copy-start | bytes 589828
  0.0 9.7 %copy-start.3 = (bf16[1536,3,3,4]{0,3,2,1:T(4,128)(2,1)S(1)}, bf16[1536,3,3,4]{0,3,2,1:T(4,128)(2,1)}, u32[]{:S(2)}) copy-start(bf16[1536,3,3,4]{0,3,2,1:T(4,128)(2,1)} %param.13) | copy-start | bytes 331780
  2.1 22.3 %all-to-all-start = ((bf16[16,4,5,1536]{3,1,2,0:T(4,128)(2,1)}), bf16[16,4,5,1536]{3,1,2,0:T(4,128)(2,1)S(1)}, u32[]{:S(2)}, u32[]{:S(2)}) async-start(bf16[16,4,5,1536]{3,1,2,0:T(4,128)(2,1)} %broadcast_in_dim.95), calls=%async_computation | async-start | bytes 1966080 | tf_op jit(solution)/shard_map/all_to_all | solution.py:114
  26.4 10.8 %copy-start.8 = (s32[4]{0:T(128)S(1)}, s32[4]{0:T(128)}, u32[]{:S(2)}) copy-start(s32[4]{0:T(128)} %param.21) | copy-start | bytes 52
  29.6 17.5 %all-to-all-start.1 = ((bf16[128,2,360]{2,1,0:T(2,128)(2,1)}), bf16[128,2,360]{2,1,0:T(2,128)(2,1)S(1)}, u32[]{:S(2)}, u32[]{:S(2)}) async-start(bf16[128,2,360]{2,1,0:T(2,128)(2,1)} %reshape.288), calls=%async_computation.1 | async-start | bytes 393216 | tf_op jit(solution)/shard_map/all_to_all | solution.py:136
  61.0 13.6 %all-to-all-start.2 = ((f32[8,4,3,8,128]{4,3,2,1,0:T(8,128)}), f32[8,4,3,8,128]{4,3,2,1,0:T(8,128)S(1)}, u32[]{:S(2)}, u32[]{:S(2)}) async-start(f32[8,4,3,8,128]{4,3,2,1,0:T(8,128)} %shard_map.109), calls=%async_computation.2 | async-start | bytes 786432 | tf_op jit(solution)/shard_map/all_to_all | solution.py:186

commit v6 on v5

--- a/solution.py
+++ b/solution.py
@@ -111,14 +111,10 @@
     logit_scale = HEAD_DIM ** (-0.5)
     seq_index = lax.axis_index("seq")
     head_start = seq_index * own_heads
-    hidden_all = lax.all_to_all(
-        jnp.broadcast_to(hidden_in[None], (fsdp_count, req_count, new_count, width)),
-        "fsdp",
-        0,
-        0,
-        tiled=True,
-    )
-    normed_all = normalize(hidden_all, norm_gain).reshape(fsdp_count * rows, width)
+    normed = normalize(hidden_in, norm_gain).reshape(rows, width)
+    normed_all = lax.all_to_all(
+        jnp.broadcast_to(normed[None], (fsdp_count, rows, width)), "fsdp", 0, 0, tiled=True
+    ).reshape(fsdp_count * rows, width)
     projected = jnp.einsum(
         "dk,nd->kn",
         w_qkv.reshape(width, own_cols),
@@ -132,7 +128,7 @@
     )
     outgoing = jnp.broadcast_to(
         outgoing, (fsdp_count, seq_count, own_heads * own_dims * 3 * rows)
-    ).reshape(fsdp_count * seq_count, own_heads * own_dims * 3 * rows)
+    ).reshape(fsdp_count * seq_count, 2, own_heads * own_dims * 3 * rows // 2)
     incoming = lax.all_to_all(outgoing, ("fsdp", "seq"), 0, 0, tiled=True)
     incoming = incoming.reshape(fsdp_count * seq_count * own_heads * own_dims, 3 * rows)
     src_row = jnp.arange(fsdp_count * seq_count * own_heads * own_dims, dtype=jnp.int32)
@@ -148,7 +144,6 @@
     all_heads = jnp.einsum(
         "kx,kj->xj", incoming, placement, preferred_element_type=jnp.float32
     ).astype(jnp.bfloat16).reshape(3, req_count, new_count, inner_width)
-    normed = normalize(hidden_in, norm_gain).reshape(rows, width)
     gate_logit = (
         jnp.dot(normed, w_forget, preferred_element_type=jnp.float32).reshape(
             req_count, new_count, head_count

time: 79.6 us -> 78.5 us (0.986)
  waiting for transfers between devices: 30.1 us -> 26.5 us
  other arithmetic: 5.93 us -> 8.15 us
  matrix products: 3.87 us -> 5.37 us
  local copies, waits for them, and re-layouts: 12.5 us -> 11.2 us
    all_to_all x1, waiting for transfers between devices: 10.7 us -> 7.13 us  [body(): lax.all_to_all(jnp.broadcast_to(normed[None], (fsdp_count, rows, width)),...]
    all_to_all x2 -> x0, other arithmetic: 2.01 us -> none  [body(): incoming = lax.all_to_all(outgoing, ('fsdp', 'seq'), 0, 0, tiled=True)]
    unnamed x21 -> x5, local copies, waits for them, and re-layouts: 1.37 us -> 0.11 us
    broadcast_in_dim x1 -> x2, local copies, waits for them, and re-layouts: 2.08 us -> 1.12 us  [body(): jnp.broadcast_to(normed[None], (fsdp_count, rows, width))]
    reduce_sum x1, other arithmetic: 0.1 us -> 1.03 us  [body(): piece_total = jnp.sum(masked, axis=-1)]
    dot_general x1, matrix products: 1.05 us -> 1.97 us  [body(): jnp.einsum('rhl,lj->rhj', masked, later_step, precision=lax.Precision.HIG...]
    reshape x1, local copies, waits for them, and re-layouts: 0.03 us -> 0.93 us  [body(): w_qkv.reshape(width, own_cols)]
  transfers between devices with their start and end apart: 3 -> 3, of which waited for: 3 -> 3; matrix products, arithmetic and copies ran while one was open for 7% -> 15% of each run, Pallas kernels for 0% -> 0%
where the time goes in v6:
time: 78.5 us; the launch traced here: 78 us
  waiting for transfers between devices  26.5 us (34%)
  starting transfers between devices  17.5 us (22%)
  local copies, waits for them, and re-layouts  11.2 us (14%)
  Pallas kernels  8.98 us (11%)
  other arithmetic  8.15 us (10%)
  matrix products  5.37 us (7%)
    all_to_all x1, waiting for transfers between devices, body(): incoming = lax.all_to_all(outgoing, ('fsdp', 'seq'), 0, 0, tiled=True)  9.91 us
    all_to_all x1, waiting for transfers between devices, body(): parts = lax.all_to_all(packed, 'seq', 0, 0, tiled=True)[:, :, :, :new_count]  9.44 us
    pallas_call x1, Pallas kernels, piece_attention(): pl.pallas_call(attention_kernel, grid=(req_count,), in_specs=[pl.BlockSpe...  8.98 us
    all_to_all x1, starting transfers between devices, body(): incoming = lax.all_to_all(outgoing, ('fsdp', 'seq'), 0, 0, tiled=True)  7.6 us
    all_to_all x1, waiting for transfers between devices, body(): lax.all_to_all(jnp.broadcast_to(normed[None], (fsdp_count, rows, width)),...  7.13 us
    all_to_all x1, starting transfers between devices, body(): lax.all_to_all(jnp.broadcast_to(normed[None], (fsdp_count, rows, width)),...  6.43 us
    all_to_all x1, starting transfers between devices, body(): parts = lax.all_to_all(packed, 'seq', 0, 0, tiled=True)[:, :, :, :new_count]  3.45 us
    dot_general x1, matrix products, body(): jnp.einsum('rhl,lj->rhj', masked, later_step, precision=lax.Precision.HIG...  1.97 us
  transfers between devices with their start and end apart: 3, of which 3 were waited for; matrix products, arithmetic and copies ran while one was open for 15% of the time, Pallas kernels for 0%

profile of v6, /device:TPU:0, one launch (start us, length us, event | category | flops | bytes accessed | tf_op | source)
XLA Modules:
  0.0 78.0 jit_solution(15991670722385830482)
XLA Ops:
  0.0 0.0 copy-start
  0.0 0.0 copy-start.1
  0.0 1.0 %fusion.10 = f32[4,5]{0,1:T(8,128)S(1)} fusion(bf16[4,5,1536]{2,0,1:T(4,128)(2,1)} %param.11), kind=kLoop, calls=%fused_computation.19 | loop fusion | flops 92140 | bytes 61520 | tf_op jit(solution)/shard_map/reduce_sum | solution.py:17
  1.0 0.9 %fusion.12 = bf16[4,5,1536]{2,0,1:T(4,128)(2,1)S(1)} fusion(bf16[4,5,1536]{2,0,1:T(4,128)(2,1)} %param.11, f32[1536]{0:T(1024)} %param.12, f32[4,5]{0,1:T(8,128)S(1)} %add_rsqrt_fusion), kind=kLoop, calls=%fused_computation.21 | loop fusion | flops 122880 | bytes 129104 | tf_op jit(solution)/shard_map/convert_element_type | solution.py:18
  2.0 1.1 %broadcast_in_dim.145 = bf16[16,20,1536]{2,1,0:T(8,128)(2,1)} broadcast(bf16[20,1536]{1,0:T(8,128)(2,1)S(1)} %broadcast_in_dim.144), dimensions={1,2} | broadcast | bytes 1044480 | tf_op jit(solution)/shard_map/broadcast_in_dim | solution.py:116
  3.1 6.4 %all-to-all-start = ((bf16[16,20,1536]{2,1,0:T(8,128)(2,1)}), bf16[16,20,1536]{2,1,0:T(8,128)(2,1)S(1)}, u32[]{:S(2)}, u32[]{:S(2)}) async-start(bf16[16,20,1536]{2,1,0:T(8,128)(2,1)} %broadcast_in_dim.145), calls=%async_computation | async-start | bytes 2359296 | tf_op jit(solution)/shard_map/all_to_all | solution.py:115
  9.5 0.8 %select_reduce_fusion.4 = s32[4]{0:T(128)S(1)} fusion(s32[4,8]{1,0:T(4,128)} %param.20, s32[]{:T(128)S(6)} %axis_index.12), kind=kLoop, calls=%fused_computation.106 | loop fusion | flops 92 | bytes 148 | tf_op jit(solution)/shard_map/reduce_sum | solution.py:157
  10.3 0.0 copy-done
  10.3 0.8 %fusion.59 = (u8[4,24]{1,0:T(4,128)(4,1)S(1)}, f32[4,5,24]{2,0,1:T(4,128)S(1)}) fusion(f32[24]{0:T(128)} %param.15, bf16[4,5,1536]{2,0,1:T(4,128)(2,1)S(1)} %fusion.12, bf16[1536,24]{0,1:T(8,128)(2,1)S(1)} %copy-done), kind=kOutput, calls=%fused_computation.105 | convolution fusion | flops 1477824 | bytes 137280 | tf_op jit(solution)/shard_map/dot_general | solution.py:148
  11.2 0.7 add_compare_fusion
  11.9 1.0 %select_reduce_fusion = f32[4,24]{1,0:T(4,128)S(1)} fusion(f32[4,24,512]{2,1,0:T(8,128)} %param.18, pred[4,512]{1,0:T(4,128)(4,1)S(1)} %add_compare_fusion), kind=kLoop, calls=%fused_computation.15 | loop fusion | flops 98208 | bytes 199040 | tf_op jit(solution)/shard_map/reduce_sum | solution.py:162
  13.0 0.1 dynamic-slice_bitcast_fusion
  13.1 0.1 copy.211
  13.2 0.1 copy.210
  13.3 0.9 %reshape.263 = bf16[1536,36]{0,1:T(8,128)(2,1)S(1)} reshape(bf16[1536,3,3,4]{0,3,2,1:T(4,128)(2,1)} %param.13) | data formatting | bytes 221184 | tf_op jit(solution)/shard_map/reshape | solution.py:120
  14.2 0.1 copy.235
  14.4 0.9 %reshape.272.prefix_ref = f32[4,192,1]{2,1,0:T(8,128)} reshape(f32[4,24,8]{2,1,0:T(8,128)S(1)} %pad.9.clone) | data formatting | bytes 6144 | tf_op jit(solution)/shard_map/reshape | solution.py:171
  15.3 0.1 broadcast_in_dim.152
  15.4 0.9 %reshape.273.total_ref = f32[4,192,1]{2,1,0:T(8,128)} reshape(f32[4,24,8]{2,1,0:T(8,128)S(1)} %broadcast_in_dim.152) | data formatting | bytes 6144 | tf_op jit(solution)/shard_map/reshape | solution.py:177
  16.3 0.8 select_reduce_fusion.3
  17.1 0.1 broadcast_compare_fusion
  17.1 1.3 %compare_convert_fusion.live_ref = f32[4,1,512]{2,1,0:T(1,128)} fusion(s32[4]{0:T(128)} %param.19, s32[4]{0:T(128)S(1)} %broadcast_multiply_fusion), kind=kLoop, calls=%fused_computation.26 | loop fusion | flops 6144 | bytes 8224 | tf_op jit(solution)/shard_map/convert_element_type | solution.py:174
  18.5 2.0 %fusion.6.trail_ref = f32[4,24,512]{2,1,0:T(8,128)} fusion(f32[4,24,512]{2,1,0:T(8,128)} %param.18, pred[4,512]{1,0:T(4,128)(4,1)S(1)} %add_compare_fusion), kind=kOutput, calls=%fused_computation.10 | convolution fusion | flops 302301184 | bytes 395264 | tf_op jit(solution)/shard_map/rhl,lj->rhj/dot_general | solution.py:164
  20.4 7.1 %all-to-all-done = bf16[16,20,1536]{2,1,0:T(8,128)(2,1)S(1)} async-done(((bf16[16,20,1536]{2,1,0:T(8,128)(2,1)}), bf16[16,20,1536]{2,1,0:T(8,128)(2,1)S(1)}, u32[]{:S(2)}, u32[]{:S(2)}) %all-to-all-start) | async-done | bytes 983072 | tf_op jit(solution)/shard_map/all_to_all | solution.py:115
  27.6 0.2 reshape.262
  27.8 0.4 fusion.3
  28.2 0.2 reshape.264
  28.5 0.1 copy.251
  28.6 0.2 broadcast_in_dim.146
  28.8 0.9 %reshape.265 = bf16[128,2,360]{2,1,0:T(2,128)(2,1)} reshape(bf16[16,8,720]{2,1,0:T(8,128)(2,1)S(1)} %broadcast_in_dim.147) | data formatting | bytes 368640 | tf_op jit(solution)/shard_map/reshape | solution.py:131
  29.7 7.6 %all-to-all-start.1 = ((bf16[128,2,360]{2,1,0:T(2,128)(2,1)}), bf16[128,2,360]{2,1,0:T(2,128)(2,1)S(1)}, u32[]{:S(2)}, u32[]{:S(2)}) async-start(bf16[128,2,360]{2,1,0:T(2,128)(2,1)} %reshape.265), calls=%async_computation.1 | async-start | bytes 393216 | tf_op jit(solution)/shard_map/all_to_all | solution.py:132
  37.3 0.0 copy-done.1
  37.3 9.9 %all-to-all-done.1 = bf16[128,2,360]{2,1,0:T(2,128)(2,1)S(1)} async-done(((bf16[128,2,360]{2,1,0:T(2,128)(2,1)}), bf16[128,2,360]{2,1,0:T(2,128)(2,1)S(1)}, u32[]{:S(2)}, u32[]{:S(2)}) %all-to-all-start.1) | async-done | bytes 184352 | tf_op jit(solution)/shard_map/all_to_all | solution.py:132
  47.2 0.6 reshape.266
  47.8 1.9 %fusion.2 = bf16[60,1536]{1,0:T(8,128)(2,1)S(1)} fusion(bf16[1536,60]{1,0:T(8,128)(2,1)S(1)} %reshape.266, s32[1536]{0:T(1024)S(1)} %fusion.45), kind=kOutput, calls=%fused_computation.3 | convolution fusion | flops 285566976 | bytes 374784 | tf_op jit(solution)/shard_map/kx,kj->xj/dot_general | solution.py:144
  49.8 0.1 reshape.269
  49.9 0.1 constant_dynamic-slice_fusion
  50.0 0.1 reshape.276
  50.1 0.7 pad.8.q_ref
  50.7 9.0 %shard_map.109 = f32[8,4,3,8,128]{4,3,2,1,0:T(8,128)} custom-call(bf16[4,8,1536]{2,1,0:T(8,128)(2,1)} %pad.8.q_ref, bf16[4,512,1536]{2,1,0:T(8,128)(2,1)} %k_ref.1, bf16[4,512,1536]{2,1,0:T(8,128)(2,1)} %v_ref.1, f32[4,24,512]{2,1,0:T(8,128)} %fusion.6.trail_ref, f32[4,192,1]{2,1,0:T(8,128)} %reshape.272.prefix_ref, ...), custom_call_target="tpu_custom_call" | custom-call | tf_op jit(solution)/shard_map/pallas_call | solution.py:71
  59.7 3.5 %all-to-all-start.2 = ((f32[8,4,3,8,128]{4,3,2,1,0:T(8,128)}), f32[8,4,3,8,128]{4,3,2,1,0:T(8,128)S(1)}, u32[]{:S(2)}, u32[]{:S(2)}) async-start(f32[8,4,3,8,128]{4,3,2,1,0:T(8,128)} %shard_map.109), calls=%async_computation.2 | async-start | bytes 786432 | tf_op jit(solution)/shard_map/all_to_all | solution.py:181
  63.2 0.1 reshape.275
  63.3 0.1 reshape.274
  63.4 0.1 fusion.21
  63.5 0.2 copy.209
  63.6 0.2 select_reduce_fusion.2
  63.8 9.4 %all-to-all-done.2 = f32[8,4,3,8,128]{4,3,2,1,0:T(8,128)S(1)} async-done(((f32[8,4,3,8,128]{4,3,2,1,0:T(8,128)}), f32[8,4,3,8,128]{4,3,2,1,0:T(8,128)S(1)}, u32[]{:S(2)}, u32[]{:S(2)}) %all-to-all-start.2) | async-done | bytes 393248 | tf_op jit(solution)/shard_map/all_to_all | solution.py:181
  73.3 0.2 slice.44
  73.4 0.2 copy.225
  73.6 0.1 select_reduce_fusion.1
  73.7 0.1 copy.198
  73.8 0.2 slice.43
  74.0 0.5 copy.199
  74.5 0.1 fusion.18
  74.6 0.1 copy.201
  74.7 0.2 fusion.62
  74.9 0.4 fusion.65
  75.3 0.9 %copy.226 = f32[8,4,3,5,1]{3,2,1,0,4:T(4,128)S(1)} copy(f32[8,4,3,5,1]{4,3,2,1,0:T(8,128)S(1)} %get-tuple-element.8) | data formatting | bytes 3840 | tf_op jit(solution)/shard_map/mul | solution.py:192
  76.1 0.5 copy.220
  76.6 0.2 fusion.16
  76.8 0.1 fusion.19
  77.0 0.2 fusion.8
  77.1 0.1 select_convert_fusion
  77.3 0.7 convert_element_type.48
  (19 shorter events, 0.2 us)
Async XLA Ops:
  0.0 10.3 %copy-start = (bf16[1536,24]{0,1:T(8,128)(2,1)S(1)}, bf16[1536,24]{0,1:T(8,128)(2,1)}, u32[]{:S(2)}) copy-start(bf16[1536,24]{0,1:T(8,128)(2,1)} %param.14) | copy-start | bytes 221188
  0.0 37.3 %copy-start.1 = (s32[4]{0:T(128)S(1)}, s32[4]{0:T(128)}, u32[]{:S(2)}) copy-start(s32[4]{0:T(128)} %param.21) | copy-start | bytes 52
  3.1 24.5 %all-to-all-start = ((bf16[16,20,1536]{2,1,0:T(8,128)(2,1)}), bf16[16,20,1536]{2,1,0:T(8,128)(2,1)S(1)}, u32[]{:S(2)}, u32[]{:S(2)}) async-start(bf16[16,20,1536]{2,1,0:T(8,128)(2,1)} %broadcast_in_dim.145), calls=%async_computation | async-start | bytes 2359296 | tf_op jit(solution)/shard_map/all_to_all | solution.py:115
  29.7 17.5 %all-to-all-start.1 = ((bf16[128,2,360]{2,1,0:T(2,128)(2,1)}), bf16[128,2,360]{2,1,0:T(2,128)(2,1)S(1)}, u32[]{:S(2)}, u32[]{:S(2)}) async-start(bf16[128,2,360]{2,1,0:T(2,128)(2,1)} %reshape.265), calls=%async_computation.1 | async-start | bytes 393216 | tf_op jit(solution)/shard_map/all_to_all | solution.py:132
  59.7 13.6 %all-to-all-start.2 = ((f32[8,4,3,8,128]{4,3,2,1,0:T(8,128)}), f32[8,4,3,8,128]{4,3,2,1,0:T(8,128)S(1)}, u32[]{:S(2)}, u32[]{:S(2)}) async-start(f32[8,4,3,8,128]{4,3,2,1,0:T(8,128)} %shard_map.109), calls=%async_computation.2 | async-start | bytes 786432 | tf_op jit(solution)/shard_map/all_to_all | solution.py:181

commit v7 on v6

--- a/solution.py
+++ b/solution.py
@@ -16,6 +16,22 @@
     values = rows.astype(jnp.float32)
     mean_sq = jnp.mean(values * values, axis=-1, keepdims=True)
     return (values * lax.rsqrt(mean_sq + norm_eps) * gain).astype(jnp.bfloat16)
+
+
+def normalize_kernel(rows_ref, gain_ref, out_ref):
+    values = rows_ref[...].astype(jnp.float32)
+    mean_sq = jnp.mean(values * values, axis=-1, keepdims=True)
+    normed = (values * lax.rsqrt(mean_sq + norm_eps) * gain_ref[...]).astype(jnp.bfloat16)
+    for copy in range(out_ref.shape[0]):
+        out_ref[copy] = normed
+
+
+def normalize_copies(rows, gain, copies):
+    row_count, width = rows.shape
+    return pl.pallas_call(
+        normalize_kernel,
+        out_shape=jax.ShapeDtypeStruct((copies, row_count, width), jnp.bfloat16),
+    )(rows, gain.reshape(1, width))
 
 
 def attention_kernel(q_ref, k_ref, v_ref, trail_ref, prefix_ref, live_ref, total_ref, out_ref):
@@ -111,10 +127,11 @@
     logit_scale = HEAD_DIM ** (-0.5)
     seq_index = lax.axis_index("seq")
     head_start = seq_index * own_heads
-    normed = normalize(hidden_in, norm_gain).reshape(rows, width)
-    normed_all = lax.all_to_all(
-        jnp.broadcast_to(normed[None], (fsdp_count, rows, width)), "fsdp", 0, 0, tiled=True
-    ).reshape(fsdp_count * rows, width)
+    normed_copies = normalize_copies(hidden_in.reshape(rows, width), norm_gain, fsdp_count)
+    normed = normed_copies[0]
+    normed_all = lax.all_to_all(normed_copies, "fsdp", 0, 0, tiled=True).reshape(
+        fsdp_count * rows, width
+    )
     projected = jnp.einsum(
         "dk,nd->kn",
         w_qkv.reshape(width, own_cols),

time: 78.5 us -> 80.4 us (1.024)
  local copies, waits for them, and re-layouts: 11.2 us -> 13.8 us
  Pallas kernels: 8.98 us -> 11 us
  other arithmetic: 8.15 us -> 6.25 us
  waiting for transfers between devices: 26.5 us -> 25.6 us
    pallas_call x0 -> x1, Pallas kernels: none -> 2.07 us  [normalize_copies(): pl.pallas_call(normalize_kernel, out_shape=jax.ShapeDtypeStruct((copies,...]
    reshape x1 -> x3, local copies, waits for them, and re-layouts: 0.23 us -> 2.18 us  [the longest x1 1.29 us: normalize_copies(): gain.reshape(1, width)]
    broadcast_in_dim x2 -> x0, local copies, waits for them, and re-layouts: 1.12 us -> none  [body(): jnp.broadcast_to(normed[None], (fsdp_count, rows, width))]
    reduce_sum x1 -> x0, other arithmetic: 0.98 us -> none  [normalize(): mean_sq = jnp.mean(values * values, axis=-1, keepdims=True)]
    convert_element_type x1 -> x0, other arithmetic: 0.93 us -> none  [normalize(): return (values * lax.rsqrt(mean_sq + norm_eps) * gain).astype(jnp.bfloat16)]
    all_to_all x1, waiting for transfers between devices: 7.13 us -> 6.2 us  [body(): lax.all_to_all(normed_copies, 'fsdp', 0, 0, tiled=True)]
    slice x0 -> x1, local copies, waits for them, and re-layouts: none -> 0.89 us  [body(): normed = normed_copies[0]]
    unnamed x5 -> x6, local copies, waits for them, and re-layouts: 0.11 us -> 0.99 us
  transfers between devices with their start and end apart: 3 -> 3, of which waited for: 3 -> 3; matrix products, arithmetic and copies ran while one was open for 15% -> 16% of each run, Pallas kernels for 0% -> 0%
where the time goes in v7:
time: 80.4 us; the launch traced here: 79.8 us
  waiting for transfers between devices  25.6 us (32%)
  starting transfers between devices  17.5 us (22%)
  local copies, waits for them, and re-layouts  13.8 us (17%)
  Pallas kernels  11 us (14%)
  other arithmetic  6.25 us (8%)
  matrix products  5.37 us (7%)
    all_to_all x1, waiting for transfers between devices, body(): incoming = lax.all_to_all(outgoing, ('fsdp', 'seq'), 0, 0, tiled=True)  9.91 us
    all_to_all x1, waiting for transfers between devices, body(): parts = lax.all_to_all(packed, 'seq', 0, 0, tiled=True)[:, :, :, :new_count]  9.45 us
    pallas_call x1, Pallas kernels, piece_attention(): pl.pallas_call(attention_kernel, grid=(req_count,), in_specs=[pl.BlockSpe...  8.98 us
    all_to_all x1, starting transfers between devices, body(): incoming = lax.all_to_all(outgoing, ('fsdp', 'seq'), 0, 0, tiled=True)  7.6 us
    all_to_all x1, starting transfers between devices, body(): lax.all_to_all(normed_copies, 'fsdp', 0, 0, tiled=True)  6.43 us
    all_to_all x1, waiting for transfers between devices, body(): lax.all_to_all(normed_copies, 'fsdp', 0, 0, tiled=True)  6.2 us
    all_to_all x1, starting transfers between devices, body(): parts = lax.all_to_all(packed, 'seq', 0, 0, tiled=True)[:, :, :, :new_count]  3.45 us
    pallas_call x1, Pallas kernels, normalize_copies(): pl.pallas_call(normalize_kernel, out_shape=jax.ShapeDtypeStruct((copies,...  2.07 us
  transfers between devices with their start and end apart: 3, of which 3 were waited for; matrix products, arithmetic and copies ran while one was open for 16% of the time, Pallas kernels for 0%

profile of v7, /device:TPU:0, one launch (start us, length us, event | category | flops | bytes accessed | tf_op | source)
XLA Modules:
  0.0 79.8 jit_solution(4226128382130895463)
XLA Ops:
  0.0 0.0 copy-start
  0.0 0.9 %copy.190 = bf16[4,5,1536]{2,1,0:T(8,128)(2,1)S(1)} copy(bf16[4,5,1536]{2,0,1:T(4,128)(2,1)} %param.11) | data formatting | bytes 122880 | tf_op args[0]
  0.9 0.7 reshape.257.rows_ref
  1.5 1.3 %reshape.258.gain_ref = f32[1,1536]{1,0:T(1,128)} reshape(f32[1536]{0:T(1024)} %param.12) | data formatting | bytes 12288 | tf_op jit(solution)/shard_map/reshape | solution.py:34
  2.8 2.1 %shard_map.109 = bf16[16,20,1536]{2,1,0:T(8,128)(2,1)} custom-call(bf16[20,1536]{1,0:T(8,128)(2,1)} %reshape.257.rows_ref, f32[1,1536]{1,0:T(1,128)} %reshape.258.gain_ref), custom_call_target="tpu_custom_call" | custom-call | tf_op jit(solution)/shard_map/pallas_call | solution.py:31
  4.9 6.4 %all-to-all-start = ((bf16[16,20,1536]{2,1,0:T(8,128)(2,1)}), bf16[16,20,1536]{2,1,0:T(8,128)(2,1)S(1)}, u32[]{:S(2)}, u32[]{:S(2)}) async-start(bf16[16,20,1536]{2,1,0:T(8,128)(2,1)} %shard_map.109), calls=%async_computation | async-start | bytes 2359296 | tf_op jit(solution)/shard_map/all_to_all | solution.py:132
  11.4 0.9 %slice.46 = bf16[1,20,1536]{2,1,0:T(8,128)(2,1)S(1)} slice(bf16[16,20,1536]{2,1,0:T(8,128)(2,1)} %shard_map.109), slice={[0:1], [0:20], [0:1536]} | slice | bytes 122880 | tf_op jit(solution)/shard_map/slice | solution.py:131
  12.2 0.8 select_reduce_fusion.4
  13.1 0.7 add_compare_fusion
  13.8 0.0 copy-done
  13.8 0.8 %fusion.46 = (u8[5,24]{1,0:T(8,128)(4,1)S(1)}, f32[4,5,24]{2,1,0:T(8,128)S(1)}) fusion(f32[24]{0:T(128)} %param.15, bf16[4,5,1536]{2,1,0:T(8,128)(2,1)S(1)} %dot_general.25, bf16[1536,24]{0,1:T(8,128)(2,1)S(1)} %copy-done), kind=kOutput, calls=%fused_computation.88 | convolution fusion | flops 1477800 | bytes 137304 | tf_op jit(solution)/shard_map/dot_general | solution.py:165
  14.7 1.0 %select_reduce_fusion = f32[4,24]{1,0:T(4,128)S(1)} fusion(f32[4,24,512]{2,1,0:T(8,128)} %param.18, pred[4,512]{1,0:T(4,128)(4,1)S(1)} %add_compare_fusion), kind=kLoop, calls=%fused_computation.15 | loop fusion | flops 98208 | bytes 199040 | tf_op jit(solution)/shard_map/reduce_sum | solution.py:179
  15.7 0.1 dynamic-slice_bitcast_fusion
  15.8 0.1 copy.210
  15.9 0.1 copy.209
  16.1 0.9 %reshape.260 = bf16[1536,36]{0,1:T(8,128)(2,1)S(1)} reshape(bf16[1536,3,3,4]{0,3,2,1:T(4,128)(2,1)} %param.13) | data formatting | bytes 221184 | tf_op jit(solution)/shard_map/reshape | solution.py:137
  17.0 0.1 copy.234
  17.1 0.9 %reshape.269.prefix_ref = f32[4,192,1]{2,1,0:T(8,128)} reshape(f32[4,24,8]{2,1,0:T(8,128)S(1)} %pad.9.clone) | data formatting | bytes 6144 | tf_op jit(solution)/shard_map/reshape | solution.py:188
  18.1 0.1 broadcast_in_dim.141
  18.1 0.9 %reshape.270.total_ref = f32[4,192,1]{2,1,0:T(8,128)} reshape(f32[4,24,8]{2,1,0:T(8,128)S(1)} %broadcast_in_dim.141) | data formatting | bytes 6144 | tf_op jit(solution)/shard_map/reshape | solution.py:194
  19.1 0.8 select_reduce_fusion.3
  19.8 0.1 broadcast_compare_fusion
  19.9 1.3 %compare_convert_fusion.live_ref = f32[4,1,512]{2,1,0:T(1,128)} fusion(s32[4]{0:T(128)} %param.19, s32[4]{0:T(128)S(1)} %broadcast_multiply_fusion), kind=kLoop, calls=%fused_computation.21 | loop fusion | flops 6144 | bytes 8224 | tf_op jit(solution)/shard_map/convert_element_type | solution.py:191
  21.2 2.0 %fusion.6.trail_ref = f32[4,24,512]{2,1,0:T(8,128)} fusion(f32[4,24,512]{2,1,0:T(8,128)} %param.18, pred[4,512]{1,0:T(4,128)(4,1)S(1)} %add_compare_fusion), kind=kOutput, calls=%fused_computation.10 | convolution fusion | flops 302301184 | bytes 395264 | tf_op jit(solution)/shard_map/rhl,lj->rhj/dot_general | solution.py:181
  23.2 6.2 %all-to-all-done = bf16[16,20,1536]{2,1,0:T(8,128)(2,1)S(1)} async-done(((bf16[16,20,1536]{2,1,0:T(8,128)(2,1)}), bf16[16,20,1536]{2,1,0:T(8,128)(2,1)S(1)}, u32[]{:S(2)}, u32[]{:S(2)}) %all-to-all-start) | async-done | bytes 983072 | tf_op jit(solution)/shard_map/all_to_all | solution.py:132
  29.4 0.2 reshape.259
  29.6 0.4 fusion.3
  30.0 0.2 reshape.261
  30.3 0.1 copy.250
  30.4 0.2 broadcast_in_dim.135
  30.6 0.9 %reshape.262 = bf16[128,2,360]{2,1,0:T(2,128)(2,1)} reshape(bf16[16,8,720]{2,1,0:T(8,128)(2,1)S(1)} %broadcast_in_dim.136) | data formatting | bytes 368640 | tf_op jit(solution)/shard_map/reshape | solution.py:148
  31.5 7.6 %all-to-all-start.1 = ((bf16[128,2,360]{2,1,0:T(2,128)(2,1)}), bf16[128,2,360]{2,1,0:T(2,128)(2,1)S(1)}, u32[]{:S(2)}, u32[]{:S(2)}) async-start(bf16[128,2,360]{2,1,0:T(2,128)(2,1)} %reshape.262), calls=%async_computation.1 | async-start | bytes 393216 | tf_op jit(solution)/shard_map/all_to_all | solution.py:149
  39.2 9.9 %all-to-all-done.1 = bf16[128,2,360]{2,1,0:T(2,128)(2,1)S(1)} async-done(((bf16[128,2,360]{2,1,0:T(2,128)(2,1)}), bf16[128,2,360]{2,1,0:T(2,128)(2,1)S(1)}, u32[]{:S(2)}, u32[]{:S(2)}) %all-to-all-start.1) | async-done | bytes 184352 | tf_op jit(solution)/shard_map/all_to_all | solution.py:149
  49.1 0.6 reshape.263
  49.6 1.9 %fusion.2 = bf16[60,1536]{1,0:T(8,128)(2,1)S(1)} fusion(bf16[1536,60]{1,0:T(8,128)(2,1)S(1)} %reshape.263, s32[1536]{0:T(1024)S(1)} %fusion.33), kind=kOutput, calls=%fused_computation.3 | convolution fusion | flops 285566976 | bytes 374784 | tf_op jit(solution)/shard_map/kx,kj->xj/dot_general | solution.py:161
  51.6 0.1 reshape.266
  51.7 0.1 constant_dynamic-slice_fusion
  51.8 0.1 reshape.273
  51.9 0.7 pad.8.q_ref
  52.6 9.0 %shard_map.110 = f32[8,4,3,8,128]{4,3,2,1,0:T(8,128)} custom-call(bf16[4,8,1536]{2,1,0:T(8,128)(2,1)} %pad.8.q_ref, bf16[4,512,1536]{2,1,0:T(8,128)(2,1)} %k_ref.1, bf16[4,512,1536]{2,1,0:T(8,128)(2,1)} %v_ref.1, f32[4,24,512]{2,1,0:T(8,128)} %fusion.6.trail_ref, f32[4,192,1]{2,1,0:T(8,128)} %reshape.269.prefix_ref, ...), custom_call_target="tpu_custom_call" | custom-call | tf_op jit(solution)/shard_map/pallas_call | solution.py:87
  61.6 3.5 %all-to-all-start.2 = ((f32[8,4,3,8,128]{4,3,2,1,0:T(8,128)}), f32[8,4,3,8,128]{4,3,2,1,0:T(8,128)S(1)}, u32[]{:S(2)}, u32[]{:S(2)}) async-start(f32[8,4,3,8,128]{4,3,2,1,0:T(8,128)} %shard_map.110), calls=%async_computation.2 | async-start | bytes 786432 | tf_op jit(solution)/shard_map/all_to_all | solution.py:198
  65.0 0.1 reshape.272
  65.1 0.1 reshape.271
  65.2 0.1 fusion.18
  65.3 0.2 copy.208
  65.5 0.2 select_reduce_fusion.2
  65.7 9.5 %all-to-all-done.2 = f32[8,4,3,8,128]{4,3,2,1,0:T(8,128)S(1)} async-done(((f32[8,4,3,8,128]{4,3,2,1,0:T(8,128)}), f32[8,4,3,8,128]{4,3,2,1,0:T(8,128)S(1)}, u32[]{:S(2)}, u32[]{:S(2)}) %all-to-all-start.2) | async-done | bytes 393248 | tf_op jit(solution)/shard_map/all_to_all | solution.py:198
  75.1 0.2 slice.49
  75.3 0.2 copy.224
  75.4 0.1 select_reduce_fusion.1
  75.6 0.1 copy.197
  75.7 0.2 slice.48
  75.8 0.5 copy.198
  76.3 0.1 fusion.15
  76.4 0.1 copy.200
  76.5 0.2 fusion.48
  76.7 0.4 fusion.51
  77.1 0.9 %copy.225 = f32[8,4,3,5,1]{3,2,1,0,4:T(4,128)S(1)} copy(f32[8,4,3,5,1]{4,3,2,1,0:T(8,128)S(1)} %get-tuple-element.8) | data formatting | bytes 3840 | tf_op jit(solution)/shard_map/mul | solution.py:209
  78.0 0.5 copy.219
  78.5 0.2 fusion.13
  78.7 0.1 fusion.16
  78.8 0.2 fusion.8
  79.0 0.1 select_convert_fusion
  79.1 0.7 convert_element_type.40
  (19 shorter events, 0.2 us)
Async XLA Ops:
  0.0 13.8 %copy-start = (bf16[1536,24]{0,1:T(8,128)(2,1)S(1)}, bf16[1536,24]{0,1:T(8,128)(2,1)}, u32[]{:S(2)}) copy-start(bf16[1536,24]{0,1:T(8,128)(2,1)} %param.14) | copy-start | bytes 221188
  0.0 39.1 %copy-start.1 = (s32[4]{0:T(128)S(1)}, s32[4]{0:T(128)}, u32[]{:S(2)}) copy-start(s32[4]{0:T(128)} %param.21) | copy-start | bytes 52
  4.9 24.5 %all-to-all-start = ((bf16[16,20,1536]{2,1,0:T(8,128)(2,1)}), bf16[16,20,1536]{2,1,0:T(8,128)(2,1)S(1)}, u32[]{:S(2)}, u32[]{:S(2)}) async-start(bf16[16,20,1536]{2,1,0:T(8,128)(2,1)} %shard_map.109), calls=%async_computation | async-start | bytes 2359296 | tf_op jit(solution)/shard_map/all_to_all | solution.py:132
  31.5 17.5 %all-to-all-start.1 = ((bf16[128,2,360]{2,1,0:T(2,128)(2,1)}), bf16[128,2,360]{2,1,0:T(2,128)(2,1)S(1)}, u32[]{:S(2)}, u32[]{:S(2)}) async-start(bf16[128,2,360]{2,1,0:T(2,128)(2,1)} %reshape.262), calls=%async_computation.1 | async-start | bytes 393216 | tf_op jit(solution)/shard_map/all_to_all | solution.py:149
  61.6 13.6 %all-to-all-start.2 = ((f32[8,4,3,8,128]{4,3,2,1,0:T(8,128)}), f32[8,4,3,8,128]{4,3,2,1,0:T(8,128)S(1)}, u32[]{:S(2)}, u32[]{:S(2)}) async-start(f32[8,4,3,8,128]{4,3,2,1,0:T(8,128)} %shard_map.110), calls=%async_computation.2 | async-start | bytes 786432 | tf_op jit(solution)/shard_map/all_to_all | solution.py:198

commit v8 on v6

--- a/solution.py
+++ b/solution.py
@@ -178,6 +178,33 @@
     packed = piece_attention(
         query_rows, cache_keys, cache_values, trailing_part, prefix_rows, live_row, total_rows, seq_count
     )
+    own_rows = lax.dynamic_slice_in_dim(
+        all_heads, head_start * HEAD_DIM, own_heads * HEAD_DIM, 3
+    ).reshape(3, req_count, new_count, own_heads, HEAD_DIM)
+    own_prefix = jnp.transpose(
+        lax.dynamic_slice_in_dim(prefix, head_start, own_heads, 2), (0, 2, 1)
+    )
+    fresh_logits = (
+        jnp.einsum(
+            "rmhd,rnhd->rhmn",
+            own_rows[0],
+            own_rows[1],
+            preferred_element_type=jnp.float32,
+        )
+        * logit_scale
+    )
+    fresh_logits = fresh_logits + own_prefix[..., :, None] - own_prefix[..., None, :]
+    step_ids = jnp.arange(new_count, dtype=jnp.int32)
+    causal = (step_ids[None, :] <= step_ids[:, None])[None, None]
+    fresh_max = jnp.max(jnp.where(causal, fresh_logits, neg_fill), axis=-1)
+    new_weights = jnp.where(causal, jnp.exp(fresh_logits - fresh_max[..., None]), 0.0)
+    fresh_sum = jnp.sum(new_weights, axis=-1)
+    fresh_acc = jnp.einsum(
+        "rhmn,rnhd->rhmd",
+        new_weights.astype(jnp.bfloat16),
+        own_rows[2],
+        preferred_element_type=jnp.float32,
+    )
     parts = lax.all_to_all(packed, "seq", 0, 0, tiled=True)[:, :, :, :new_count]
     part_acc = parts[..., :HEAD_DIM]
     part_max = parts[..., HEAD_DIM]
@@ -186,38 +213,11 @@
     later_piece = (piece_of_slot.T[None, :, :] > piece_of_slot.T[:, None, :])[..., None]
     later_sum = jnp.sum(jnp.where(later_piece, part_total[None], 0.0), axis=1)
     part_max = part_max + later_sum[..., None]
-    cache_max = jnp.max(part_max, axis=0)
-    factor = jnp.exp(part_max - cache_max[None])
-    cache_sum = jnp.sum(part_sum * factor, axis=0)
-    cache_acc = jnp.sum(part_acc * factor[..., None], axis=0)
-    own_rows = lax.dynamic_slice_in_dim(
-        all_heads, head_start * HEAD_DIM, own_heads * HEAD_DIM, 3
-    ).reshape(3, req_count, new_count, own_heads, HEAD_DIM)
-    own_prefix = jnp.transpose(
-        lax.dynamic_slice_in_dim(prefix, head_start, own_heads, 2), (0, 2, 1)
-    )
-    fresh_logits = (
-        jnp.einsum(
-            "rmhd,rnhd->rhmn",
-            own_rows[0],
-            own_rows[1],
-            preferred_element_type=jnp.float32,
-        )
-        * logit_scale
-    )
-    fresh_logits = fresh_logits + own_prefix[..., :, None] - own_prefix[..., None, :]
-    step_ids = jnp.arange(new_count, dtype=jnp.int32)
-    causal = (step_ids[None, :] <= step_ids[:, None])[None, None]
-    joint_max = jnp.maximum(cache_max, jnp.max(jnp.where(causal, fresh_logits, neg_fill), axis=-1))
-    new_weights = jnp.where(causal, jnp.exp(fresh_logits - joint_max[..., None]), 0.0)
-    carried = jnp.exp(cache_max - joint_max)
-    total_sum = cache_sum * carried + jnp.sum(new_weights, axis=-1)
-    blend_weights = cache_acc * carried[..., None] + jnp.einsum(
-        "rhmn,rnhd->rhmd",
-        new_weights.astype(jnp.bfloat16),
-        own_rows[2],
-        preferred_element_type=jnp.float32,
-    )
+    joint_max = jnp.maximum(jnp.max(part_max, axis=0), fresh_max)
+    factor = jnp.exp(part_max - joint_max[None])
+    carried = jnp.exp(fresh_max - joint_max)
+    total_sum = jnp.sum(part_sum * factor, axis=0) + fresh_sum * carried
+    blend_weights = jnp.sum(part_acc * factor[..., None], axis=0) + fresh_acc * carried[..., None]
     result = blend_weights / total_sum[..., None]
     live_rows = (step_ids[None, :] <= draft_counts[:, None])[:, None, :, None]
     result = jnp.where(live_rows, result, 0.0)

time: 78.5 us -> 78.7 us (level)
  no operation moved by 1% of the time
where the time goes in v8:
time: 78.7 us; the launch traced here: 78.1 us
  waiting for transfers between devices  26.6 us (34%)
  starting transfers between devices  17.5 us (22%)
  local copies, waits for them, and re-layouts  11.2 us (14%)
  Pallas kernels  8.98 us (11%)
  other arithmetic  8.14 us (10%)
  matrix products  5.38 us (7%)
    all_to_all x1, waiting for transfers between devices, body(): incoming = lax.all_to_all(outgoing, ('fsdp', 'seq'), 0, 0, tiled=True)  9.91 us
    all_to_all x1, waiting for transfers between devices, body(): parts = lax.all_to_all(packed, 'seq', 0, 0, tiled=True)[:, :, :, :new_count]  9.59 us
    pallas_call x1, Pallas kernels, piece_attention(): pl.pallas_call(attention_kernel, grid=(req_count,), in_specs=[pl.BlockSpe...  8.98 us
    all_to_all x1, starting transfers between devices, body(): incoming = lax.all_to_all(outgoing, ('fsdp', 'seq'), 0, 0, tiled=True)  7.6 us
    all_to_all x1, waiting for transfers between devices, body(): lax.all_to_all(jnp.broadcast_to(normed[None], (fsdp_count, rows, width)),...  7.12 us
    all_to_all x1, starting transfers between devices, body(): lax.all_to_all(jnp.broadcast_to(normed[None], (fsdp_count, rows, width)),...  6.43 us
    all_to_all x1, starting transfers between devices, body(): parts = lax.all_to_all(packed, 'seq', 0, 0, tiled=True)[:, :, :, :new_count]  3.45 us
    dot_general x1, matrix products, body(): jnp.einsum('rhl,lj->rhj', masked, later_step, precision=lax.Precision.HIG...  1.97 us
  transfers between devices with their start and end apart: 3, of which 3 were waited for; matrix products, arithmetic and copies ran while one was open for 15% of the time, Pallas kernels for 0%

profile of v8, /device:TPU:0, one launch (start us, length us, event | category | flops | bytes accessed | tf_op | source)
XLA Modules:
  0.0 78.1 jit_solution(14028012931453706866)
XLA Ops:
  0.0 0.0 copy-start
  0.0 0.0 copy-start.1
  0.0 1.0 %fusion.10 = f32[4,5]{0,1:T(8,128)S(1)} fusion(bf16[4,5,1536]{2,0,1:T(4,128)(2,1)} %param.11), kind=kLoop, calls=%fused_computation.19 | loop fusion | flops 92140 | bytes 61520 | tf_op jit(solution)/shard_map/reduce_sum | solution.py:17
  1.0 0.9 %fusion.12 = bf16[4,5,1536]{2,0,1:T(4,128)(2,1)S(1)} fusion(bf16[4,5,1536]{2,0,1:T(4,128)(2,1)} %param.11, f32[1536]{0:T(1024)} %param.12, f32[4,5]{0,1:T(8,128)S(1)} %add_rsqrt_fusion), kind=kLoop, calls=%fused_computation.21 | loop fusion | flops 122880 | bytes 129104 | tf_op jit(solution)/shard_map/convert_element_type | solution.py:18
  2.0 1.1 %broadcast_in_dim.145 = bf16[16,20,1536]{2,1,0:T(8,128)(2,1)} broadcast(bf16[20,1536]{1,0:T(8,128)(2,1)S(1)} %broadcast_in_dim.144), dimensions={1,2} | broadcast | bytes 1044480 | tf_op jit(solution)/shard_map/broadcast_in_dim | solution.py:116
  3.1 6.4 %all-to-all-start = ((bf16[16,20,1536]{2,1,0:T(8,128)(2,1)}), bf16[16,20,1536]{2,1,0:T(8,128)(2,1)S(1)}, u32[]{:S(2)}, u32[]{:S(2)}) async-start(bf16[16,20,1536]{2,1,0:T(8,128)(2,1)} %broadcast_in_dim.145), calls=%async_computation | async-start | bytes 2359296 | tf_op jit(solution)/shard_map/all_to_all | solution.py:115
  9.5 0.0 copy-done
  9.5 0.8 %fusion.61 = (u8[4,24]{1,0:T(4,128)(4,1)S(1)}, f32[4,5,24]{2,0,1:T(4,128)S(1)}) fusion(f32[24]{0:T(128)} %param.15, bf16[4,5,1536]{2,0,1:T(4,128)(2,1)S(1)} %fusion.12, bf16[1536,24]{0,1:T(8,128)(2,1)S(1)} %copy-done), kind=kOutput, calls=%fused_computation.105 | convolution fusion | flops 1477824 | bytes 137280 | tf_op jit(solution)/shard_map/dot_general | solution.py:148
  10.4 0.8 %select_reduce_fusion.4 = s32[4]{0:T(128)S(1)} fusion(s32[4,8]{1,0:T(4,128)} %param.20, s32[]{:T(128)S(6)} %axis_index.12), kind=kLoop, calls=%fused_computation.106 | loop fusion | flops 92 | bytes 148 | tf_op jit(solution)/shard_map/reduce_sum | solution.py:157
  11.2 0.1 dynamic-slice_bitcast_fusion
  11.3 0.7 add_compare_fusion
  12.0 1.0 %select_reduce_fusion = f32[4,24]{1,0:T(4,128)S(1)} fusion(f32[4,24,512]{2,1,0:T(8,128)} %param.18, pred[4,512]{1,0:T(4,128)(4,1)S(1)} %add_compare_fusion), kind=kLoop, calls=%fused_computation.15 | loop fusion | flops 98208 | bytes 199040 | tf_op jit(solution)/shard_map/reduce_sum | solution.py:162
  13.1 0.1 copy.206
  13.2 0.1 copy.205
  13.3 0.9 %reshape.264 = bf16[1536,36]{0,1:T(8,128)(2,1)S(1)} reshape(bf16[1536,3,3,4]{0,3,2,1:T(4,128)(2,1)} %param.13) | data formatting | bytes 221184 | tf_op jit(solution)/shard_map/reshape | solution.py:120
  14.2 0.1 copy.235
  14.4 0.9 %reshape.273.prefix_ref = f32[4,192,1]{2,1,0:T(8,128)} reshape(f32[4,24,8]{2,1,0:T(8,128)S(1)} %pad.9.clone) | data formatting | bytes 6144 | tf_op jit(solution)/shard_map/reshape | solution.py:171
  15.3 0.1 broadcast_in_dim.152
  15.4 0.9 %reshape.274.total_ref = f32[4,192,1]{2,1,0:T(8,128)} reshape(f32[4,24,8]{2,1,0:T(8,128)S(1)} %broadcast_in_dim.152) | data formatting | bytes 6144 | tf_op jit(solution)/shard_map/reshape | solution.py:177
  16.3 0.8 select_reduce_fusion.3
  17.1 0.1 broadcast_compare_fusion
  17.2 1.3 %compare_convert_fusion.live_ref = f32[4,1,512]{2,1,0:T(1,128)} fusion(s32[4]{0:T(128)} %param.19, s32[4]{0:T(128)S(1)} %broadcast_multiply_fusion), kind=kLoop, calls=%fused_computation.26 | loop fusion | flops 6144 | bytes 8224 | tf_op jit(solution)/shard_map/convert_element_type | solution.py:174
  18.5 2.0 %fusion.6.trail_ref = f32[4,24,512]{2,1,0:T(8,128)} fusion(f32[4,24,512]{2,1,0:T(8,128)} %param.18, pred[4,512]{1,0:T(4,128)(4,1)S(1)} %add_compare_fusion), kind=kOutput, calls=%fused_computation.10 | convolution fusion | flops 302301184 | bytes 395264 | tf_op jit(solution)/shard_map/rhl,lj->rhj/dot_general | solution.py:164
  20.5 7.1 %all-to-all-done = bf16[16,20,1536]{2,1,0:T(8,128)(2,1)S(1)} async-done(((bf16[16,20,1536]{2,1,0:T(8,128)(2,1)}), bf16[16,20,1536]{2,1,0:T(8,128)(2,1)S(1)}, u32[]{:S(2)}, u32[]{:S(2)}) %all-to-all-start) | async-done | bytes 983072 | tf_op jit(solution)/shard_map/all_to_all | solution.py:115
  27.6 0.2 reshape.263
  27.8 0.4 fusion.3
  28.2 0.2 reshape.265
  28.5 0.1 copy.251
  28.6 0.2 broadcast_in_dim.146
  28.8 0.9 %reshape.266 = bf16[128,2,360]{2,1,0:T(2,128)(2,1)} reshape(bf16[16,8,720]{2,1,0:T(8,128)(2,1)S(1)} %broadcast_in_dim.147) | data formatting | bytes 368640 | tf_op jit(solution)/shard_map/reshape | solution.py:131
  29.7 7.6 %all-to-all-start.1 = ((bf16[128,2,360]{2,1,0:T(2,128)(2,1)}), bf16[128,2,360]{2,1,0:T(2,128)(2,1)S(1)}, u32[]{:S(2)}, u32[]{:S(2)}) async-start(bf16[128,2,360]{2,1,0:T(2,128)(2,1)} %reshape.266), calls=%async_computation.1 | async-start | bytes 393216 | tf_op jit(solution)/shard_map/all_to_all | solution.py:132
  37.3 0.0 copy-done.1
  37.3 9.9 %all-to-all-done.1 = bf16[128,2,360]{2,1,0:T(2,128)(2,1)S(1)} async-done(((bf16[128,2,360]{2,1,0:T(2,128)(2,1)}), bf16[128,2,360]{2,1,0:T(2,128)(2,1)S(1)}, u32[]{:S(2)}, u32[]{:S(2)}) %all-to-all-start.1) | async-done | bytes 184352 | tf_op jit(solution)/shard_map/all_to_all | solution.py:132
  47.2 0.6 reshape.267
  47.8 1.9 %fusion.2 = bf16[60,1536]{1,0:T(8,128)(2,1)S(1)} fusion(bf16[1536,60]{1,0:T(8,128)(2,1)S(1)} %reshape.267, s32[1536]{0:T(1024)S(1)} %fusion.47), kind=kOutput, calls=%fused_computation.3 | convolution fusion | flops 285566976 | bytes 374784 | tf_op jit(solution)/shard_map/kx,kj->xj/dot_general | solution.py:144
  49.8 0.1 reshape.270
  49.9 0.1 constant_dynamic-slice_fusion
  50.0 0.1 reshape.277
  50.0 0.1 reshape.276
  50.1 0.1 reshape.275
  50.2 0.1 fusion.22
  50.4 0.2 copy.204
  50.6 0.7 pad.8.q_ref
  51.2 9.0 %shard_map.109 = f32[8,4,3,8,128]{4,3,2,1,0:T(8,128)} custom-call(bf16[4,8,1536]{2,1,0:T(8,128)(2,1)} %pad.8.q_ref, bf16[4,512,1536]{2,1,0:T(8,128)(2,1)} %k_ref.1, bf16[4,512,1536]{2,1,0:T(8,128)(2,1)} %v_ref.1, f32[4,24,512]{2,1,0:T(8,128)} %fusion.6.trail_ref, f32[4,192,1]{2,1,0:T(8,128)} %reshape.273.prefix_ref, ...), custom_call_target="tpu_custom_call" | custom-call | tf_op jit(solution)/shard_map/pallas_call | solution.py:71
  60.2 3.5 %all-to-all-start.2 = ((f32[8,4,3,8,128]{4,3,2,1,0:T(8,128)}), f32[8,4,3,8,128]{4,3,2,1,0:T(8,128)S(1)}, u32[]{:S(2)}, u32[]{:S(2)}) async-start(f32[8,4,3,8,128]{4,3,2,1,0:T(8,128)} %shard_map.109), calls=%async_computation.2 | async-start | bytes 786432 | tf_op jit(solution)/shard_map/all_to_all | solution.py:208
  63.7 0.2 select_reduce_fusion.2
  63.8 0.2 fusion.64
  64.0 0.1 fusion.20
  64.2 9.6 %all-to-all-done.2 = f32[8,4,3,8,128]{4,3,2,1,0:T(8,128)S(1)} async-done(((f32[8,4,3,8,128]{4,3,2,1,0:T(8,128)}), f32[8,4,3,8,128]{4,3,2,1,0:T(8,128)S(1)}, u32[]{:S(2)}, u32[]{:S(2)}) %all-to-all-start.2) | async-done | bytes 393248 | tf_op jit(solution)/shard_map/all_to_all | solution.py:208
  73.7 0.2 slice.44
  73.9 0.2 copy.225
  74.1 0.1 select_reduce_fusion.1
  74.2 0.1 copy.197
  74.3 0.2 slice.43
  74.5 0.5 copy.198
  74.9 0.1 fusion.19
  75.1 0.1 copy.209
  75.2 0.4 fusion.67
  75.6 0.9 %copy.230 = f32[8,4,3,5,1]{3,2,1,0,4:T(4,128)S(1)} copy(f32[8,4,3,5,1]{4,3,2,1,0:T(8,128)S(1)} %get-tuple-element.8) | data formatting | bytes 3840 | tf_op jit(solution)/shard_map/mul | solution.py:220
  76.4 0.5 copy.220
  76.9 0.2 fusion.16
  77.1 0.2 fusion.8
  77.3 0.1 select_convert_fusion
  77.4 0.7 convert_element_type.48
  (19 shorter events, 0.2 us)
Async XLA Ops:
  0.0 9.5 %copy-start = (bf16[1536,24]{0,1:T(8,128)(2,1)S(1)}, bf16[1536,24]{0,1:T(8,128)(2,1)}, u32[]{:S(2)}) copy-start(bf16[1536,24]{0,1:T(8,128)(2,1)} %param.14) | copy-start | bytes 221188
  0.0 37.3 %copy-start.1 = (s32[4]{0:T(128)S(1)}, s32[4]{0:T(128)}, u32[]{:S(2)}) copy-start(s32[4]{0:T(128)} %param.21) | copy-start | bytes 52
  3.1 24.5 %all-to-all-start = ((bf16[16,20,1536]{2,1,0:T(8,128)(2,1)}), bf16[16,20,1536]{2,1,0:T(8,128)(2,1)S(1)}, u32[]{:S(2)}, u32[]{:S(2)}) async-start(bf16[16,20,1536]{2,1,0:T(8,128)(2,1)} %broadcast_in_dim.145), calls=%async_computation | async-start | bytes 2359296 | tf_op jit(solution)/shard_map/all_to_all | solution.py:115
  29.7 17.5 %all-to-all-start.1 = ((bf16[128,2,360]{2,1,0:T(2,128)(2,1)}), bf16[128,2,360]{2,1,0:T(2,128)(2,1)S(1)}, u32[]{:S(2)}, u32[]{:S(2)}) async-start(bf16[128,2,360]{2,1,0:T(2,128)(2,1)} %reshape.266), calls=%async_computation.1 | async-start | bytes 393216 | tf_op jit(solution)/shard_map/all_to_all | solution.py:132
  60.2 13.6 %all-to-all-start.2 = ((f32[8,4,3,8,128]{4,3,2,1,0:T(8,128)}), f32[8,4,3,8,128]{4,3,2,1,0:T(8,128)S(1)}, u32[]{:S(2)}, u32[]{:S(2)}) async-start(f32[8,4,3,8,128]{4,3,2,1,0:T(8,128)} %shard_map.109), calls=%async_computation.2 | async-start | bytes 786432 | tf_op jit(solution)/shard_map/all_to_all | solution.py:208

commit v9 on v8

--- a/solution.py
+++ b/solution.py
@@ -16,6 +16,32 @@
     values = rows.astype(jnp.float32)
     mean_sq = jnp.mean(values * values, axis=-1, keepdims=True)
     return (values * lax.rsqrt(mean_sq + norm_eps) * gain).astype(jnp.bfloat16)
+
+
+def fold_kernel(parts_ref, later_ref, fresh_ref, keep_ref, out_ref):
+    source_count = parts_ref.shape[0]
+    fresh = fresh_ref[...]
+    raised = []
+    for source in range(source_count):
+        later = jnp.zeros_like(fresh[:, :1])
+        for other in range(source_count):
+            later = later + later_ref[source, other] * parts_ref[other][:, HEAD_DIM + 2 : HEAD_DIM + 3]
+        raised.append(parts_ref[source][:, HEAD_DIM : HEAD_DIM + 1] + later)
+    joint = fresh[:, HEAD_DIM : HEAD_DIM + 1]
+    for value in raised:
+        joint = jnp.maximum(joint, value)
+    blend = fresh * jnp.exp(fresh[:, HEAD_DIM : HEAD_DIM + 1] - joint)
+    for source in range(source_count):
+        blend = blend + parts_ref[source] * jnp.exp(raised[source] - joint)
+    result = blend[:, :HEAD_DIM] / blend[:, HEAD_DIM + 1 : HEAD_DIM + 2]
+    out_ref[...] = jnp.where(keep_ref[...] > 0.5, result, 0.0).astype(out_ref.dtype)
+
+
+def fold_partials(parts, later_rows, fresh_rows, keep_rows):
+    return pl.pallas_call(
+        fold_kernel,
+        out_shape=jax.ShapeDtypeStruct((parts.shape[1], HEAD_DIM), jnp.bfloat16),
+    )(parts, later_rows, fresh_rows, keep_rows)
 
 
 def attention_kernel(q_ref, k_ref, v_ref, trail_ref, prefix_ref, live_ref, total_ref, out_ref):
@@ -205,26 +231,33 @@
         own_rows[2],
         preferred_element_type=jnp.float32,
     )
-    parts = lax.all_to_all(packed, "seq", 0, 0, tiled=True)[:, :, :, :new_count]
-    part_acc = parts[..., :HEAD_DIM]
-    part_max = parts[..., HEAD_DIM]
-    part_sum = parts[..., HEAD_DIM + 1]
-    part_total = parts[:, :, :, 0, HEAD_DIM + 2]
-    later_piece = (piece_of_slot.T[None, :, :] > piece_of_slot.T[:, None, :])[..., None]
-    later_sum = jnp.sum(jnp.where(later_piece, part_total[None], 0.0), axis=1)
-    part_max = part_max + later_sum[..., None]
-    joint_max = jnp.maximum(jnp.max(part_max, axis=0), fresh_max)
-    factor = jnp.exp(part_max - joint_max[None])
-    carried = jnp.exp(fresh_max - joint_max)
-    total_sum = jnp.sum(part_sum * factor, axis=0) + fresh_sum * carried
-    blend_weights = jnp.sum(part_acc * factor[..., None], axis=0) + fresh_acc * carried[..., None]
-    result = blend_weights / total_sum[..., None]
-    live_rows = (step_ids[None, :] <= draft_counts[:, None])[:, None, :, None]
-    result = jnp.where(live_rows, result, 0.0)
+    pad_rows = ((0, 0), (0, 0), (0, step_rows - new_count))
+    fresh_rows = jnp.concatenate(
+        [
+            jnp.pad(fresh_acc, pad_rows + ((0, 0),)),
+            jnp.pad(fresh_max, pad_rows)[..., None],
+            jnp.pad(fresh_sum, pad_rows)[..., None],
+            jnp.zeros((req_count, own_heads, step_rows, 128 - HEAD_DIM - 2), jnp.float32),
+        ],
+        axis=-1,
+    ).reshape(req_count * own_heads * step_rows, 128)
+    later_piece = (piece_of_slot.T[:, None, :] < piece_of_slot.T[None, :, :]).astype(jnp.float32)
+    later_rows = jnp.broadcast_to(
+        later_piece[:, :, :, None, None], (seq_count, seq_count, req_count, own_heads, step_rows)
+    ).reshape(seq_count, seq_count, req_count * own_heads * step_rows, 1)
+    pad_ids = jnp.arange(step_rows, dtype=jnp.int32)
+    keep_rows = jnp.broadcast_to(
+        (pad_ids[None, :] <= draft_counts[:, None]).astype(jnp.float32)[:, None, :],
+        (req_count, own_heads, step_rows),
+    ).reshape(req_count * own_heads * step_rows, 1)
+    parts = lax.all_to_all(packed, "seq", 0, 0, tiled=True).reshape(
+        seq_count, req_count * own_heads * step_rows, 128
+    )
+    folded = fold_partials(parts, later_rows, fresh_rows, keep_rows)
+    result = folded.reshape(req_count, own_heads, step_rows, HEAD_DIM)[:, :, :new_count]
     return (
         jnp.transpose(result, (0, 2, 1, 3))
         .reshape(req_count, new_count, own_heads * HEAD_DIM)
-        .astype(jnp.bfloat16)
     )
 
 

time: 78.7 us -> 80.2 us (1.019)
  other arithmetic: 8.14 us -> 4.28 us
  Pallas kernels: 8.98 us -> 12.2 us
  waiting for transfers between devices: 26.6 us -> 28.6 us
  local copies, waits for them, and re-layouts: 11.2 us -> 13.1 us
  matrix products: 5.38 us -> 3.81 us
    reshape x0 -> x3, local copies, waits for them, and re-layouts: none -> 3.56 us  [the longest x1 2.17 us: body(): later_rows = jnp.broadcast_to(later_piece[:, :, :, None, None], (seq_coun...]
    all_to_all x1, waiting for transfers between devices: 7.12 us -> 10.4 us  [body(): lax.all_to_all(jnp.broadcast_to(normed[None], (fsdp_count, rows, width)),...]
    pallas_call x0 -> x1, Pallas kernels: none -> 3.2 us  [fold_partials(): pl.pallas_call(fold_kernel, out_shape=jax.ShapeDtypeStruct((parts.shape[1...]
    unnamed x5 -> x20, local copies, waits for them, and re-layouts: 0.11 us -> 1.84 us
    slice x5 -> x1, local copies, waits for them, and re-layouts: 1.35 us -> 0.1 us  [body(): own_rows[2]]
    reduce_sum x1, other arithmetic: 1.02 us -> 0.1 us  [body(): piece_total = jnp.sum(masked, axis=-1)]
    dot_general x1, matrix products: 1.97 us -> 1.07 us  [body(): jnp.einsum('rhl,lj->rhj', masked, later_step, precision=lax.Precision.HIG...]
    reshape x1, local copies, waits for them, and re-layouts: 0.93 us -> 0.03 us  [body(): w_qkv.reshape(width, own_cols)]
  transfers between devices with their start and end apart: 3 -> 3, of which waited for: 3 -> 3; matrix products, arithmetic and copies ran while one was open for 15% -> 12% of each run, Pallas kernels for 0% -> 0%
where the time goes in v9:
time: 80.2 us; the launch traced here: 79.8 us
  waiting for transfers between devices  28.6 us (36%)
  starting transfers between devices  17.5 us (22%)
  local copies, waits for them, and re-layouts  13.1 us (16%)
  Pallas kernels  12.2 us (15%)
  other arithmetic  4.28 us (5%)
  matrix products  3.81 us (5%)
    all_to_all x1, waiting for transfers between devices, body(): lax.all_to_all(jnp.broadcast_to(normed[None], (fsdp_count, rows, width)),...  10.4 us
    all_to_all x1, waiting for transfers between devices, body(): incoming = lax.all_to_all(outgoing, ('fsdp', 'seq'), 0, 0, tiled=True)  9.26 us
    pallas_call x1, Pallas kernels, piece_attention(): pl.pallas_call(attention_kernel, grid=(req_count,), in_specs=[pl.BlockSpe...  8.99 us
    all_to_all x1, waiting for transfers between devices, body(): lax.all_to_all(packed, 'seq', 0, 0, tiled=True)  8.93 us
    all_to_all x1, starting transfers between devices, body(): incoming = lax.all_to_all(outgoing, ('fsdp', 'seq'), 0, 0, tiled=True)  7.6 us
    all_to_all x1, starting transfers between devices, body(): lax.all_to_all(jnp.broadcast_to(normed[None], (fsdp_count, rows, width)),...  6.44 us
    all_to_all x1, starting transfers between devices, body(): lax.all_to_all(packed, 'seq', 0, 0, tiled=True)  3.45 us
    pallas_call x1, Pallas kernels, fold_partials(): pl.pallas_call(fold_kernel, out_shape=jax.ShapeDtypeStruct((parts.shape[1...  3.2 us
  transfers between devices with their start and end apart: 3, of which 3 were waited for; matrix products, arithmetic and copies ran while one was open for 12% of the time, Pallas kernels for 0%

profile of v9, /device:TPU:0, one launch (start us, length us, event | category | flops | bytes accessed | tf_op | source)
XLA Modules:
  0.0 79.8 jit_solution(8270716466757142972)
XLA Ops:
  0.0 0.0 copy-start
  0.0 0.0 copy-start.2
  0.0 0.0 copy-start.3
  0.0 1.1 %fusion.9 = f32[4,5]{0,1:T(8,128)S(1)} fusion(bf16[4,5,1536]{2,0,1:T(4,128)(2,1)} %param.11), kind=kLoop, calls=%fused_computation.16 | loop fusion | flops 92140 | bytes 61520 | tf_op jit(solution)/shard_map/reduce_sum | solution.py:17
  1.1 0.9 %fusion.11 = bf16[4,5,1536]{2,0,1:T(4,128)(2,1)S(1)} fusion(bf16[4,5,1536]{2,0,1:T(4,128)(2,1)} %param.11, f32[1536]{0:T(1024)} %param.12, f32[4,5]{0,1:T(8,128)S(1)} %add_rsqrt_fusion), kind=kLoop, calls=%fused_computation.18 | loop fusion | flops 122880 | bytes 129104 | tf_op jit(solution)/shard_map/convert_element_type | solution.py:18
  2.1 1.1 %broadcast_in_dim.75 = bf16[16,20,1536]{2,1,0:T(8,128)(2,1)} broadcast(bf16[20,1536]{1,0:T(8,128)(2,1)S(1)} %broadcast_in_dim.74), dimensions={1,2} | broadcast | bytes 1044480 | tf_op jit(solution)/shard_map/broadcast_in_dim | solution.py:142
  3.2 6.4 %all-to-all-start = ((bf16[16,20,1536]{2,1,0:T(8,128)(2,1)}), bf16[16,20,1536]{2,1,0:T(8,128)(2,1)S(1)}, u32[]{:S(2)}, u32[]{:S(2)}) async-start(bf16[16,20,1536]{2,1,0:T(8,128)(2,1)} %broadcast_in_dim.75), calls=%async_computation | async-start | bytes 2359296 | tf_op jit(solution)/shard_map/all_to_all | solution.py:141
  9.7 0.0 copy-start.6
  9.7 0.0 copy-done.4
  9.7 0.1 select_reduce_fusion.2
  9.8 0.1 select_reduce_fusion.3
  9.9 0.0 copy-done.7
  9.9 0.2 fusion.54
  10.1 0.1 add_compare_fusion
  10.2 0.1 select_reduce_fusion
  10.3 0.1 dynamic-slice_bitcast_fusion
  10.4 0.1 copy.97
  10.5 0.1 copy.98
  10.7 0.1 copy.116
  10.8 0.9 %reshape.273.prefix_ref = f32[4,192,1]{2,1,0:T(8,128)} reshape(f32[4,24,8]{2,1,0:T(8,128)S(1)} %pad.20.clone) | data formatting | bytes 6144 | tf_op jit(solution)/shard_map/reshape | solution.py:197
  11.7 0.1 broadcast_in_dim.129
  11.8 0.9 %reshape.274.total_ref = f32[4,192,1]{2,1,0:T(8,128)} reshape(f32[4,24,8]{2,1,0:T(8,128)S(1)} %broadcast_in_dim.129) | data formatting | bytes 6144 | tf_op jit(solution)/shard_map/reshape | solution.py:203
  12.7 0.1 copy.90
  12.8 0.3 broadcast_in_dim.132
  13.2 2.2 %reshape.275.later_ref = f32[8,8,96,1]{3,2,1,0:T(8,128)} reshape(f32[8,8,4,3,8]{4,3,2,1,0:T(4,128)S(1)} %broadcast_in_dim.132) | data formatting | bytes 49152 | tf_op jit(solution)/shard_map/reshape | solution.py:247
  15.3 0.1 fusion.55
  15.4 0.7 reshape.279.keep_ref
  16.1 0.1 pad.27.clone
  16.2 1.1 %fusion.6.trail_ref = f32[4,24,512]{2,1,0:T(8,128)} fusion(f32[4,24,512]{2,1,0:T(8,128)S(1)} %copy-done.2, pred[4,512]{1,0:T(4,128)(4,1)S(1)} %add_compare_fusion), kind=kOutput, calls=%fused_computation.10 | convolution fusion | flops 302301184 | bytes 395264 | tf_op jit(solution)/shard_map/rhl,lj->rhj/dot_general | solution.py:190
  17.3 10.4 %all-to-all-done = bf16[16,20,1536]{2,1,0:T(8,128)(2,1)S(1)} async-done(((bf16[16,20,1536]{2,1,0:T(8,128)(2,1)}), bf16[16,20,1536]{2,1,0:T(8,128)(2,1)S(1)}, u32[]{:S(2)}, u32[]{:S(2)}) %all-to-all-start) | async-done | bytes 983072 | tf_op jit(solution)/shard_map/all_to_all | solution.py:141
  27.7 0.2 reshape.258
  28.0 0.4 fusion.3
  28.3 0.2 reshape.260
  28.6 0.1 copy.129
  28.7 0.2 broadcast_in_dim.76
  28.9 0.9 %reshape.261 = bf16[128,2,360]{2,1,0:T(2,128)(2,1)} reshape(bf16[16,8,720]{2,1,0:T(8,128)(2,1)S(1)} %broadcast_in_dim.77) | data formatting | bytes 368640 | tf_op jit(solution)/shard_map/reshape | solution.py:157
  29.8 7.6 %all-to-all-start.1 = ((bf16[128,2,360]{2,1,0:T(2,128)(2,1)}), bf16[128,2,360]{2,1,0:T(2,128)(2,1)S(1)}, u32[]{:S(2)}, u32[]{:S(2)}) async-start(bf16[128,2,360]{2,1,0:T(2,128)(2,1)} %reshape.261), calls=%async_computation.1 | async-start | bytes 393216 | tf_op jit(solution)/shard_map/all_to_all | solution.py:158
  37.5 0.7 compare_convert_fusion.1.live_ref
  38.1 9.3 %all-to-all-done.1 = bf16[128,2,360]{2,1,0:T(2,128)(2,1)S(1)} async-done(((bf16[128,2,360]{2,1,0:T(2,128)(2,1)}), bf16[128,2,360]{2,1,0:T(2,128)(2,1)S(1)}, u32[]{:S(2)}, u32[]{:S(2)}) %all-to-all-start.1) | async-done | bytes 184352 | tf_op jit(solution)/shard_map/all_to_all | solution.py:158
  47.4 0.6 reshape.262
  48.0 1.9 %fusion.2 = bf16[60,1536]{1,0:T(8,128)(2,1)S(1)} fusion(bf16[1536,60]{1,0:T(8,128)(2,1)S(1)} %reshape.262, s32[1536]{0:T(1024)S(1)} %fusion.40), kind=kOutput, calls=%fused_computation.3 | convolution fusion | flops 285566976 | bytes 374784 | tf_op jit(solution)/shard_map/kx,kj->xj/dot_general | solution.py:170
  49.9 0.1 reshape.267
  50.0 0.1 constant_dynamic-slice_fusion.1
  50.1 0.1 reshape.276
  50.2 0.1 reshape.277
  50.3 0.1 fusion.17
  50.4 0.2 copy.96
  50.6 0.2 select_reduce_fusion.1
  50.7 0.2 fusion.59
  50.9 0.1 copy.117
  51.1 0.1 reshape.278
  51.2 0.7 pad.19.q_ref
  51.8 9.0 %shard_map.109 = f32[8,4,3,8,128]{4,3,2,1,0:T(8,128)} custom-call(bf16[4,8,1536]{2,1,0:T(8,128)(2,1)} %pad.19.q_ref, bf16[4,512,1536]{2,1,0:T(8,128)(2,1)} %k_ref.1, bf16[4,512,1536]{2,1,0:T(8,128)(2,1)} %v_ref.1, f32[4,24,512]{2,1,0:T(8,128)} %fusion.6.trail_ref, f32[4,192,1]{2,1,0:T(8,128)} %reshape.273.prefix_ref, ...), custom_call_target="tpu_custom_call" | custom-call | tf_op jit(solution)/shard_map/pallas_call | solution.py:97
  60.8 3.5 %all-to-all-start.2 = ((f32[8,4,3,8,128]{4,3,2,1,0:T(8,128)}), f32[8,4,3,8,128]{4,3,2,1,0:T(8,128)S(1)}, u32[]{:S(2)}, u32[]{:S(2)}) async-start(f32[8,4,3,8,128]{4,3,2,1,0:T(8,128)} %shard_map.109), calls=%async_computation.2 | async-start | bytes 786432 | tf_op jit(solution)/shard_map/all_to_all | solution.py:253
  64.3 0.1 fusion.15
  64.4 0.1 copy.118
  64.5 0.1 concatenate.15
  64.7 0.1 concatenate.14
  64.7 0.7 maximum_maximum_fusion.fresh_ref
  65.5 8.9 %all-to-all-done.2 = f32[8,4,3,8,128]{4,3,2,1,0:T(8,128)S(1)} async-done(((f32[8,4,3,8,128]{4,3,2,1,0:T(8,128)}), f32[8,4,3,8,128]{4,3,2,1,0:T(8,128)S(1)}, u32[]{:S(2)}, u32[]{:S(2)}) %all-to-all-start.2) | async-done | bytes 393248 | tf_op jit(solution)/shard_map/all_to_all | solution.py:253
  74.4 0.7 copy-done.1
  75.1 3.2 %shard_map.110 = bf16[96,64]{1,0:T(8,128)(2,1)} custom-call(f32[8,96,128]{2,1,0:T(8,128)} %bitcast.32, f32[8,8,96,1]{3,2,1,0:T(8,128)} %reshape.275.later_ref, f32[96,128]{1,0:T(8,128)} %maximum_maximum_fusion.fresh_ref, f32[96,1]{1,0:T(8,128)} %reshape.279.keep_ref), custom_call_target="tpu_custom_call" | custom-call | tf_op jit(solution)/shard_map/pallas_call | solution.py:41
  78.3 0.7 copy.130
  79.1 0.7 reshape.270
  (28 shorter events, 0.3 us)
Async XLA Ops:
  0.0 9.9 %copy-start = (bf16[1536,24]{0,1:T(8,128)(2,1)S(1)}, bf16[1536,24]{0,1:T(8,128)(2,1)}, u32[]{:S(2)}) copy-start(bf16[1536,24]{0,1:T(8,128)(2,1)} %param.14) | copy-start | bytes 221188
  0.0 9.7 %copy-start.4 = (s32[4,8]{1,0:T(4,128)S(1)}, s32[4,8]{1,0:T(4,128)}, u32[]{:S(2)}) copy-start(s32[4,8]{1,0:T(4,128)} %param.20) | copy-start | bytes 388
  0.0 9.9 %copy-start.7 = (f32[24]{0:T(128)S(1)}, f32[24]{0:T(128)}, u32[]{:S(2)}) copy-start(f32[24]{0:T(128)} %param.15) | copy-start | bytes 292
  0.0 10.1 %copy-start.5 = (s32[4]{0:T(128)S(1)}, s32[4]{0:T(128)}, u32[]{:S(2)}) copy-start(s32[4]{0:T(128)} %param.19) | copy-start | bytes 52
  0.0 10.2 %copy-start.2 = (f32[4,24,512]{2,1,0:T(8,128)S(1)}, f32[4,24,512]{2,1,0:T(8,128)}, u32[]{:S(2)}) copy-start(f32[4,24,512]{2,1,0:T(8,128)} %param.18) | copy-start | bytes 589828
  0.0 10.6 %copy-start.3 = (bf16[1536,3,3,4]{0,3,2,1:T(4,128)(2,1)S(1)}, bf16[1536,3,3,4]{0,3,2,1:T(4,128)(2,1)}, u32[]{:S(2)}) copy-start(bf16[1536,3,3,4]{0,3,2,1:T(4,128)(2,1)} %param.13) | copy-start | bytes 331780
  3.2 24.5 %all-to-all-start = ((bf16[16,20,1536]{2,1,0:T(8,128)(2,1)}), bf16[16,20,1536]{2,1,0:T(8,128)(2,1)S(1)}, u32[]{:S(2)}, u32[]{:S(2)}) async-start(bf16[16,20,1536]{2,1,0:T(8,128)(2,1)} %broadcast_in_dim.75), calls=%async_computation | async-start | bytes 2359296 | tf_op jit(solution)/shard_map/all_to_all | solution.py:141
  9.7 5.7 %copy-start.6 = (s32[4]{0:T(128)S(1)}, s32[4]{0:T(128)}, u32[]{:S(2)}) copy-start(s32[4]{0:T(128)} %param.21) | copy-start | bytes 52
  29.8 17.5 %all-to-all-start.1 = ((bf16[128,2,360]{2,1,0:T(2,128)(2,1)}), bf16[128,2,360]{2,1,0:T(2,128)(2,1)S(1)}, u32[]{:S(2)}, u32[]{:S(2)}) async-start(bf16[128,2,360]{2,1,0:T(2,128)(2,1)} %reshape.261), calls=%async_computation.1 | async-start | bytes 393216 | tf_op jit(solution)/shard_map/all_to_all | solution.py:158
  60.8 13.6 %all-to-all-start.2 = ((f32[8,4,3,8,128]{4,3,2,1,0:T(8,128)}), f32[8,4,3,8,128]{4,3,2,1,0:T(8,128)S(1)}, u32[]{:S(2)}, u32[]{:S(2)}) async-start(f32[8,4,3,8,128]{4,3,2,1,0:T(8,128)} %shard_map.109), calls=%async_computation.2 | async-start | bytes 786432 | tf_op jit(solution)/shard_map/all_to_all | solution.py:253
  74.4 0.7 copy-start.1

commit v10 on v6

--- a/solution.py
+++ b/solution.py
@@ -19,15 +19,19 @@
 
 
 def attention_kernel(q_ref, k_ref, v_ref, trail_ref, prefix_ref, live_ref, total_ref, out_ref):
-    step_rows = q_ref.shape[1]
     head_count = trail_ref.shape[1]
     piece_len = trail_ref.shape[2]
-    inner_width = q_ref.shape[2]
-    row_count = head_count * step_rows
+    row_count = prefix_ref.shape[1]
+    step_rows = row_count // head_count
+    query_count, inner_width = q_ref.shape
+    new_count = query_count // 3 // pl.num_programs(0)
     pair_count = inner_width // 128
-    row_step = lax.broadcasted_iota(jnp.int32, (row_count, step_rows), 0) % step_rows
-    spread = (row_step == lax.broadcasted_iota(jnp.int32, (row_count, step_rows), 1)).astype(jnp.bfloat16)
-    repeated = jnp.dot(spread, q_ref[0], preferred_element_type=jnp.float32)
+    row_step = lax.broadcasted_iota(jnp.int32, (row_count, query_count), 0) % step_rows
+    source = lax.broadcasted_iota(jnp.int32, (row_count, query_count), 1)
+    spread = (
+        (source == pl.program_id(0) * new_count + row_step) & (row_step < new_count)
+    ).astype(jnp.bfloat16)
+    repeated = jnp.dot(spread, q_ref[...], preferred_element_type=jnp.float32)
     row_head = lax.broadcasted_iota(jnp.int32, (row_count, inner_width), 0) // step_rows
     col_head = lax.broadcasted_iota(jnp.int32, (row_count, inner_width), 1) // HEAD_DIM
     query_blocks = jnp.where(row_head == col_head, repeated, 0.0).astype(jnp.bfloat16)
@@ -63,16 +67,18 @@
 
 
 def piece_attention(query_rows, keys, values, trailing, prefix_rows, live_row, total_rows, seq_count):
-    req_count, step_rows, inner_width = query_rows.shape
+    query_count, inner_width = query_rows.shape
+    req_count = keys.shape[0]
     head_count = trailing.shape[1]
     piece_len = keys.shape[1]
-    row_count = head_count * step_rows
+    row_count = prefix_rows.shape[1]
+    step_rows = row_count // head_count
     own_heads = head_count // seq_count
     return pl.pallas_call(
         attention_kernel,
         grid=(req_count,),
         in_specs=[
-            pl.BlockSpec((1, step_rows, inner_width), lambda r: (r, 0, 0)),
+            pl.BlockSpec((query_count, inner_width), lambda r: (0, 0)),
             pl.BlockSpec((1, piece_len, inner_width), lambda r: (r, 0, 0)),
             pl.BlockSpec((1, piece_len, inner_width), lambda r: (r, 0, 0)),
             pl.BlockSpec((1, head_count, piece_len), lambda r: (r, 0, 0)),
@@ -141,9 +147,10 @@
     placement = (target[:, None] == jnp.arange(inner_width, dtype=jnp.int32)[None, :]).astype(
         jnp.bfloat16
     )
-    all_heads = jnp.einsum(
+    head_rows = jnp.einsum(
         "kx,kj->xj", incoming, placement, preferred_element_type=jnp.float32
-    ).astype(jnp.bfloat16).reshape(3, req_count, new_count, inner_width)
+    ).astype(jnp.bfloat16)
+    all_heads = head_rows.reshape(3, req_count, new_count, inner_width)
     gate_logit = (
         jnp.dot(normed, w_forget, preferred_element_type=jnp.float32).reshape(
             req_count, new_count, head_count
@@ -167,7 +174,6 @@
     )
     step_rows = 8
     pad_steps = ((0, 0), (0, step_rows - new_count))
-    query_rows = jnp.pad(all_heads[0], pad_steps + ((0, 0),))
     prefix_rows = jnp.pad(jnp.transpose(prefix, (0, 2, 1)), ((0, 0),) + pad_steps).reshape(
         req_count, head_count * step_rows, 1
     )
@@ -176,7 +182,7 @@
         piece_total[:, :, None], (req_count, head_count, step_rows)
     ).reshape(req_count, head_count * step_rows, 1)
     packed = piece_attention(
-        query_rows, cache_keys, cache_values, trailing_part, prefix_rows, live_row, total_rows, seq_count
+        head_rows, cache_keys, cache_values, trailing_part, prefix_rows, live_row, total_rows, seq_count
     )
     parts = lax.all_to_all(packed, "seq", 0, 0, tiled=True)[:, :, :, :new_count]
     part_acc = parts[..., :HEAD_DIM]

time: 78.5 us -> 79.2 us (level)
  Pallas kernels: 8.98 us -> 9.97 us
    pallas_call x1, Pallas kernels: 8.98 us -> 9.97 us  [piece_attention(): pl.pallas_call(attention_kernel, grid=(req_count,), in_specs=[pl.BlockSpe...]
where the time goes in v10:
time: 79.2 us; the launch traced here: 78.6 us
  waiting for transfers between devices  26.5 us (33%)
  starting transfers between devices  17.5 us (22%)
  local copies, waits for them, and re-layouts  10.9 us (14%)
  Pallas kernels  9.97 us (13%)
  other arithmetic  8.15 us (10%)
  matrix products  5.37 us (7%)
    pallas_call x1, Pallas kernels, piece_attention(): pl.pallas_call(attention_kernel, grid=(req_count,), in_specs=[pl.BlockSpe...  9.97 us
    all_to_all x1, waiting for transfers between devices, body(): incoming = lax.all_to_all(outgoing, ('fsdp', 'seq'), 0, 0, tiled=True)  9.91 us
    all_to_all x1, waiting for transfers between devices, body(): parts = lax.all_to_all(packed, 'seq', 0, 0, tiled=True)[:, :, :, :new_count]  9.44 us
    all_to_all x1, starting transfers between devices, body(): incoming = lax.all_to_all(outgoing, ('fsdp', 'seq'), 0, 0, tiled=True)  7.6 us
    all_to_all x1, waiting for transfers between devices, body(): lax.all_to_all(jnp.broadcast_to(normed[None], (fsdp_count, rows, width)),...  7.13 us
    all_to_all x1, starting transfers between devices, body(): lax.all_to_all(jnp.broadcast_to(normed[None], (fsdp_count, rows, width)),...  6.43 us
    all_to_all x1, starting transfers between devices, body(): parts = lax.all_to_all(packed, 'seq', 0, 0, tiled=True)[:, :, :, :new_count]  3.45 us
    dot_general x1, matrix products, body(): jnp.einsum('rhl,lj->rhj', masked, later_step, precision=lax.Precision.HIG...  1.97 us
  transfers between devices with their start and end apart: 3, of which 3 were waited for; matrix products, arithmetic and copies ran while one was open for 15% of the time, Pallas kernels for 0%

profile of v10, /device:TPU:0, one launch (start us, length us, event | category | flops | bytes accessed | tf_op | source)
XLA Modules:
  0.0 78.6 jit_solution(4863298802453211208)
XLA Ops:
  0.0 0.0 copy-start
  0.0 1.0 %fusion.10 = f32[4,5]{0,1:T(8,128)S(1)} fusion(bf16[4,5,1536]{2,0,1:T(4,128)(2,1)} %param.11), kind=kLoop, calls=%fused_computation.19 | loop fusion | flops 92140 | bytes 61520 | tf_op jit(solution)/shard_map/reduce_sum | solution.py:17
  1.0 0.9 %fusion.12 = bf16[4,5,1536]{2,0,1:T(4,128)(2,1)S(1)} fusion(bf16[4,5,1536]{2,0,1:T(4,128)(2,1)} %param.11, f32[1536]{0:T(1024)} %param.12, f32[4,5]{0,1:T(8,128)S(1)} %add_rsqrt_fusion), kind=kLoop, calls=%fused_computation.21 | loop fusion | flops 122880 | bytes 129104 | tf_op jit(solution)/shard_map/convert_element_type | solution.py:18
  2.0 1.1 %broadcast_in_dim.145 = bf16[16,20,1536]{2,1,0:T(8,128)(2,1)} broadcast(bf16[20,1536]{1,0:T(8,128)(2,1)S(1)} %broadcast_in_dim.144), dimensions={1,2} | broadcast | bytes 1044480 | tf_op jit(solution)/shard_map/broadcast_in_dim | solution.py:122
  3.1 6.4 %all-to-all-start = ((bf16[16,20,1536]{2,1,0:T(8,128)(2,1)}), bf16[16,20,1536]{2,1,0:T(8,128)(2,1)S(1)}, u32[]{:S(2)}, u32[]{:S(2)}) async-start(bf16[16,20,1536]{2,1,0:T(8,128)(2,1)} %broadcast_in_dim.145), calls=%async_computation | async-start | bytes 2359296 | tf_op jit(solution)/shard_map/all_to_all | solution.py:121
  9.5 0.8 %select_reduce_fusion.4 = s32[4]{0:T(128)S(1)} fusion(s32[4,8]{1,0:T(4,128)} %param.20, s32[]{:T(128)S(6)} %axis_index.12), kind=kLoop, calls=%fused_computation.106 | loop fusion | flops 92 | bytes 148 | tf_op jit(solution)/shard_map/reduce_sum | solution.py:164
  10.3 0.0 copy-done
  10.3 0.8 %fusion.59 = (u8[4,24]{1,0:T(4,128)(4,1)S(1)}, f32[4,5,24]{2,0,1:T(4,128)S(1)}) fusion(f32[24]{0:T(128)} %param.15, bf16[4,5,1536]{2,0,1:T(4,128)(2,1)S(1)} %fusion.12, bf16[1536,24]{0,1:T(8,128)(2,1)S(1)} %copy-done), kind=kOutput, calls=%fused_computation.105 | convolution fusion | flops 1477824 | bytes 137280 | tf_op jit(solution)/shard_map/dot_general | solution.py:155
  11.2 0.7 add_compare_fusion
  11.9 1.0 %select_reduce_fusion = f32[4,24]{1,0:T(4,128)S(1)} fusion(f32[4,24,512]{2,1,0:T(8,128)} %param.18, pred[4,512]{1,0:T(4,128)(4,1)S(1)} %add_compare_fusion), kind=kLoop, calls=%fused_computation.15 | loop fusion | flops 98208 | bytes 199040 | tf_op jit(solution)/shard_map/reduce_sum | solution.py:169
  13.0 0.1 dynamic-slice_bitcast_fusion
  13.1 0.1 copy.211
  13.2 0.1 copy.210
  13.3 0.9 %reshape.261 = bf16[1536,36]{0,1:T(8,128)(2,1)S(1)} reshape(bf16[1536,3,3,4]{0,3,2,1:T(4,128)(2,1)} %param.13) | data formatting | bytes 221184 | tf_op jit(solution)/shard_map/reshape | solution.py:126
  14.2 0.1 copy.235
  14.4 0.9 %reshape.270.prefix_ref = f32[4,192,1]{2,1,0:T(8,128)} reshape(f32[4,24,8]{2,1,0:T(8,128)S(1)} %pad.4.clone) | data formatting | bytes 6144 | tf_op jit(solution)/shard_map/reshape | solution.py:177
  15.3 0.1 broadcast_in_dim.152
  15.4 0.9 %reshape.271.total_ref = f32[4,192,1]{2,1,0:T(8,128)} reshape(f32[4,24,8]{2,1,0:T(8,128)S(1)} %broadcast_in_dim.152) | data formatting | bytes 6144 | tf_op jit(solution)/shard_map/reshape | solution.py:183
  16.3 0.8 select_reduce_fusion.3
  17.1 0.1 broadcast_compare_fusion
  17.1 1.3 %compare_convert_fusion.live_ref = f32[4,1,512]{2,1,0:T(1,128)} fusion(s32[4]{0:T(128)} %param.19, s32[4]{0:T(128)S(1)} %broadcast_multiply_fusion), kind=kLoop, calls=%fused_computation.26 | loop fusion | flops 6144 | bytes 8224 | tf_op jit(solution)/shard_map/convert_element_type | solution.py:180
  18.5 2.0 %fusion.6.trail_ref = f32[4,24,512]{2,1,0:T(8,128)} fusion(f32[4,24,512]{2,1,0:T(8,128)} %param.18, pred[4,512]{1,0:T(4,128)(4,1)S(1)} %add_compare_fusion), kind=kOutput, calls=%fused_computation.10 | convolution fusion | flops 302301184 | bytes 395264 | tf_op jit(solution)/shard_map/rhl,lj->rhj/dot_general | solution.py:171
  20.4 7.1 %all-to-all-done = bf16[16,20,1536]{2,1,0:T(8,128)(2,1)S(1)} async-done(((bf16[16,20,1536]{2,1,0:T(8,128)(2,1)}), bf16[16,20,1536]{2,1,0:T(8,128)(2,1)S(1)}, u32[]{:S(2)}, u32[]{:S(2)}) %all-to-all-start) | async-done | bytes 983072 | tf_op jit(solution)/shard_map/all_to_all | solution.py:121
  27.6 0.2 reshape.260
  27.8 0.4 fusion.3
  28.2 0.2 reshape.262
  28.5 0.1 copy.251
  28.6 0.2 broadcast_in_dim.146
  28.8 0.9 %reshape.263 = bf16[128,2,360]{2,1,0:T(2,128)(2,1)} reshape(bf16[16,8,720]{2,1,0:T(8,128)(2,1)S(1)} %broadcast_in_dim.147) | data formatting | bytes 368640 | tf_op jit(solution)/shard_map/reshape | solution.py:137
  29.7 7.6 %all-to-all-start.1 = ((bf16[128,2,360]{2,1,0:T(2,128)(2,1)}), bf16[128,2,360]{2,1,0:T(2,128)(2,1)S(1)}, u32[]{:S(2)}, u32[]{:S(2)}) async-start(bf16[128,2,360]{2,1,0:T(2,128)(2,1)} %reshape.263), calls=%async_computation.1 | async-start | bytes 393216 | tf_op jit(solution)/shard_map/all_to_all | solution.py:138
  37.3 0.0 copy-done.2
  37.3 9.9 %all-to-all-done.1 = bf16[128,2,360]{2,1,0:T(2,128)(2,1)S(1)} async-done(((bf16[128,2,360]{2,1,0:T(2,128)(2,1)}), bf16[128,2,360]{2,1,0:T(2,128)(2,1)S(1)}, u32[]{:S(2)}, u32[]{:S(2)}) %all-to-all-start.1) | async-done | bytes 184352 | tf_op jit(solution)/shard_map/all_to_all | solution.py:138
  47.2 0.6 reshape.264
  47.8 1.9 %fusion.2.q_ref = bf16[60,1536]{1,0:T(8,128)(2,1)S(1)} fusion(bf16[1536,60]{1,0:T(8,128)(2,1)S(1)} %reshape.264, s32[1536]{0:T(1024)S(1)} %fusion.45), kind=kOutput, calls=%fused_computation.3 | convolution fusion | flops 285566976 | bytes 374784 | tf_op jit(solution)/shard_map/kx,kj->xj/dot_general | solution.py:150
  49.8 0.0 copy-start.1
  49.8 0.1 reshape.267
  49.8 0.1 constant_dynamic-slice_fusion
  50.0 0.1 reshape.274
  50.0 0.4 copy-done.1
  50.4 10.0 %shard_map.109 = f32[8,4,3,8,128]{4,3,2,1,0:T(8,128)} custom-call(bf16[60,1536]{1,0:T(8,128)(2,1)} %copy-done.1, bf16[4,512,1536]{2,1,0:T(8,128)(2,1)} %k_ref.1, bf16[4,512,1536]{2,1,0:T(8,128)(2,1)} %v_ref.1, f32[4,24,512]{2,1,0:T(8,128)} %fusion.6.trail_ref, f32[4,192,1]{2,1,0:T(8,128)} %reshape.270.prefix_ref, f32[4,1,512]{2,1,0:T(1,128)} %compare_convert_fusion.live_ref, ...), custom_call_target="tpu_custom_call" | custom-call | tf_op jit(solution)/shard_map/pallas_call | solution.py:77
  60.4 3.5 %all-to-all-start.2 = ((f32[8,4,3,8,128]{4,3,2,1,0:T(8,128)}), f32[8,4,3,8,128]{4,3,2,1,0:T(8,128)S(1)}, u32[]{:S(2)}, u32[]{:S(2)}) async-start(f32[8,4,3,8,128]{4,3,2,1,0:T(8,128)} %shard_map.109), calls=%async_computation.2 | async-start | bytes 786432 | tf_op jit(solution)/shard_map/all_to_all | solution.py:187
  63.9 0.1 reshape.273
  63.9 0.1 reshape.272
  64.0 0.1 fusion.21
  64.2 0.2 copy.209
  64.3 0.2 select_reduce_fusion.2
  64.5 9.4 %all-to-all-done.2 = f32[8,4,3,8,128]{4,3,2,1,0:T(8,128)S(1)} async-done(((f32[8,4,3,8,128]{4,3,2,1,0:T(8,128)}), f32[8,4,3,8,128]{4,3,2,1,0:T(8,128)S(1)}, u32[]{:S(2)}, u32[]{:S(2)}) %all-to-all-start.2) | async-done | bytes 393248 | tf_op jit(solution)/shard_map/all_to_all | solution.py:187
  73.9 0.2 slice.38
  74.1 0.2 copy.225
  74.3 0.1 select_reduce_fusion.1
  74.4 0.1 copy.198
  74.5 0.2 slice.37
  74.7 0.5 copy.199
  75.1 0.1 fusion.18
  75.2 0.1 copy.201
  75.4 0.2 fusion.62
  75.6 0.4 fusion.65
  75.9 0.9 %copy.226 = f32[8,4,3,5,1]{3,2,1,0,4:T(4,128)S(1)} copy(f32[8,4,3,5,1]{4,3,2,1,0:T(8,128)S(1)} %get-tuple-element.8) | data formatting | bytes 3840 | tf_op jit(solution)/shard_map/mul | solution.py:198
  76.8 0.5 copy.220
  77.3 0.2 fusion.16
  77.5 0.1 fusion.19
  77.6 0.2 fusion.8
  77.8 0.1 select_convert_fusion
  78.0 0.7 convert_element_type.46
  (18 shorter events, 0.2 us)
Async XLA Ops:
  0.0 10.3 %copy-start = (bf16[1536,24]{0,1:T(8,128)(2,1)S(1)}, bf16[1536,24]{0,1:T(8,128)(2,1)}, u32[]{:S(2)}) copy-start(bf16[1536,24]{0,1:T(8,128)(2,1)} %param.14) | copy-start | bytes 221188
  0.0 37.3 %copy-start.2 = (s32[4]{0:T(128)S(1)}, s32[4]{0:T(128)}, u32[]{:S(2)}) copy-start(s32[4]{0:T(128)} %param.21) | copy-start | bytes 52
  3.1 24.5 %all-to-all-start = ((bf16[16,20,1536]{2,1,0:T(8,128)(2,1)}), bf16[16,20,1536]{2,1,0:T(8,128)(2,1)S(1)}, u32[]{:S(2)}, u32[]{:S(2)}) async-start(bf16[16,20,1536]{2,1,0:T(8,128)(2,1)} %broadcast_in_dim.145), calls=%async_computation | async-start | bytes 2359296 | tf_op jit(solution)/shard_map/all_to_all | solution.py:121
  29.7 17.5 %all-to-all-start.1 = ((bf16[128,2,360]{2,1,0:T(2,128)(2,1)}), bf16[128,2,360]{2,1,0:T(2,128)(2,1)S(1)}, u32[]{:S(2)}, u32[]{:S(2)}) async-start(bf16[128,2,360]{2,1,0:T(2,128)(2,1)} %reshape.263), calls=%async_computation.1 | async-start | bytes 393216 | tf_op jit(solution)/shard_map/all_to_all | solution.py:138
  49.8 0.7 copy-start.1
  60.4 13.6 %all-to-all-start.2 = ((f32[8,4,3,8,128]{4,3,2,1,0:T(8,128)}), f32[8,4,3,8,128]{4,3,2,1,0:T(8,128)S(1)}, u32[]{:S(2)}, u32[]{:S(2)}) async-start(f32[8,4,3,8,128]{4,3,2,1,0:T(8,128)} %shard_map.109), calls=%async_computation.2 | async-start | bytes 786432 | tf_op jit(solution)/shard_map/all_to_all | solution.py:187

commit v11 on v6

--- a/solution.py
+++ b/solution.py
@@ -129,6 +129,7 @@
     outgoing = jnp.broadcast_to(
         outgoing, (fsdp_count, seq_count, own_heads * own_dims * 3 * rows)
     ).reshape(fsdp_count * seq_count, 2, own_heads * own_dims * 3 * rows // 2)
+    outgoing, cache_forget, normed = lax.optimization_barrier((outgoing, cache_forget, normed))
     incoming = lax.all_to_all(outgoing, ("fsdp", "seq"), 0, 0, tiled=True)
     incoming = incoming.reshape(fsdp_count * seq_count * own_heads * own_dims, 3 * rows)
     src_row = jnp.arange(fsdp_count * seq_count * own_heads * own_dims, dtype=jnp.int32)

time: 78.5 us -> 79.9 us (1.018)
  waiting for transfers between devices: 26.5 us -> 29.8 us
  matrix products: 5.37 us -> 3.76 us
    all_to_all x1, waiting for transfers between devices: 7.13 us -> 12.7 us  [body(): lax.all_to_all(jnp.broadcast_to(normed[None], (fsdp_count, rows, width)),...]
    all_to_all x1, waiting for transfers between devices: 9.91 us -> 7.86 us  [body(): incoming = lax.all_to_all(outgoing, ('fsdp', 'seq'), 0, 0, tiled=True)]
    reduce_sum x1, other arithmetic: 1.03 us -> 0.1 us  [body(): piece_total = jnp.sum(masked, axis=-1)]
    dot_general x1, matrix products: 1.97 us -> 1.06 us  [body(): jnp.einsum('rhl,lj->rhj', masked, later_step, precision=lax.Precision.HIG...]
  transfers between devices with their start and end apart: 3 -> 3, of which waited for: 3 -> 3; matrix products, arithmetic and copies ran while one was open for 15% -> 10% of each run, Pallas kernels for 0% -> 0%
where the time goes in v11:
time: 79.9 us; the launch traced here: 79.5 us
  waiting for transfers between devices  29.8 us (37%)
  starting transfers between devices  17.5 us (22%)
  local copies, waits for them, and re-layouts  11.2 us (14%)
  Pallas kernels  8.97 us (11%)
  other arithmetic  7.91 us (10%)
  matrix products  3.76 us (5%)
    all_to_all x1, waiting for transfers between devices, body(): lax.all_to_all(jnp.broadcast_to(normed[None], (fsdp_count, rows, width)),...  12.7 us
    all_to_all x1, waiting for transfers between devices, body(): parts = lax.all_to_all(packed, 'seq', 0, 0, tiled=True)[:, :, :, :new_count]  9.24 us
    pallas_call x1, Pallas kernels, piece_attention(): pl.pallas_call(attention_kernel, grid=(req_count,), in_specs=[pl.BlockSpe...  8.97 us
    all_to_all x1, waiting for transfers between devices, body(): incoming = lax.all_to_all(outgoing, ('fsdp', 'seq'), 0, 0, tiled=True)  7.86 us
    all_to_all x1, starting transfers between devices, body(): incoming = lax.all_to_all(outgoing, ('fsdp', 'seq'), 0, 0, tiled=True)  7.6 us
    all_to_all x1, starting transfers between devices, body(): lax.all_to_all(jnp.broadcast_to(normed[None], (fsdp_count, rows, width)),...  6.43 us
    all_to_all x1, starting transfers between devices, body(): parts = lax.all_to_all(packed, 'seq', 0, 0, tiled=True)[:, :, :, :new_count]  3.45 us
    dot_general x1, matrix products, body(): jnp.einsum('kx,kj->xj', incoming, placement, preferred_element_type=jnp.f...  1.93 us
  transfers between devices with their start and end apart: 3, of which 3 were waited for; matrix products, arithmetic and copies ran while one was open for 10% of the time, Pallas kernels for 0%

profile of v11, /device:TPU:0, one launch (start us, length us, event | category | flops | bytes accessed | tf_op | source)
XLA Modules:
  0.0 79.5 jit_solution(3905062734136196883)
XLA Ops:
  0.0 0.0 copy-start
  0.0 1.0 %fusion.9 = f32[4,5]{0,1:T(8,128)S(1)} fusion(bf16[4,5,1536]{2,0,1:T(4,128)(2,1)} %param.11), kind=kLoop, calls=%fused_computation.17 | loop fusion | flops 92140 | bytes 61520 | tf_op jit(solution)/shard_map/reduce_sum | solution.py:17
  1.0 0.9 %fusion.11 = bf16[4,5,1536]{2,0,1:T(4,128)(2,1)S(1)} fusion(bf16[4,5,1536]{2,0,1:T(4,128)(2,1)} %param.11, f32[1536]{0:T(1024)} %param.12, f32[4,5]{0,1:T(8,128)S(1)} %add_rsqrt_fusion), kind=kLoop, calls=%fused_computation.19 | loop fusion | flops 122880 | bytes 129104 | tf_op jit(solution)/shard_map/convert_element_type | solution.py:18
  2.0 1.1 %broadcast_in_dim.145 = bf16[16,20,1536]{2,1,0:T(8,128)(2,1)} broadcast(bf16[20,1536]{1,0:T(8,128)(2,1)S(1)} %broadcast_in_dim.144), dimensions={1,2} | broadcast | bytes 1044480 | tf_op jit(solution)/shard_map/broadcast_in_dim | solution.py:116
  3.1 6.4 %all-to-all-start = ((bf16[16,20,1536]{2,1,0:T(8,128)(2,1)}), bf16[16,20,1536]{2,1,0:T(8,128)(2,1)S(1)}, u32[]{:S(2)}, u32[]{:S(2)}) async-start(bf16[16,20,1536]{2,1,0:T(8,128)(2,1)} %broadcast_in_dim.145), calls=%async_computation | async-start | bytes 2359296 | tf_op jit(solution)/shard_map/all_to_all | solution.py:115
  9.6 0.8 select_reduce_fusion.3
  10.3 0.8 %select_reduce_fusion.4 = s32[4]{0:T(128)S(1)} fusion(s32[4,8]{1,0:T(4,128)} %param.20, s32[]{:T(128)S(6)} %axis_index.12), kind=kLoop, calls=%fused_computation.92 | loop fusion | flops 92 | bytes 148 | tf_op jit(solution)/shard_map/reduce_sum | solution.py:158
  11.2 0.9 %reshape.263 = bf16[1536,36]{0,1:T(8,128)(2,1)S(1)} reshape(bf16[1536,3,3,4]{0,3,2,1:T(4,128)(2,1)} %param.13) | data formatting | bytes 221184 | tf_op jit(solution)/shard_map/reshape | solution.py:120
  12.1 0.7 iota_compare_fusion.7
  12.8 0.7 add_compare_fusion
  13.5 0.1 broadcast_compare_fusion
  13.6 1.3 %compare_convert_fusion.live_ref = f32[4,1,512]{2,1,0:T(1,128)} fusion(s32[4]{0:T(128)} %param.19, s32[4]{0:T(128)S(1)} %broadcast_multiply_fusion), kind=kLoop, calls=%fused_computation.24 | loop fusion | flops 6144 | bytes 8224 | tf_op jit(solution)/shard_map/convert_element_type | solution.py:175
  14.9 12.7 %all-to-all-done = bf16[16,20,1536]{2,1,0:T(8,128)(2,1)S(1)} async-done(((bf16[16,20,1536]{2,1,0:T(8,128)(2,1)}), bf16[16,20,1536]{2,1,0:T(8,128)(2,1)S(1)}, u32[]{:S(2)}, u32[]{:S(2)}) %all-to-all-start) | async-done | bytes 983072 | tf_op jit(solution)/shard_map/all_to_all | solution.py:115
  27.6 0.2 reshape.262
  27.8 0.4 fusion.3
  28.2 0.2 reshape.264
  28.5 0.1 copy.247
  28.6 0.2 broadcast_in_dim.146
  28.8 0.9 %reshape.265 = bf16[128,2,360]{2,1,0:T(2,128)(2,1)} reshape(bf16[16,8,720]{2,1,0:T(8,128)(2,1)S(1)} %broadcast_in_dim.147) | data formatting | bytes 368640 | tf_op jit(solution)/shard_map/reshape | solution.py:131
  29.7 0.1 fusion.53
  29.9 0.0 copy-done.2
  29.9 0.1 dynamic-slice_bitcast_fusion
  30.0 0.1 copy.206
  30.2 0.1 copy.207
  30.3 0.0 copy-done.1
  30.3 0.1 select_reduce_fusion
  30.4 0.1 broadcast_in_dim.152
  30.4 0.9 %reshape.273.total_ref = f32[4,192,1]{2,1,0:T(8,128)} reshape(f32[4,24,8]{2,1,0:T(8,128)S(1)} %broadcast_in_dim.152) | data formatting | bytes 6144 | tf_op jit(solution)/shard_map/reshape | solution.py:178
  31.4 7.6 %all-to-all-start.1 = ((bf16[128,2,360]{2,1,0:T(2,128)(2,1)}), bf16[128,2,360]{2,1,0:T(2,128)(2,1)S(1)}, u32[]{:S(2)}, u32[]{:S(2)}) async-start(bf16[128,2,360]{2,1,0:T(2,128)(2,1)} %reshape.265), calls=%async_computation.1 | async-start | bytes 393216 | tf_op jit(solution)/shard_map/all_to_all | solution.py:133
  39.0 0.1 copy.231
  39.1 0.9 %reshape.272.prefix_ref = f32[4,192,1]{2,1,0:T(8,128)} reshape(f32[4,24,8]{2,1,0:T(8,128)S(1)} %pad.9.clone) | data formatting | bytes 6144 | tf_op jit(solution)/shard_map/reshape | solution.py:172
  40.0 1.1 %fusion.5.trail_ref = f32[4,24,512]{2,1,0:T(8,128)} fusion(f32[4,24,512]{2,1,0:T(8,128)S(1)} %copy-done.1, pred[4,512]{1,0:T(4,128)(4,1)S(1)} %add_compare_fusion), kind=kOutput, calls=%fused_computation.8 | convolution fusion | flops 302301184 | bytes 395264 | tf_op jit(solution)/shard_map/rhl,lj->rhj/dot_general | solution.py:165
  41.1 7.9 %all-to-all-done.1 = bf16[128,2,360]{2,1,0:T(2,128)(2,1)S(1)} async-done(((bf16[128,2,360]{2,1,0:T(2,128)(2,1)}), bf16[128,2,360]{2,1,0:T(2,128)(2,1)S(1)}, u32[]{:S(2)}, u32[]{:S(2)}) %all-to-all-start.1) | async-done | bytes 184352 | tf_op jit(solution)/shard_map/all_to_all | solution.py:133
  48.9 0.6 reshape.266
  49.5 1.9 %fusion.2 = bf16[60,1536]{1,0:T(8,128)(2,1)S(1)} fusion(bf16[1536,60]{1,0:T(8,128)(2,1)S(1)} %reshape.266, s32[1536]{0:T(1024)S(1)} %fusion.35), kind=kOutput, calls=%fused_computation.3 | convolution fusion | flops 285566976 | bytes 374784 | tf_op jit(solution)/shard_map/kx,kj->xj/dot_general | solution.py:145
  51.4 0.1 reshape.270
  51.6 0.7 pad.8.q_ref
  52.2 9.0 %shard_map.109 = f32[8,4,3,8,128]{4,3,2,1,0:T(8,128)} custom-call(bf16[4,8,1536]{2,1,0:T(8,128)(2,1)} %pad.8.q_ref, bf16[4,512,1536]{2,1,0:T(8,128)(2,1)} %k_ref.1, bf16[4,512,1536]{2,1,0:T(8,128)(2,1)} %v_ref.1, f32[4,24,512]{2,1,0:T(8,128)} %fusion.5.trail_ref, f32[4,192,1]{2,1,0:T(8,128)} %reshape.272.prefix_ref, ...), custom_call_target="tpu_custom_call" | custom-call | tf_op jit(solution)/shard_map/pallas_call | solution.py:71
  61.2 3.5 %all-to-all-start.2 = ((f32[8,4,3,8,128]{4,3,2,1,0:T(8,128)}), f32[8,4,3,8,128]{4,3,2,1,0:T(8,128)S(1)}, u32[]{:S(2)}, u32[]{:S(2)}) async-start(f32[8,4,3,8,128]{4,3,2,1,0:T(8,128)} %shard_map.109), calls=%async_computation.2 | async-start | bytes 786432 | tf_op jit(solution)/shard_map/all_to_all | solution.py:182
  64.7 0.1 constant_dynamic-slice_fusion
  64.8 0.1 reshape.274
  64.9 0.1 reshape.275
  65.0 0.1 fusion.19
  65.1 0.2 copy.205
  65.2 0.1 reshape.276
  65.3 0.2 select_reduce_fusion.2
  65.5 9.2 %all-to-all-done.2 = f32[8,4,3,8,128]{4,3,2,1,0:T(8,128)S(1)} async-done(((f32[8,4,3,8,128]{4,3,2,1,0:T(8,128)}), f32[8,4,3,8,128]{4,3,2,1,0:T(8,128)S(1)}, u32[]{:S(2)}, u32[]{:S(2)}) %all-to-all-start.2) | async-done | bytes 393248 | tf_op jit(solution)/shard_map/all_to_all | solution.py:182
  74.8 0.2 slice.44
  74.9 0.2 copy.221
  75.1 0.1 select_reduce_fusion.1
  75.2 0.1 copy.194
  75.3 0.2 slice.43
  75.5 0.5 copy.195
  76.0 0.1 fusion.16
  76.0 0.1 copy.197
  76.2 0.4 fusion.52
  76.6 0.5 copy.216
  77.0 0.2 fusion.14
  77.2 0.2 fusion.49
  77.5 0.9 %copy.222 = f32[8,4,3,5,1]{3,2,1,0,4:T(4,128)S(1)} copy(f32[8,4,3,5,1]{4,3,2,1,0:T(8,128)S(1)} %get-tuple-element.14) | data formatting | bytes 3840 | tf_op jit(solution)/shard_map/mul | solution.py:193
  78.3 0.1 fusion.17
  78.5 0.2 fusion.7
  78.6 0.1 select_convert_fusion
  78.8 0.7 convert_element_type.48
  (22 shorter events, 0.3 us)
Async XLA Ops:
  0.0 29.7 %copy-start = (bf16[1536,24]{0,1:T(8,128)(2,1)S(1)}, bf16[1536,24]{0,1:T(8,128)(2,1)}, u32[]{:S(2)}) copy-start(bf16[1536,24]{0,1:T(8,128)(2,1)} %param.14) | copy-start | bytes 221188
  0.0 30.3 %copy-start.1 = (f32[4,24,512]{2,1,0:T(8,128)S(1)}, f32[4,24,512]{2,1,0:T(8,128)}, u32[]{:S(2)}) copy-start(f32[4,24,512]{2,1,0:T(8,128)} %param.18) | copy-start | bytes 589828
  0.0 29.9 %copy-start.2 = (f32[24]{0:T(128)S(1)}, f32[24]{0:T(128)}, u32[]{:S(2)}) copy-start(f32[24]{0:T(128)} %param.15) | copy-start | bytes 292
  3.1 24.5 %all-to-all-start = ((bf16[16,20,1536]{2,1,0:T(8,128)(2,1)}), bf16[16,20,1536]{2,1,0:T(8,128)(2,1)S(1)}, u32[]{:S(2)}, u32[]{:S(2)}) async-start(bf16[16,20,1536]{2,1,0:T(8,128)(2,1)} %broadcast_in_dim.145), calls=%async_computation | async-start | bytes 2359296 | tf_op jit(solution)/shard_map/all_to_all | solution.py:115
  31.4 17.5 %all-to-all-start.1 = ((bf16[128,2,360]{2,1,0:T(2,128)(2,1)}), bf16[128,2,360]{2,1,0:T(2,128)(2,1)S(1)}, u32[]{:S(2)}, u32[]{:S(2)}) async-start(bf16[128,2,360]{2,1,0:T(2,128)(2,1)} %reshape.265), calls=%async_computation.1 | async-start | bytes 393216 | tf_op jit(solution)/shard_map/all_to_all | solution.py:133
  61.2 13.6 %all-to-all-start.2 = ((f32[8,4,3,8,128]{4,3,2,1,0:T(8,128)}), f32[8,4,3,8,128]{4,3,2,1,0:T(8,128)S(1)}, u32[]{:S(2)}, u32[]{:S(2)}) async-start(f32[8,4,3,8,128]{4,3,2,1,0:T(8,128)} %shard_map.109), calls=%async_computation.2 | async-start | bytes 786432 | tf_op jit(solution)/shard_map/all_to_all | solution.py:182

commit v12 on v6

--- a/solution.py
+++ b/solution.py
@@ -111,10 +111,12 @@
     logit_scale = HEAD_DIM ** (-0.5)
     seq_index = lax.axis_index("seq")
     head_start = seq_index * own_heads
-    normed = normalize(hidden_in, norm_gain).reshape(rows, width)
-    normed_all = lax.all_to_all(
-        jnp.broadcast_to(normed[None], (fsdp_count, rows, width)), "fsdp", 0, 0, tiled=True
-    ).reshape(fsdp_count * rows, width)
+    hidden_rows = hidden_in.reshape(rows, width)
+    hidden_all = lax.all_to_all(
+        jnp.broadcast_to(hidden_rows[None], (fsdp_count, rows, width)), "fsdp", 0, 0, tiled=True
+    )
+    normed_all = normalize(hidden_all, norm_gain).reshape(fsdp_count * rows, width)
+    normed = normalize(hidden_rows, norm_gain)
     projected = jnp.einsum(
         "dk,nd->kn",
         w_qkv.reshape(width, own_cols),

time: 78.5 us -> 78 us (level)
  waiting for transfers between devices: 26.5 us -> 32.3 us
  other arithmetic: 8.15 us -> 3.43 us
  matrix products: 5.37 us -> 3.87 us
    all_to_all x1, waiting for transfers between devices: 7.13 us -> 12.9 us  [body(): lax.all_to_all(jnp.broadcast_to(hidden_rows[None], (fsdp_count, rows, wid...]
    reduce_sum x1, other arithmetic: 1.03 us -> 0.1 us  [body(): piece_total = jnp.sum(masked, axis=-1)]
    unnamed x5 -> x20, local copies, waits for them, and re-layouts: 0.11 us -> 1.04 us
    dot_general x1, matrix products: 1.97 us -> 1.05 us  [body(): jnp.einsum('rhl,lj->rhj', masked, later_step, precision=lax.Precision.HIG...]
    reshape x1, local copies, waits for them, and re-layouts: 0.93 us -> 0.03 us  [body(): w_qkv.reshape(width, own_cols)]
  transfers between devices with their start and end apart: 3 -> 3, of which waited for: 3 -> 3; matrix products, arithmetic and copies ran while one was open for 15% -> 7% of each run, Pallas kernels for 0% -> 0%
where the time goes in v12:
time: 78 us; the launch traced here: 77.7 us
  waiting for transfers between devices  32.3 us (41%)
  starting transfers between devices  17.5 us (22%)
  local copies, waits for them, and re-layouts  11.2 us (14%)
  Pallas kernels  8.98 us (12%)
  matrix products  3.87 us (5%)
  other arithmetic  3.43 us (4%)
    all_to_all x1, waiting for transfers between devices, body(): lax.all_to_all(jnp.broadcast_to(hidden_rows[None], (fsdp_count, rows, wid...  12.9 us
    all_to_all x1, waiting for transfers between devices, body(): incoming = lax.all_to_all(outgoing, ('fsdp', 'seq'), 0, 0, tiled=True)  9.91 us
    all_to_all x1, waiting for transfers between devices, body(): parts = lax.all_to_all(packed, 'seq', 0, 0, tiled=True)[:, :, :, :new_count]  9.45 us
    pallas_call x1, Pallas kernels, piece_attention(): pl.pallas_call(attention_kernel, grid=(req_count,), in_specs=[pl.BlockSpe...  8.98 us
    all_to_all x1, starting transfers between devices, body(): incoming = lax.all_to_all(outgoing, ('fsdp', 'seq'), 0, 0, tiled=True)  7.6 us
    all_to_all x1, starting transfers between devices, body(): lax.all_to_all(jnp.broadcast_to(hidden_rows[None], (fsdp_count, rows, wid...  6.44 us
    all_to_all x1, starting transfers between devices, body(): parts = lax.all_to_all(packed, 'seq', 0, 0, tiled=True)[:, :, :, :new_count]  3.45 us
    dot_general x1, matrix products, body(): jnp.einsum('kx,kj->xj', incoming, placement, preferred_element_type=jnp.f...  1.93 us
  transfers between devices with their start and end apart: 3, of which 3 were waited for; matrix products, arithmetic and copies ran while one was open for 7% of the time, Pallas kernels for 0%

profile of v12, /device:TPU:0, one launch (start us, length us, event | category | flops | bytes accessed | tf_op | source)
XLA Modules:
  0.0 77.7 jit_solution(4121680012094103376)
XLA Ops:
  0.1 0.9 %copy.191 = bf16[4,5,1536]{2,1,0:T(8,128)(2,1)S(1)} copy(bf16[4,5,1536]{2,0,1:T(4,128)(2,1)} %param.11) | data formatting | bytes 122880 | tf_op args[0]
  1.0 1.1 %broadcast_in_dim.147 = bf16[16,20,1536]{2,1,0:T(8,128)(2,1)} broadcast(bf16[20,1536]{1,0:T(8,128)(2,1)S(1)} %broadcast_in_dim.146), dimensions={1,2} | broadcast | bytes 1044480 | tf_op jit(solution)/shard_map/broadcast_in_dim | solution.py:116
  2.1 6.4 %all-to-all-start = ((bf16[16,20,1536]{2,1,0:T(8,128)(2,1)}), bf16[16,20,1536]{2,1,0:T(8,128)(2,1)S(1)}, u32[]{:S(2)}, u32[]{:S(2)}) async-start(bf16[16,20,1536]{2,1,0:T(8,128)(2,1)} %broadcast_in_dim.147), calls=%async_computation | async-start | bytes 2359296 | tf_op jit(solution)/shard_map/all_to_all | solution.py:115
  8.5 0.0 copy-done.1
  8.5 0.1 fusion.13
  8.6 0.0 copy-done.5
  8.7 0.1 select_reduce_fusion.4
  8.8 0.3 fusion.65
  9.1 0.1 add_compare_fusion
  9.2 0.1 select_reduce_fusion
  9.3 0.1 dynamic-slice_bitcast_fusion
  9.4 0.1 copy.211
  9.5 0.1 copy.210
  9.7 0.1 copy.235
  9.8 0.9 %reshape.293.prefix_ref = f32[4,192,1]{2,1,0:T(8,128)} reshape(f32[4,24,8]{2,1,0:T(8,128)S(1)} %pad.9.clone) | data formatting | bytes 6144 | tf_op jit(solution)/shard_map/reshape | solution.py:173
  10.7 0.1 broadcast_in_dim.154
  10.8 0.9 %reshape.294.total_ref = f32[4,192,1]{2,1,0:T(8,128)} reshape(f32[4,24,8]{2,1,0:T(8,128)S(1)} %broadcast_in_dim.154) | data formatting | bytes 6144 | tf_op jit(solution)/shard_map/reshape | solution.py:179
  11.7 0.1 select_reduce_fusion.3
  11.8 0.1 broadcast_compare_fusion
  11.9 0.7 compare_convert_fusion.live_ref
  12.6 1.1 %fusion.9.trail_ref = f32[4,24,512]{2,1,0:T(8,128)} fusion(f32[4,24,512]{2,1,0:T(8,128)S(1)} %copy-done.2, pred[4,512]{1,0:T(4,128)(4,1)S(1)} %add_compare_fusion), kind=kOutput, calls=%fused_computation.15 | convolution fusion | flops 302301184 | bytes 395264 | tf_op jit(solution)/shard_map/rhl,lj->rhj/dot_general | solution.py:166
  13.6 12.9 %all-to-all-done = bf16[16,20,1536]{2,1,0:T(8,128)(2,1)S(1)} async-done(((bf16[16,20,1536]{2,1,0:T(8,128)(2,1)}), bf16[16,20,1536]{2,1,0:T(8,128)(2,1)S(1)}, u32[]{:S(2)}, u32[]{:S(2)}) %all-to-all-start) | async-done | bytes 983072 | tf_op jit(solution)/shard_map/all_to_all | solution.py:115
  26.6 0.3 fusion.2
  26.9 0.3 fusion.4
  27.3 0.0 copy-start.8
  27.3 0.3 reshape.283
  27.5 0.4 fusion.6
  27.9 0.2 reshape.285
  28.2 0.1 copy.251
  28.3 0.2 broadcast_in_dim.148
  28.5 0.9 %reshape.286 = bf16[128,2,360]{2,1,0:T(2,128)(2,1)} reshape(bf16[16,8,720]{2,1,0:T(8,128)(2,1)S(1)} %broadcast_in_dim.149) | data formatting | bytes 368640 | tf_op jit(solution)/shard_map/reshape | solution.py:133
  29.4 7.6 %all-to-all-start.1 = ((bf16[128,2,360]{2,1,0:T(2,128)(2,1)}), bf16[128,2,360]{2,1,0:T(2,128)(2,1)S(1)}, u32[]{:S(2)}, u32[]{:S(2)}) async-start(bf16[128,2,360]{2,1,0:T(2,128)(2,1)} %reshape.286), calls=%async_computation.1 | async-start | bytes 393216 | tf_op jit(solution)/shard_map/all_to_all | solution.py:134
  37.1 9.9 %all-to-all-done.1 = bf16[128,2,360]{2,1,0:T(2,128)(2,1)S(1)} async-done(((bf16[128,2,360]{2,1,0:T(2,128)(2,1)}), bf16[128,2,360]{2,1,0:T(2,128)(2,1)S(1)}, u32[]{:S(2)}, u32[]{:S(2)}) %all-to-all-start.1) | async-done | bytes 184352 | tf_op jit(solution)/shard_map/all_to_all | solution.py:134
  47.0 0.6 reshape.287
  47.5 1.9 %fusion.5 = bf16[60,1536]{1,0:T(8,128)(2,1)S(1)} fusion(bf16[1536,60]{1,0:T(8,128)(2,1)S(1)} %reshape.287, s32[1536]{0:T(1024)S(1)} %fusion.51), kind=kOutput, calls=%fused_computation.8 | convolution fusion | flops 285566976 | bytes 374784 | tf_op jit(solution)/shard_map/kx,kj->xj/dot_general | solution.py:146
  49.5 0.1 reshape.290
  49.6 0.1 constant_dynamic-slice_fusion
  49.7 0.1 reshape.297
  49.8 0.7 pad.8.q_ref
  50.5 9.0 %shard_map.109 = f32[8,4,3,8,128]{4,3,2,1,0:T(8,128)} custom-call(bf16[4,8,1536]{2,1,0:T(8,128)(2,1)} %pad.8.q_ref, bf16[4,512,1536]{2,1,0:T(8,128)(2,1)} %k_ref.1, bf16[4,512,1536]{2,1,0:T(8,128)(2,1)} %v_ref.1, f32[4,24,512]{2,1,0:T(8,128)} %fusion.9.trail_ref, f32[4,192,1]{2,1,0:T(8,128)} %reshape.293.prefix_ref, ...), custom_call_target="tpu_custom_call" | custom-call | tf_op jit(solution)/shard_map/pallas_call | solution.py:71
  59.4 3.5 %all-to-all-start.2 = ((f32[8,4,3,8,128]{4,3,2,1,0:T(8,128)}), f32[8,4,3,8,128]{4,3,2,1,0:T(8,128)S(1)}, u32[]{:S(2)}, u32[]{:S(2)}) async-start(f32[8,4,3,8,128]{4,3,2,1,0:T(8,128)} %shard_map.109), calls=%async_computation.2 | async-start | bytes 786432 | tf_op jit(solution)/shard_map/all_to_all | solution.py:183
  62.9 0.1 reshape.296
  63.0 0.1 reshape.295
  63.1 0.1 fusion.27
  63.2 0.2 copy.209
  63.4 0.2 select_reduce_fusion.2
  63.6 9.5 %all-to-all-done.2 = f32[8,4,3,8,128]{4,3,2,1,0:T(8,128)S(1)} async-done(((f32[8,4,3,8,128]{4,3,2,1,0:T(8,128)}), f32[8,4,3,8,128]{4,3,2,1,0:T(8,128)S(1)}, u32[]{:S(2)}, u32[]{:S(2)}) %all-to-all-start.2) | async-done | bytes 393248 | tf_op jit(solution)/shard_map/all_to_all | solution.py:183
  73.0 0.2 slice.44
  73.2 0.2 copy.225
  73.3 0.1 select_reduce_fusion.1
  73.5 0.1 copy.198
  73.6 0.2 slice.43
  73.7 0.5 copy.199
  74.2 0.1 fusion.24
  74.3 0.1 copy.201
  74.4 0.2 fusion.68
  74.6 0.4 fusion.71
  75.0 0.9 %copy.226 = f32[8,4,3,5,1]{3,2,1,0,4:T(4,128)S(1)} copy(f32[8,4,3,5,1]{4,3,2,1,0:T(8,128)S(1)} %get-tuple-element.8) | data formatting | bytes 3840 | tf_op jit(solution)/shard_map/mul | solution.py:194
  75.9 0.5 copy.220
  76.3 0.2 fusion.22
  76.6 0.1 fusion.25
  76.7 0.2 fusion.11
  76.9 0.1 select_convert_fusion
  77.0 0.7 convert_element_type.59
  (35 shorter events, 0.3 us)
Async XLA Ops:
  0.0 8.8 %copy-start = (bf16[1536,24]{0,1:T(8,128)(2,1)S(1)}, bf16[1536,24]{0,1:T(8,128)(2,1)}, u32[]{:S(2)}) copy-start(bf16[1536,24]{0,1:T(8,128)(2,1)} %param.14) | copy-start | bytes 221188
  0.0 8.5 %copy-start.1 = (bf16[4,5,1536]{2,0,1:T(4,128)(2,1)S(1)}, bf16[4,5,1536]{2,0,1:T(4,128)(2,1)}, u32[]{:S(2)}) copy-start(bf16[4,5,1536]{2,0,1:T(4,128)(2,1)} %param.11) | copy-start | bytes 184324
  0.0 8.6 %copy-start.5 = (s32[4,8]{1,0:T(4,128)S(1)}, s32[4,8]{1,0:T(4,128)}, u32[]{:S(2)}) copy-start(s32[4,8]{1,0:T(4,128)} %param.20) | copy-start | bytes 388
  0.0 8.8 %copy-start.4 = (f32[1536]{0:T(1024)S(1)}, f32[1536]{0:T(1024)}, u32[]{:S(2)}) copy-start(f32[1536]{0:T(1024)} %param.12) | copy-start | bytes 18436
  0.0 8.8 %copy-start.7 = (f32[24]{0:T(128)S(1)}, f32[24]{0:T(128)}, u32[]{:S(2)}) copy-start(f32[24]{0:T(128)} %param.15) | copy-start | bytes 292
  0.0 9.1 %copy-start.6 = (s32[4]{0:T(128)S(1)}, s32[4]{0:T(128)}, u32[]{:S(2)}) copy-start(s32[4]{0:T(128)} %param.19) | copy-start | bytes 52
  0.0 9.2 %copy-start.2 = (f32[4,24,512]{2,1,0:T(8,128)S(1)}, f32[4,24,512]{2,1,0:T(8,128)}, u32[]{:S(2)}) copy-start(f32[4,24,512]{2,1,0:T(8,128)} %param.18) | copy-start | bytes 589828
  0.0 9.6 %copy-start.3 = (bf16[1536,3,3,4]{0,3,2,1:T(4,128)(2,1)S(1)}, bf16[1536,3,3,4]{0,3,2,1:T(4,128)(2,1)}, u32[]{:S(2)}) copy-start(bf16[1536,3,3,4]{0,3,2,1:T(4,128)(2,1)} %param.13) | copy-start | bytes 331780
  2.1 24.5 %all-to-all-start = ((bf16[16,20,1536]{2,1,0:T(8,128)(2,1)}), bf16[16,20,1536]{2,1,0:T(8,128)(2,1)S(1)}, u32[]{:S(2)}, u32[]{:S(2)}) async-start(bf16[16,20,1536]{2,1,0:T(8,128)(2,1)} %broadcast_in_dim.147), calls=%async_computation | async-start | bytes 2359296 | tf_op jit(solution)/shard_map/all_to_all | solution.py:115
  27.3 9.8 %copy-start.8 = (s32[4]{0:T(128)S(1)}, s32[4]{0:T(128)}, u32[]{:S(2)}) copy-start(s32[4]{0:T(128)} %param.21) | copy-start | bytes 52
  29.4 17.5 %all-to-all-start.1 = ((bf16[128,2,360]{2,1,0:T(2,128)(2,1)}), bf16[128,2,360]{2,1,0:T(2,128)(2,1)S(1)}, u32[]{:S(2)}, u32[]{:S(2)}) async-start(bf16[128,2,360]{2,1,0:T(2,128)(2,1)} %reshape.286), calls=%async_computation.1 | async-start | bytes 393216 | tf_op jit(solution)/shard_map/all_to_all | solution.py:134
  59.4 13.6 %all-to-all-start.2 = ((f32[8,4,3,8,128]{4,3,2,1,0:T(8,128)}), f32[8,4,3,8,128]{4,3,2,1,0:T(8,128)S(1)}, u32[]{:S(2)}, u32[]{:S(2)}) async-start(f32[8,4,3,8,128]{4,3,2,1,0:T(8,128)} %shard_map.109), calls=%async_computation.2 | async-start | bytes 786432 | tf_op jit(solution)/shard_map/all_to_all | solution.py:183

commit v13 on v5

--- a/solution.py
+++ b/solution.py
@@ -119,6 +119,7 @@
         tiled=True,
     )
     normed_all = normalize(hidden_all, norm_gain).reshape(fsdp_count * rows, width)
+    normed = normalize(hidden_in, norm_gain).reshape(rows, width)
     projected = jnp.einsum(
         "dk,nd->kn",
         w_qkv.reshape(width, own_cols),
@@ -132,7 +133,7 @@
     )
     outgoing = jnp.broadcast_to(
         outgoing, (fsdp_count, seq_count, own_heads * own_dims * 3 * rows)
-    ).reshape(fsdp_count * seq_count, own_heads * own_dims * 3 * rows)
+    ).reshape(fsdp_count * seq_count, 2, own_heads * own_dims * 3 * rows // 2)
     incoming = lax.all_to_all(outgoing, ("fsdp", "seq"), 0, 0, tiled=True)
     incoming = incoming.reshape(fsdp_count * seq_count * own_heads * own_dims, 3 * rows)
     src_row = jnp.arange(fsdp_count * seq_count * own_heads * own_dims, dtype=jnp.int32)
@@ -148,7 +149,6 @@
     all_heads = jnp.einsum(
         "kx,kj->xj", incoming, placement, preferred_element_type=jnp.float32
     ).astype(jnp.bfloat16).reshape(3, req_count, new_count, inner_width)
-    normed = normalize(hidden_in, norm_gain).reshape(rows, width)
     gate_logit = (
         jnp.dot(normed, w_forget, preferred_element_type=jnp.float32).reshape(
             req_count, new_count, head_count

time: 79.6 us -> 76.9 us (0.966)
  other arithmetic: 5.93 us -> 3.92 us
    all_to_all x2 -> x0, other arithmetic: 2.01 us -> none  [body(): incoming = lax.all_to_all(outgoing, ('fsdp', 'seq'), 0, 0, tiled=True)]
    unnamed x21 -> x19, local copies, waits for them, and re-layouts: 1.37 us -> 0.14 us
    reshape x0 -> x1, local copies, waits for them, and re-layouts: none -> 0.89 us  [body(): outgoing = jnp.broadcast_to(outgoing, (fsdp_count, seq_count, own_heads *...]
where the time goes in v13:
time: 76.9 us; the launch traced here: 76.5 us
  waiting for transfers between devices  30.1 us (39%)
  starting transfers between devices  17.5 us (23%)
  local copies, waits for them, and re-layouts  11.8 us (15%)
  Pallas kernels  8.98 us (12%)
  other arithmetic  3.92 us (5%)
  matrix products  3.87 us (5%)
    all_to_all x1, waiting for transfers between devices, body(): lax.all_to_all(jnp.broadcast_to(hidden_in[None], (fsdp_count, req_count,...  10.7 us
    all_to_all x1, waiting for transfers between devices, body(): incoming = lax.all_to_all(outgoing, ('fsdp', 'seq'), 0, 0, tiled=True)  9.91 us
    all_to_all x1, waiting for transfers between devices, body(): parts = lax.all_to_all(packed, 'seq', 0, 0, tiled=True)[:, :, :, :new_count]  9.45 us
    pallas_call x1, Pallas kernels, piece_attention(): pl.pallas_call(attention_kernel, grid=(req_count,), in_specs=[pl.BlockSpe...  8.98 us
    all_to_all x1, starting transfers between devices, body(): incoming = lax.all_to_all(outgoing, ('fsdp', 'seq'), 0, 0, tiled=True)  7.58 us
    all_to_all x1, starting transfers between devices, body(): lax.all_to_all(jnp.broadcast_to(hidden_in[None], (fsdp_count, req_count,...  6.44 us
    all_to_all x1, starting transfers between devices, body(): parts = lax.all_to_all(packed, 'seq', 0, 0, tiled=True)[:, :, :, :new_count]  3.45 us
    broadcast_in_dim x1, local copies, waits for them, and re-layouts, body(): jnp.broadcast_to(hidden_in[None], (fsdp_count, req_count, new_count, width))  2.08 us
  transfers between devices with their start and end apart: 3, of which 3 were waited for; matrix products, arithmetic and copies ran while one was open for 7% of the time, Pallas kernels for 0%

profile of v13, /device:TPU:0, one launch (start us, length us, event | category | flops | bytes accessed | tf_op | source)
XLA Modules:
  0.0 76.5 jit_solution(4390264231738500021)
XLA Ops:
  0.1 2.1 %broadcast_in_dim.95 = bf16[16,4,5,1536]{3,1,2,0:T(4,128)(2,1)} broadcast(bf16[4,5,1536]{2,0,1:T(4,128)(2,1)} %param.11), dimensions={1,2,3} | broadcast | bytes 1044480 | tf_op jit(solution)/shard_map/broadcast_in_dim | solution.py:115
  2.1 6.4 %all-to-all-start = ((bf16[16,4,5,1536]{3,1,2,0:T(4,128)(2,1)}), bf16[16,4,5,1536]{3,1,2,0:T(4,128)(2,1)S(1)}, u32[]{:S(2)}, u32[]{:S(2)}) async-start(bf16[16,4,5,1536]{3,1,2,0:T(4,128)(2,1)} %broadcast_in_dim.95), calls=%async_computation | async-start | bytes 1966080 | tf_op jit(solution)/shard_map/all_to_all | solution.py:114
  8.6 0.1 fusion.13
  8.7 0.1 select_reduce_fusion.4
  8.9 0.3 fusion.65
  9.2 0.1 add_compare_fusion
  9.3 0.0 copy-done.2
  9.3 0.1 select_reduce_fusion
  9.4 0.1 dynamic-slice_bitcast_fusion
  9.5 0.1 copy.212
  9.6 0.1 copy.211
  9.7 0.0 copy-done.3
  9.7 0.1 copy.236
  9.9 0.9 %reshape.281.prefix_ref = f32[4,192,1]{2,1,0:T(8,128)} reshape(f32[4,24,8]{2,1,0:T(8,128)S(1)} %pad.9.clone) | data formatting | bytes 6144 | tf_op jit(solution)/shard_map/reshape | solution.py:176
  10.8 0.1 broadcast_in_dim.152
  10.9 0.9 %reshape.282.total_ref = f32[4,192,1]{2,1,0:T(8,128)} reshape(f32[4,24,8]{2,1,0:T(8,128)S(1)} %broadcast_in_dim.152) | data formatting | bytes 6144 | tf_op jit(solution)/shard_map/reshape | solution.py:182
  11.8 0.1 select_reduce_fusion.3
  11.9 0.1 broadcast_compare_fusion
  12.0 0.7 compare_convert_fusion.live_ref
  12.7 1.0 %fusion.9.trail_ref = f32[4,24,512]{2,1,0:T(8,128)} fusion(f32[4,24,512]{2,1,0:T(8,128)S(1)} %copy-done.2, pred[4,512]{1,0:T(4,128)(4,1)S(1)} %add_compare_fusion), kind=kOutput, calls=%fused_computation.15 | convolution fusion | flops 302301184 | bytes 395264 | tf_op jit(solution)/shard_map/rhl,lj->rhj/dot_general | solution.py:169
  13.7 10.7 %all-to-all-done = bf16[16,4,5,1536]{3,1,2,0:T(4,128)(2,1)S(1)} async-done(((bf16[16,4,5,1536]{3,1,2,0:T(4,128)(2,1)}), bf16[16,4,5,1536]{3,1,2,0:T(4,128)(2,1)S(1)}, u32[]{:S(2)}, u32[]{:S(2)}) %all-to-all-start) | async-done | bytes 983072 | tf_op jit(solution)/shard_map/all_to_all | solution.py:114
  24.4 0.6 fusion.3
  25.0 0.6 fusion.5
  25.6 0.3 copy.192
  25.9 0.5 reshape.271
  26.4 0.0 copy-start.8
  26.4 0.4 fusion.6
  26.8 0.2 reshape.273
  27.0 0.1 copy.252
  27.2 0.2 broadcast_in_dim.146
  27.4 0.9 %reshape.274 = bf16[128,2,360]{2,1,0:T(2,128)(2,1)} reshape(bf16[16,8,720]{2,1,0:T(8,128)(2,1)S(1)} %broadcast_in_dim.147) | data formatting | bytes 368640 | tf_op jit(solution)/shard_map/reshape | solution.py:136
  28.3 7.6 %all-to-all-start.1 = ((bf16[128,2,360]{2,1,0:T(2,128)(2,1)}), bf16[128,2,360]{2,1,0:T(2,128)(2,1)S(1)}, u32[]{:S(2)}, u32[]{:S(2)}) async-start(bf16[128,2,360]{2,1,0:T(2,128)(2,1)} %reshape.274), calls=%async_computation.1 | async-start | bytes 393216 | tf_op jit(solution)/shard_map/all_to_all | solution.py:137
  35.9 9.9 %all-to-all-done.1 = bf16[128,2,360]{2,1,0:T(2,128)(2,1)S(1)} async-done(((bf16[128,2,360]{2,1,0:T(2,128)(2,1)}), bf16[128,2,360]{2,1,0:T(2,128)(2,1)S(1)}, u32[]{:S(2)}, u32[]{:S(2)}) %all-to-all-start.1) | async-done | bytes 184352 | tf_op jit(solution)/shard_map/all_to_all | solution.py:137
  45.8 0.6 reshape.275
  46.4 1.9 %fusion.2 = bf16[60,1536]{1,0:T(8,128)(2,1)S(1)} fusion(bf16[1536,60]{1,0:T(8,128)(2,1)S(1)} %reshape.275, s32[1536]{0:T(1024)S(1)} %fusion.51), kind=kOutput, calls=%fused_computation.5 | convolution fusion | flops 285566976 | bytes 374784 | tf_op jit(solution)/shard_map/kx,kj->xj/dot_general | solution.py:149
  48.3 0.1 reshape.278
  48.4 0.1 constant_dynamic-slice_fusion
  48.5 0.1 reshape.285
  48.6 0.7 pad.8.q_ref
  49.3 9.0 %shard_map.109 = f32[8,4,3,8,128]{4,3,2,1,0:T(8,128)} custom-call(bf16[4,8,1536]{2,1,0:T(8,128)(2,1)} %pad.8.q_ref, bf16[4,512,1536]{2,1,0:T(8,128)(2,1)} %k_ref.1, bf16[4,512,1536]{2,1,0:T(8,128)(2,1)} %v_ref.1, f32[4,24,512]{2,1,0:T(8,128)} %fusion.9.trail_ref, f32[4,192,1]{2,1,0:T(8,128)} %reshape.281.prefix_ref, ...), custom_call_target="tpu_custom_call" | custom-call | tf_op jit(solution)/shard_map/pallas_call | solution.py:71
  58.3 3.5 %all-to-all-start.2 = ((f32[8,4,3,8,128]{4,3,2,1,0:T(8,128)}), f32[8,4,3,8,128]{4,3,2,1,0:T(8,128)S(1)}, u32[]{:S(2)}, u32[]{:S(2)}) async-start(f32[8,4,3,8,128]{4,3,2,1,0:T(8,128)} %shard_map.109), calls=%async_computation.2 | async-start | bytes 786432 | tf_op jit(solution)/shard_map/all_to_all | solution.py:186
  61.7 0.1 reshape.284
  61.8 0.1 reshape.283
  61.9 0.1 fusion.27
  62.0 0.2 copy.210
  62.2 0.2 select_reduce_fusion.2
  62.4 9.5 %all-to-all-done.2 = f32[8,4,3,8,128]{4,3,2,1,0:T(8,128)S(1)} async-done(((f32[8,4,3,8,128]{4,3,2,1,0:T(8,128)}), f32[8,4,3,8,128]{4,3,2,1,0:T(8,128)S(1)}, u32[]{:S(2)}, u32[]{:S(2)}) %all-to-all-start.2) | async-done | bytes 393248 | tf_op jit(solution)/shard_map/all_to_all | solution.py:186
  71.8 0.2 slice.44
  72.0 0.2 copy.226
  72.2 0.1 select_reduce_fusion.1
  72.3 0.1 copy.199
  72.4 0.2 slice.43
  72.6 0.5 copy.200
  73.0 0.1 fusion.24
  73.1 0.1 copy.202
  73.2 0.2 fusion.68
  73.4 0.4 fusion.71
  73.8 0.9 %copy.227 = f32[8,4,3,5,1]{3,2,1,0,4:T(4,128)S(1)} copy(f32[8,4,3,5,1]{4,3,2,1,0:T(8,128)S(1)} %get-tuple-element.8) | data formatting | bytes 3840 | tf_op jit(solution)/shard_map/mul | solution.py:197
  74.7 0.5 copy.221
  75.2 0.2 fusion.22
  75.4 0.1 fusion.25
  75.5 0.2 fusion.11
  75.7 0.1 select_convert_fusion
  75.8 0.7 convert_element_type.56
  (34 shorter events, 0.3 us)
Async XLA Ops:
  0.0 8.8 %copy-start = (bf16[1536,24]{0,1:T(8,128)(2,1)S(1)}, bf16[1536,24]{0,1:T(8,128)(2,1)}, u32[]{:S(2)}) copy-start(bf16[1536,24]{0,1:T(8,128)(2,1)} %param.14) | copy-start | bytes 221188
  0.0 8.6 %copy-start.1 = (bf16[4,5,1536]{2,0,1:T(4,128)(2,1)S(1)}, bf16[4,5,1536]{2,0,1:T(4,128)(2,1)}, u32[]{:S(2)}) copy-start(bf16[4,5,1536]{2,0,1:T(4,128)(2,1)} %param.11) | copy-start | bytes 184324
  0.0 8.7 %copy-start.5 = (s32[4,8]{1,0:T(4,128)S(1)}, s32[4,8]{1,0:T(4,128)}, u32[]{:S(2)}) copy-start(s32[4,8]{1,0:T(4,128)} %param.20) | copy-start | bytes 388
  0.0 8.9 %copy-start.4 = (f32[1536]{0:T(1024)S(1)}, f32[1536]{0:T(1024)}, u32[]{:S(2)}) copy-start(f32[1536]{0:T(1024)} %param.12) | copy-start | bytes 18436
  0.0 8.9 %copy-start.7 = (f32[24]{0:T(128)S(1)}, f32[24]{0:T(128)}, u32[]{:S(2)}) copy-start(f32[24]{0:T(128)} %param.15) | copy-start | bytes 292
  0.0 9.1 %copy-start.6 = (s32[4]{0:T(128)S(1)}, s32[4]{0:T(128)}, u32[]{:S(2)}) copy-start(s32[4]{0:T(128)} %param.19) | copy-start | bytes 52
  0.0 9.2 %copy-start.2 = (f32[4,24,512]{2,1,0:T(8,128)S(1)}, f32[4,24,512]{2,1,0:T(8,128)}, u32[]{:S(2)}) copy-start(f32[4,24,512]{2,1,0:T(8,128)} %param.18) | copy-start | bytes 589828
  0.0 9.7 %copy-start.3 = (bf16[1536,3,3,4]{0,3,2,1:T(4,128)(2,1)S(1)}, bf16[1536,3,3,4]{0,3,2,1:T(4,128)(2,1)}, u32[]{:S(2)}) copy-start(bf16[1536,3,3,4]{0,3,2,1:T(4,128)(2,1)} %param.13) | copy-start | bytes 331780
  2.1 22.3 %all-to-all-start = ((bf16[16,4,5,1536]{3,1,2,0:T(4,128)(2,1)}), bf16[16,4,5,1536]{3,1,2,0:T(4,128)(2,1)S(1)}, u32[]{:S(2)}, u32[]{:S(2)}) async-start(bf16[16,4,5,1536]{3,1,2,0:T(4,128)(2,1)} %broadcast_in_dim.95), calls=%async_computation | async-start | bytes 1966080 | tf_op jit(solution)/shard_map/all_to_all | solution.py:114
  26.4 9.5 %copy-start.8 = (s32[4]{0:T(128)S(1)}, s32[4]{0:T(128)}, u32[]{:S(2)}) copy-start(s32[4]{0:T(128)} %param.21) | copy-start | bytes 52
  28.3 17.5 %all-to-all-start.1 = ((bf16[128,2,360]{2,1,0:T(2,128)(2,1)}), bf16[128,2,360]{2,1,0:T(2,128)(2,1)S(1)}, u32[]{:S(2)}, u32[]{:S(2)}) async-start(bf16[128,2,360]{2,1,0:T(2,128)(2,1)} %reshape.274), calls=%async_computation.1 | async-start | bytes 393216 | tf_op jit(solution)/shard_map/all_to_all | solution.py:137
  58.3 13.6 %all-to-all-start.2 = ((f32[8,4,3,8,128]{4,3,2,1,0:T(8,128)}), f32[8,4,3,8,128]{4,3,2,1,0:T(8,128)S(1)}, u32[]{:S(2)}, u32[]{:S(2)}) async-start(f32[8,4,3,8,128]{4,3,2,1,0:T(8,128)} %shard_map.109), calls=%async_computation.2 | async-start | bytes 786432 | tf_op jit(solution)/shard_map/all_to_all | solution.py:186

commit v14 on v8

--- a/solution.py
+++ b/solution.py
@@ -111,10 +111,15 @@
     logit_scale = HEAD_DIM ** (-0.5)
     seq_index = lax.axis_index("seq")
     head_start = seq_index * own_heads
+    hidden_all = lax.all_to_all(
+        jnp.broadcast_to(hidden_in[None], (fsdp_count, req_count, new_count, width)),
+        "fsdp",
+        0,
+        0,
+        tiled=True,
+    )
+    normed_all = normalize(hidden_all, norm_gain).reshape(fsdp_count * rows, width)
     normed = normalize(hidden_in, norm_gain).reshape(rows, width)
-    normed_all = lax.all_to_all(
-        jnp.broadcast_to(normed[None], (fsdp_count, rows, width)), "fsdp", 0, 0, tiled=True
-    ).reshape(fsdp_count * rows, width)
     projected = jnp.einsum(
         "dk,nd->kn",
         w_qkv.reshape(width, own_cols),

time: 78.7 us -> 77 us (0.978)
  other arithmetic: 8.14 us -> 3.91 us
  waiting for transfers between devices: 26.6 us -> 30.3 us
  matrix products: 5.38 us -> 3.87 us
    all_to_all x1, waiting for transfers between devices: 7.12 us -> 10.8 us  [body(): lax.all_to_all(jnp.broadcast_to(hidden_in[None], (fsdp_count, req_count,...]
    broadcast_in_dim x2 -> x1, local copies, waits for them, and re-layouts: 1.12 us -> 2.08 us  [body(): jnp.broadcast_to(hidden_in[None], (fsdp_count, req_count, new_count, width))]
    reduce_sum x1, other arithmetic: 1.02 us -> 0.1 us  [body(): piece_total = jnp.sum(masked, axis=-1)]
    dot_general x1, matrix products: 1.97 us -> 1.05 us  [body(): jnp.einsum('rhl,lj->rhj', masked, later_step, precision=lax.Precision.HIG...]
    reshape x1, local copies, waits for them, and re-layouts: 0.93 us -> 0.03 us  [body(): w_qkv.reshape(width, own_cols)]
  transfers between devices with their start and end apart: 3 -> 3, of which waited for: 3 -> 3; matrix products, arithmetic and copies ran while one was open for 15% -> 7% of each run, Pallas kernels for 0% -> 0%
where the time goes in v14:
time: 77 us; the launch traced here: 76.7 us
  waiting for transfers between devices  30.3 us (39%)
  starting transfers between devices  17.5 us (23%)
  local copies, waits for them, and re-layouts  11.8 us (15%)
  Pallas kernels  8.98 us (12%)
  other arithmetic  3.91 us (5%)
  matrix products  3.87 us (5%)
    all_to_all x1, waiting for transfers between devices, body(): lax.all_to_all(jnp.broadcast_to(hidden_in[None], (fsdp_count, req_count,...  10.8 us
    all_to_all x1, waiting for transfers between devices, body(): incoming = lax.all_to_all(outgoing, ('fsdp', 'seq'), 0, 0, tiled=True)  9.91 us
    all_to_all x1, waiting for transfers between devices, body(): parts = lax.all_to_all(packed, 'seq', 0, 0, tiled=True)[:, :, :, :new_count]  9.6 us
    pallas_call x1, Pallas kernels, piece_attention(): pl.pallas_call(attention_kernel, grid=(req_count,), in_specs=[pl.BlockSpe...  8.98 us
    all_to_all x1, starting transfers between devices, body(): incoming = lax.all_to_all(outgoing, ('fsdp', 'seq'), 0, 0, tiled=True)  7.58 us
    all_to_all x1, starting transfers between devices, body(): lax.all_to_all(jnp.broadcast_to(hidden_in[None], (fsdp_count, req_count,...  6.44 us
    all_to_all x1, starting transfers between devices, body(): parts = lax.all_to_all(packed, 'seq', 0, 0, tiled=True)[:, :, :, :new_count]  3.45 us
    broadcast_in_dim x1, local copies, waits for them, and re-layouts, body(): jnp.broadcast_to(hidden_in[None], (fsdp_count, req_count, new_count, width))  2.08 us
  transfers between devices with their start and end apart: 3, of which 3 were waited for; matrix products, arithmetic and copies ran while one was open for 7% of the time, Pallas kernels for 0%

profile of v14, /device:TPU:0, one launch (start us, length us, event | category | flops | bytes accessed | tf_op | source)
XLA Modules:
  0.0 76.7 jit_solution(16245637688763160477)
XLA Ops:
  0.1 2.1 %broadcast_in_dim.95 = bf16[16,4,5,1536]{3,1,2,0:T(4,128)(2,1)} broadcast(bf16[4,5,1536]{2,0,1:T(4,128)(2,1)} %param.11), dimensions={1,2,3} | broadcast | bytes 1044480 | tf_op jit(solution)/shard_map/broadcast_in_dim | solution.py:115
  2.1 6.4 %all-to-all-start = ((bf16[16,4,5,1536]{3,1,2,0:T(4,128)(2,1)}), bf16[16,4,5,1536]{3,1,2,0:T(4,128)(2,1)S(1)}, u32[]{:S(2)}, u32[]{:S(2)}) async-start(bf16[16,4,5,1536]{3,1,2,0:T(4,128)(2,1)} %broadcast_in_dim.95), calls=%async_computation | async-start | bytes 1966080 | tf_op jit(solution)/shard_map/all_to_all | solution.py:114
  8.6 0.1 fusion.13
  8.7 0.0 copy-done.7
  8.7 0.3 fusion.67
  9.0 0.1 select_reduce_fusion.4
  9.2 0.1 dynamic-slice_bitcast_fusion
  9.3 0.0 copy-done.6
  9.3 0.1 add_compare_fusion
  9.3 0.1 select_reduce_fusion
  9.4 0.1 copy.207
  9.6 0.1 copy.206
  9.7 0.1 copy.236
  9.8 0.9 %reshape.282.prefix_ref = f32[4,192,1]{2,1,0:T(8,128)} reshape(f32[4,24,8]{2,1,0:T(8,128)S(1)} %pad.9.clone) | data formatting | bytes 6144 | tf_op jit(solution)/shard_map/reshape | solution.py:176
  10.8 0.1 broadcast_in_dim.152
  10.8 0.9 %reshape.283.total_ref = f32[4,192,1]{2,1,0:T(8,128)} reshape(f32[4,24,8]{2,1,0:T(8,128)S(1)} %broadcast_in_dim.152) | data formatting | bytes 6144 | tf_op jit(solution)/shard_map/reshape | solution.py:182
  11.8 0.1 select_reduce_fusion.3
  11.9 0.1 broadcast_compare_fusion
  12.0 0.7 compare_convert_fusion.live_ref
  12.6 1.0 %fusion.9.trail_ref = f32[4,24,512]{2,1,0:T(8,128)} fusion(f32[4,24,512]{2,1,0:T(8,128)S(1)} %copy-done.2, pred[4,512]{1,0:T(4,128)(4,1)S(1)} %add_compare_fusion), kind=kOutput, calls=%fused_computation.15 | convolution fusion | flops 302301184 | bytes 395264 | tf_op jit(solution)/shard_map/rhl,lj->rhj/dot_general | solution.py:169
  13.7 10.8 %all-to-all-done = bf16[16,4,5,1536]{3,1,2,0:T(4,128)(2,1)S(1)} async-done(((bf16[16,4,5,1536]{3,1,2,0:T(4,128)(2,1)}), bf16[16,4,5,1536]{3,1,2,0:T(4,128)(2,1)S(1)}, u32[]{:S(2)}, u32[]{:S(2)}) %all-to-all-start) | async-done | bytes 983072 | tf_op jit(solution)/shard_map/all_to_all | solution.py:114
  24.4 0.6 fusion.3
  25.0 0.6 fusion.5
  25.6 0.3 copy.191
  25.9 0.5 reshape.272
  26.4 0.0 copy-start.8
  26.4 0.4 fusion.6
  26.8 0.2 reshape.274
  27.0 0.1 copy.252
  27.2 0.2 broadcast_in_dim.146
  27.4 0.9 %reshape.275 = bf16[128,2,360]{2,1,0:T(2,128)(2,1)} reshape(bf16[16,8,720]{2,1,0:T(8,128)(2,1)S(1)} %broadcast_in_dim.147) | data formatting | bytes 368640 | tf_op jit(solution)/shard_map/reshape | solution.py:136
  28.3 7.6 %all-to-all-start.1 = ((bf16[128,2,360]{2,1,0:T(2,128)(2,1)}), bf16[128,2,360]{2,1,0:T(2,128)(2,1)S(1)}, u32[]{:S(2)}, u32[]{:S(2)}) async-start(bf16[128,2,360]{2,1,0:T(2,128)(2,1)} %reshape.275), calls=%async_computation.1 | async-start | bytes 393216 | tf_op jit(solution)/shard_map/all_to_all | solution.py:137
  35.9 9.9 %all-to-all-done.1 = bf16[128,2,360]{2,1,0:T(2,128)(2,1)S(1)} async-done(((bf16[128,2,360]{2,1,0:T(2,128)(2,1)}), bf16[128,2,360]{2,1,0:T(2,128)(2,1)S(1)}, u32[]{:S(2)}, u32[]{:S(2)}) %all-to-all-start.1) | async-done | bytes 184352 | tf_op jit(solution)/shard_map/all_to_all | solution.py:137
  45.8 0.6 reshape.276
  46.4 1.9 %fusion.2 = bf16[60,1536]{1,0:T(8,128)(2,1)S(1)} fusion(bf16[1536,60]{1,0:T(8,128)(2,1)S(1)} %reshape.276, s32[1536]{0:T(1024)S(1)} %fusion.53), kind=kOutput, calls=%fused_computation.5 | convolution fusion | flops 285566976 | bytes 374784 | tf_op jit(solution)/shard_map/kx,kj->xj/dot_general | solution.py:149
  48.3 0.1 reshape.279
  48.4 0.1 constant_dynamic-slice_fusion
  48.5 0.1 reshape.286
  48.6 0.1 reshape.285
  48.7 0.1 reshape.284
  48.8 0.1 fusion.28
  48.9 0.2 copy.205
  49.1 0.7 pad.8.q_ref
  49.8 9.0 %shard_map.109 = f32[8,4,3,8,128]{4,3,2,1,0:T(8,128)} custom-call(bf16[4,8,1536]{2,1,0:T(8,128)(2,1)} %pad.8.q_ref, bf16[4,512,1536]{2,1,0:T(8,128)(2,1)} %k_ref.1, bf16[4,512,1536]{2,1,0:T(8,128)(2,1)} %v_ref.1, f32[4,24,512]{2,1,0:T(8,128)} %fusion.9.trail_ref, f32[4,192,1]{2,1,0:T(8,128)} %reshape.282.prefix_ref, ...), custom_call_target="tpu_custom_call" | custom-call | tf_op jit(solution)/shard_map/pallas_call | solution.py:71
  58.7 3.5 %all-to-all-start.2 = ((f32[8,4,3,8,128]{4,3,2,1,0:T(8,128)}), f32[8,4,3,8,128]{4,3,2,1,0:T(8,128)S(1)}, u32[]{:S(2)}, u32[]{:S(2)}) async-start(f32[8,4,3,8,128]{4,3,2,1,0:T(8,128)} %shard_map.109), calls=%async_computation.2 | async-start | bytes 786432 | tf_op jit(solution)/shard_map/all_to_all | solution.py:213
  62.2 0.2 select_reduce_fusion.2
  62.4 0.2 fusion.70
  62.6 0.1 fusion.26
  62.7 9.6 %all-to-all-done.2 = f32[8,4,3,8,128]{4,3,2,1,0:T(8,128)S(1)} async-done(((f32[8,4,3,8,128]{4,3,2,1,0:T(8,128)}), f32[8,4,3,8,128]{4,3,2,1,0:T(8,128)S(1)}, u32[]{:S(2)}, u32[]{:S(2)}) %all-to-all-start.2) | async-done | bytes 393248 | tf_op jit(solution)/shard_map/all_to_all | solution.py:213
  72.3 0.2 slice.44
  72.5 0.2 copy.226
  72.6 0.1 select_reduce_fusion.1
  72.8 0.1 copy.198
  72.9 0.2 slice.43
  73.0 0.5 copy.199
  73.5 0.1 fusion.25
  73.6 0.1 copy.210
  73.7 0.4 fusion.73
  74.1 0.9 %copy.231 = f32[8,4,3,5,1]{3,2,1,0,4:T(4,128)S(1)} copy(f32[8,4,3,5,1]{4,3,2,1,0:T(8,128)S(1)} %get-tuple-element.8) | data formatting | bytes 3840 | tf_op jit(solution)/shard_map/mul | solution.py:225
  75.0 0.5 copy.221
  75.5 0.2 fusion.22
  75.7 0.2 fusion.11
  75.9 0.1 select_convert_fusion
  76.0 0.7 convert_element_type.56
  (34 shorter events, 0.3 us)
Async XLA Ops:
  0.0 8.7 %copy-start = (bf16[1536,24]{0,1:T(8,128)(2,1)S(1)}, bf16[1536,24]{0,1:T(8,128)(2,1)}, u32[]{:S(2)}) copy-start(bf16[1536,24]{0,1:T(8,128)(2,1)} %param.14) | copy-start | bytes 221188
  0.0 8.6 %copy-start.1 = (bf16[4,5,1536]{2,0,1:T(4,128)(2,1)S(1)}, bf16[4,5,1536]{2,0,1:T(4,128)(2,1)}, u32[]{:S(2)}) copy-start(bf16[4,5,1536]{2,0,1:T(4,128)(2,1)} %param.11) | copy-start | bytes 184324
  0.0 8.7 %copy-start.4 = (f32[1536]{0:T(1024)S(1)}, f32[1536]{0:T(1024)}, u32[]{:S(2)}) copy-start(f32[1536]{0:T(1024)} %param.12) | copy-start | bytes 18436
  0.0 8.7 %copy-start.7 = (f32[24]{0:T(128)S(1)}, f32[24]{0:T(128)}, u32[]{:S(2)}) copy-start(f32[24]{0:T(128)} %param.15) | copy-start | bytes 292
  0.0 9.0 %copy-start.5 = (s32[4,8]{1,0:T(4,128)S(1)}, s32[4,8]{1,0:T(4,128)}, u32[]{:S(2)}) copy-start(s32[4,8]{1,0:T(4,128)} %param.20) | copy-start | bytes 388
  0.0 9.2 %copy-start.6 = (s32[4]{0:T(128)S(1)}, s32[4]{0:T(128)}, u32[]{:S(2)}) copy-start(s32[4]{0:T(128)} %param.19) | copy-start | bytes 52
  0.0 9.3 %copy-start.2 = (f32[4,24,512]{2,1,0:T(8,128)S(1)}, f32[4,24,512]{2,1,0:T(8,128)}, u32[]{:S(2)}) copy-start(f32[4,24,512]{2,1,0:T(8,128)} %param.18) | copy-start | bytes 589828
  0.0 9.7 %copy-start.3 = (bf16[1536,3,3,4]{0,3,2,1:T(4,128)(2,1)S(1)}, bf16[1536,3,3,4]{0,3,2,1:T(4,128)(2,1)}, u32[]{:S(2)}) copy-start(bf16[1536,3,3,4]{0,3,2,1:T(4,128)(2,1)} %param.13) | copy-start | bytes 331780
  2.1 22.3 %all-to-all-start = ((bf16[16,4,5,1536]{3,1,2,0:T(4,128)(2,1)}), bf16[16,4,5,1536]{3,1,2,0:T(4,128)(2,1)S(1)}, u32[]{:S(2)}, u32[]{:S(2)}) async-start(bf16[16,4,5,1536]{3,1,2,0:T(4,128)(2,1)} %broadcast_in_dim.95), calls=%async_computation | async-start | bytes 1966080 | tf_op jit(solution)/shard_map/all_to_all | solution.py:114
  26.4 9.5 %copy-start.8 = (s32[4]{0:T(128)S(1)}, s32[4]{0:T(128)}, u32[]{:S(2)}) copy-start(s32[4]{0:T(128)} %param.21) | copy-start | bytes 52
  28.3 17.5 %all-to-all-start.1 = ((bf16[128,2,360]{2,1,0:T(2,128)(2,1)}), bf16[128,2,360]{2,1,0:T(2,128)(2,1)S(1)}, u32[]{:S(2)}, u32[]{:S(2)}) async-start(bf16[128,2,360]{2,1,0:T(2,128)(2,1)} %reshape.275), calls=%async_computation.1 | async-start | bytes 393216 | tf_op jit(solution)/shard_map/all_to_all | solution.py:137
  58.7 13.6 %all-to-all-start.2 = ((f32[8,4,3,8,128]{4,3,2,1,0:T(8,128)}), f32[8,4,3,8,128]{4,3,2,1,0:T(8,128)S(1)}, u32[]{:S(2)}, u32[]{:S(2)}) async-start(f32[8,4,3,8,128]{4,3,2,1,0:T(8,128)} %shard_map.109), calls=%async_computation.2 | async-start | bytes 786432 | tf_op jit(solution)/shard_map/all_to_all | solution.py:213

commit v15 on v13

--- a/solution.py
+++ b/solution.py
@@ -226,11 +226,12 @@
     result = blend_weights / total_sum[..., None]
     live_rows = (step_ids[None, :] <= draft_counts[:, None])[:, None, :, None]
     result = jnp.where(live_rows, result, 0.0)
-    return (
-        jnp.transpose(result, (0, 2, 1, 3))
-        .reshape(req_count, new_count, own_heads * HEAD_DIM)
+    step_major = (
+        jnp.transpose(result, (2, 0, 1, 3))
+        .reshape(new_count, req_count, own_heads * HEAD_DIM)
         .astype(jnp.bfloat16)
     )
+    return jnp.transpose(step_major, (1, 0, 2))
 
 
 def solution(mesh):

time: 76.9 us -> 76.9 us (level)
  no operation moved by 1% of the time
where the time goes in v15:
time: 76.9 us; the launch traced here: 76.5 us
  waiting for transfers between devices  30.1 us (39%)
  starting transfers between devices  17.5 us (23%)
  local copies, waits for them, and re-layouts  11.8 us (15%)
  Pallas kernels  8.98 us (12%)
  other arithmetic  3.92 us (5%)
  matrix products  3.87 us (5%)
    all_to_all x1, waiting for transfers between devices, body(): lax.all_to_all(jnp.broadcast_to(hidden_in[None], (fsdp_count, req_count,...  10.7 us
    all_to_all x1, waiting for transfers between devices, body(): incoming = lax.all_to_all(outgoing, ('fsdp', 'seq'), 0, 0, tiled=True)  9.91 us
    all_to_all x1, waiting for transfers between devices, body(): parts = lax.all_to_all(packed, 'seq', 0, 0, tiled=True)[:, :, :, :new_count]  9.45 us
    pallas_call x1, Pallas kernels, piece_attention(): pl.pallas_call(attention_kernel, grid=(req_count,), in_specs=[pl.BlockSpe...  8.98 us
    all_to_all x1, starting transfers between devices, body(): incoming = lax.all_to_all(outgoing, ('fsdp', 'seq'), 0, 0, tiled=True)  7.58 us
    all_to_all x1, starting transfers between devices, body(): lax.all_to_all(jnp.broadcast_to(hidden_in[None], (fsdp_count, req_count,...  6.44 us
    all_to_all x1, starting transfers between devices, body(): parts = lax.all_to_all(packed, 'seq', 0, 0, tiled=True)[:, :, :, :new_count]  3.45 us
    broadcast_in_dim x1, local copies, waits for them, and re-layouts, body(): jnp.broadcast_to(hidden_in[None], (fsdp_count, req_count, new_count, width))  2.08 us
  transfers between devices with their start and end apart: 3, of which 3 were waited for; matrix products, arithmetic and copies ran while one was open for 7% of the time, Pallas kernels for 0%

profile of v15, /device:TPU:0, one launch (start us, length us, event | category | flops | bytes accessed | tf_op | source)
XLA Modules:
  0.0 76.5 jit_solution(4390264231738500021)
XLA Ops:
  0.1 2.1 %broadcast_in_dim.95 = bf16[16,4,5,1536]{3,1,2,0:T(4,128)(2,1)} broadcast(bf16[4,5,1536]{2,0,1:T(4,128)(2,1)} %param.11), dimensions={1,2,3} | broadcast | bytes 1044480 | tf_op jit(solution)/shard_map/broadcast_in_dim | solution.py:115
  2.1 6.4 %all-to-all-start = ((bf16[16,4,5,1536]{3,1,2,0:T(4,128)(2,1)}), bf16[16,4,5,1536]{3,1,2,0:T(4,128)(2,1)S(1)}, u32[]{:S(2)}, u32[]{:S(2)}) async-start(bf16[16,4,5,1536]{3,1,2,0:T(4,128)(2,1)} %broadcast_in_dim.95), calls=%async_computation | async-start | bytes 1966080 | tf_op jit(solution)/shard_map/all_to_all | solution.py:114
  8.6 0.1 fusion.13
  8.7 0.1 select_reduce_fusion.4
  8.9 0.3 fusion.65
  9.2 0.1 add_compare_fusion
  9.3 0.0 copy-done.2
  9.3 0.1 select_reduce_fusion
  9.4 0.1 dynamic-slice_bitcast_fusion
  9.5 0.1 copy.212
  9.6 0.1 copy.211
  9.7 0.0 copy-done.3
  9.7 0.1 copy.236
  9.9 0.9 %reshape.281.prefix_ref = f32[4,192,1]{2,1,0:T(8,128)} reshape(f32[4,24,8]{2,1,0:T(8,128)S(1)} %pad.9.clone) | data formatting | bytes 6144 | tf_op jit(solution)/shard_map/reshape | solution.py:176
  10.8 0.1 broadcast_in_dim.152
  10.9 0.9 %reshape.282.total_ref = f32[4,192,1]{2,1,0:T(8,128)} reshape(f32[4,24,8]{2,1,0:T(8,128)S(1)} %broadcast_in_dim.152) | data formatting | bytes 6144 | tf_op jit(solution)/shard_map/reshape | solution.py:182
  11.8 0.1 select_reduce_fusion.3
  11.9 0.1 broadcast_compare_fusion
  12.0 0.7 compare_convert_fusion.live_ref
  12.7 1.0 %fusion.9.trail_ref = f32[4,24,512]{2,1,0:T(8,128)} fusion(f32[4,24,512]{2,1,0:T(8,128)S(1)} %copy-done.2, pred[4,512]{1,0:T(4,128)(4,1)S(1)} %add_compare_fusion), kind=kOutput, calls=%fused_computation.15 | convolution fusion | flops 302301184 | bytes 395264 | tf_op jit(solution)/shard_map/rhl,lj->rhj/dot_general | solution.py:169
  13.7 10.7 %all-to-all-done = bf16[16,4,5,1536]{3,1,2,0:T(4,128)(2,1)S(1)} async-done(((bf16[16,4,5,1536]{3,1,2,0:T(4,128)(2,1)}), bf16[16,4,5,1536]{3,1,2,0:T(4,128)(2,1)S(1)}, u32[]{:S(2)}, u32[]{:S(2)}) %all-to-all-start) | async-done | bytes 983072 | tf_op jit(solution)/shard_map/all_to_all | solution.py:114
  24.4 0.6 fusion.3
  25.0 0.6 fusion.5
  25.6 0.3 copy.192
  25.9 0.5 reshape.271
  26.4 0.0 copy-start.8
  26.4 0.4 fusion.6
  26.8 0.2 reshape.273
  27.0 0.1 copy.252
  27.2 0.2 broadcast_in_dim.146
  27.4 0.9 %reshape.274 = bf16[128,2,360]{2,1,0:T(2,128)(2,1)} reshape(bf16[16,8,720]{2,1,0:T(8,128)(2,1)S(1)} %broadcast_in_dim.147) | data formatting | bytes 368640 | tf_op jit(solution)/shard_map/reshape | solution.py:136
  28.3 7.6 %all-to-all-start.1 = ((bf16[128,2,360]{2,1,0:T(2,128)(2,1)}), bf16[128,2,360]{2,1,0:T(2,128)(2,1)S(1)}, u32[]{:S(2)}, u32[]{:S(2)}) async-start(bf16[128,2,360]{2,1,0:T(2,128)(2,1)} %reshape.274), calls=%async_computation.1 | async-start | bytes 393216 | tf_op jit(solution)/shard_map/all_to_all | solution.py:137
  35.9 9.9 %all-to-all-done.1 = bf16[128,2,360]{2,1,0:T(2,128)(2,1)S(1)} async-done(((bf16[128,2,360]{2,1,0:T(2,128)(2,1)}), bf16[128,2,360]{2,1,0:T(2,128)(2,1)S(1)}, u32[]{:S(2)}, u32[]{:S(2)}) %all-to-all-start.1) | async-done | bytes 184352 | tf_op jit(solution)/shard_map/all_to_all | solution.py:137
  45.8 0.6 reshape.275
  46.4 1.9 %fusion.2 = bf16[60,1536]{1,0:T(8,128)(2,1)S(1)} fusion(bf16[1536,60]{1,0:T(8,128)(2,1)S(1)} %reshape.275, s32[1536]{0:T(1024)S(1)} %fusion.51), kind=kOutput, calls=%fused_computation.5 | convolution fusion | flops 285566976 | bytes 374784 | tf_op jit(solution)/shard_map/kx,kj->xj/dot_general | solution.py:149
  48.3 0.1 reshape.278
  48.4 0.1 constant_dynamic-slice_fusion
  48.5 0.1 reshape.285
  48.6 0.7 pad.8.q_ref
  49.3 9.0 %shard_map.109 = f32[8,4,3,8,128]{4,3,2,1,0:T(8,128)} custom-call(bf16[4,8,1536]{2,1,0:T(8,128)(2,1)} %pad.8.q_ref, bf16[4,512,1536]{2,1,0:T(8,128)(2,1)} %k_ref.1, bf16[4,512,1536]{2,1,0:T(8,128)(2,1)} %v_ref.1, f32[4,24,512]{2,1,0:T(8,128)} %fusion.9.trail_ref, f32[4,192,1]{2,1,0:T(8,128)} %reshape.281.prefix_ref, ...), custom_call_target="tpu_custom_call" | custom-call | tf_op jit(solution)/shard_map/pallas_call | solution.py:71
  58.3 3.5 %all-to-all-start.2 = ((f32[8,4,3,8,128]{4,3,2,1,0:T(8,128)}), f32[8,4,3,8,128]{4,3,2,1,0:T(8,128)S(1)}, u32[]{:S(2)}, u32[]{:S(2)}) async-start(f32[8,4,3,8,128]{4,3,2,1,0:T(8,128)} %shard_map.109), calls=%async_computation.2 | async-start | bytes 786432 | tf_op jit(solution)/shard_map/all_to_all | solution.py:186
  61.7 0.1 reshape.284
  61.8 0.1 reshape.283
  61.9 0.1 fusion.27
  62.0 0.2 copy.210
  62.2 0.2 select_reduce_fusion.2
  62.4 9.5 %all-to-all-done.2 = f32[8,4,3,8,128]{4,3,2,1,0:T(8,128)S(1)} async-done(((f32[8,4,3,8,128]{4,3,2,1,0:T(8,128)}), f32[8,4,3,8,128]{4,3,2,1,0:T(8,128)S(1)}, u32[]{:S(2)}, u32[]{:S(2)}) %all-to-all-start.2) | async-done | bytes 393248 | tf_op jit(solution)/shard_map/all_to_all | solution.py:186
  71.8 0.2 slice.44
  72.0 0.2 copy.226
  72.2 0.1 select_reduce_fusion.1
  72.3 0.1 copy.199
  72.4 0.2 slice.43
  72.6 0.5 copy.200
  73.0 0.1 fusion.24
  73.1 0.1 copy.202
  73.2 0.2 fusion.68
  73.4 0.4 fusion.71
  73.8 0.9 %copy.227 = f32[8,4,3,5,1]{3,2,1,0,4:T(4,128)S(1)} copy(f32[8,4,3,5,1]{4,3,2,1,0:T(8,128)S(1)} %get-tuple-element.8) | data formatting | bytes 3840 | tf_op jit(solution)/shard_map/mul | solution.py:197
  74.7 0.5 copy.221
  75.2 0.2 fusion.22
  75.4 0.1 fusion.25
  75.5 0.2 fusion.11
  75.7 0.1 select_convert_fusion
  75.8 0.7 convert_element_type.56
  (34 shorter events, 0.3 us)
Async XLA Ops:
  0.0 8.8 %copy-start = (bf16[1536,24]{0,1:T(8,128)(2,1)S(1)}, bf16[1536,24]{0,1:T(8,128)(2,1)}, u32[]{:S(2)}) copy-start(bf16[1536,24]{0,1:T(8,128)(2,1)} %param.14) | copy-start | bytes 221188
  0.0 8.6 %copy-start.1 = (bf16[4,5,1536]{2,0,1:T(4,128)(2,1)S(1)}, bf16[4,5,1536]{2,0,1:T(4,128)(2,1)}, u32[]{:S(2)}) copy-start(bf16[4,5,1536]{2,0,1:T(4,128)(2,1)} %param.11) | copy-start | bytes 184324
  0.0 8.7 %copy-start.5 = (s32[4,8]{1,0:T(4,128)S(1)}, s32[4,8]{1,0:T(4,128)}, u32[]{:S(2)}) copy-start(s32[4,8]{1,0:T(4,128)} %param.20) | copy-start | bytes 388
  0.0 8.9 %copy-start.4 = (f32[1536]{0:T(1024)S(1)}, f32[1536]{0:T(1024)}, u32[]{:S(2)}) copy-start(f32[1536]{0:T(1024)} %param.12) | copy-start | bytes 18436
  0.0 8.9 %copy-start.7 = (f32[24]{0:T(128)S(1)}, f32[24]{0:T(128)}, u32[]{:S(2)}) copy-start(f32[24]{0:T(128)} %param.15) | copy-start | bytes 292
  0.0 9.1 %copy-start.6 = (s32[4]{0:T(128)S(1)}, s32[4]{0:T(128)}, u32[]{:S(2)}) copy-start(s32[4]{0:T(128)} %param.19) | copy-start | bytes 52
  0.0 9.2 %copy-start.2 = (f32[4,24,512]{2,1,0:T(8,128)S(1)}, f32[4,24,512]{2,1,0:T(8,128)}, u32[]{:S(2)}) copy-start(f32[4,24,512]{2,1,0:T(8,128)} %param.18) | copy-start | bytes 589828
  0.0 9.7 %copy-start.3 = (bf16[1536,3,3,4]{0,3,2,1:T(4,128)(2,1)S(1)}, bf16[1536,3,3,4]{0,3,2,1:T(4,128)(2,1)}, u32[]{:S(2)}) copy-start(bf16[1536,3,3,4]{0,3,2,1:T(4,128)(2,1)} %param.13) | copy-start | bytes 331780
  2.1 22.3 %all-to-all-start = ((bf16[16,4,5,1536]{3,1,2,0:T(4,128)(2,1)}), bf16[16,4,5,1536]{3,1,2,0:T(4,128)(2,1)S(1)}, u32[]{:S(2)}, u32[]{:S(2)}) async-start(bf16[16,4,5,1536]{3,1,2,0:T(4,128)(2,1)} %broadcast_in_dim.95), calls=%async_computation | async-start | bytes 1966080 | tf_op jit(solution)/shard_map/all_to_all | solution.py:114
  26.4 9.5 %copy-start.8 = (s32[4]{0:T(128)S(1)}, s32[4]{0:T(128)}, u32[]{:S(2)}) copy-start(s32[4]{0:T(128)} %param.21) | copy-start | bytes 52
  28.3 17.5 %all-to-all-start.1 = ((bf16[128,2,360]{2,1,0:T(2,128)(2,1)}), bf16[128,2,360]{2,1,0:T(2,128)(2,1)S(1)}, u32[]{:S(2)}, u32[]{:S(2)}) async-start(bf16[128,2,360]{2,1,0:T(2,128)(2,1)} %reshape.274), calls=%async_computation.1 | async-start | bytes 393216 | tf_op jit(solution)/shard_map/all_to_all | solution.py:137
  58.3 13.6 %all-to-all-start.2 = ((f32[8,4,3,8,128]{4,3,2,1,0:T(8,128)}), f32[8,4,3,8,128]{4,3,2,1,0:T(8,128)S(1)}, u32[]{:S(2)}, u32[]{:S(2)}) async-start(f32[8,4,3,8,128]{4,3,2,1,0:T(8,128)} %shard_map.109), calls=%async_computation.2 | async-start | bytes 786432 | tf_op jit(solution)/shard_map/all_to_all | solution.py:186

commit v16 on v13

--- a/solution.py
+++ b/solution.py
@@ -133,7 +133,7 @@
     )
     outgoing = jnp.broadcast_to(
         outgoing, (fsdp_count, seq_count, own_heads * own_dims * 3 * rows)
-    ).reshape(fsdp_count * seq_count, 2, own_heads * own_dims * 3 * rows // 2)
+    ).reshape(fsdp_count * seq_count, 6, own_heads * own_dims * 3 * rows // 6)
     incoming = lax.all_to_all(outgoing, ("fsdp", "seq"), 0, 0, tiled=True)
     incoming = incoming.reshape(fsdp_count * seq_count * own_heads * own_dims, 3 * rows)
     src_row = jnp.arange(fsdp_count * seq_count * own_heads * own_dims, dtype=jnp.int32)

time: 76.9 us -> 77.2 us (level)
  no operation moved by 1% of the time
where the time goes in v16:
time: 77.2 us; the launch traced here: 76.8 us
  waiting for transfers between devices  30.7 us (40%)
  starting transfers between devices  17.5 us (23%)
  local copies, waits for them, and re-layouts  11.5 us (15%)
  Pallas kernels  8.98 us (12%)
  other arithmetic  3.92 us (5%)
  matrix products  3.87 us (5%)
    all_to_all x1, waiting for transfers between devices, body(): lax.all_to_all(jnp.broadcast_to(hidden_in[None], (fsdp_count, req_count,...  10.7 us
    all_to_all x1, waiting for transfers between devices, body(): incoming = lax.all_to_all(outgoing, ('fsdp', 'seq'), 0, 0, tiled=True)  10.5 us
    all_to_all x1, waiting for transfers between devices, body(): parts = lax.all_to_all(packed, 'seq', 0, 0, tiled=True)[:, :, :, :new_count]  9.44 us
    pallas_call x1, Pallas kernels, piece_attention(): pl.pallas_call(attention_kernel, grid=(req_count,), in_specs=[pl.BlockSpe...  8.98 us
    all_to_all x1, starting transfers between devices, body(): incoming = lax.all_to_all(outgoing, ('fsdp', 'seq'), 0, 0, tiled=True)  7.58 us
    all_to_all x1, starting transfers between devices, body(): lax.all_to_all(jnp.broadcast_to(hidden_in[None], (fsdp_count, req_count,...  6.44 us
    all_to_all x1, starting transfers between devices, body(): parts = lax.all_to_all(packed, 'seq', 0, 0, tiled=True)[:, :, :, :new_count]  3.45 us
    broadcast_in_dim x1, local copies, waits for them, and re-layouts, body(): jnp.broadcast_to(hidden_in[None], (fsdp_count, req_count, new_count, width))  2.08 us
  transfers between devices with their start and end apart: 3, of which 3 were waited for; matrix products, arithmetic and copies ran while one was open for 7% of the time, Pallas kernels for 0%

profile of v16, /device:TPU:0, one launch (start us, length us, event | category | flops | bytes accessed | tf_op | source)
XLA Modules:
  0.0 76.8 jit_solution(8467562891467382166)
XLA Ops:
  0.1 2.1 %broadcast_in_dim.95 = bf16[16,4,5,1536]{3,1,2,0:T(4,128)(2,1)} broadcast(bf16[4,5,1536]{2,0,1:T(4,128)(2,1)} %param.11), dimensions={1,2,3} | broadcast | bytes 1044480 | tf_op jit(solution)/shard_map/broadcast_in_dim | solution.py:115
  2.1 6.4 %all-to-all-start = ((bf16[16,4,5,1536]{3,1,2,0:T(4,128)(2,1)}), bf16[16,4,5,1536]{3,1,2,0:T(4,128)(2,1)S(1)}, u32[]{:S(2)}, u32[]{:S(2)}) async-start(bf16[16,4,5,1536]{3,1,2,0:T(4,128)(2,1)} %broadcast_in_dim.95), calls=%async_computation | async-start | bytes 1966080 | tf_op jit(solution)/shard_map/all_to_all | solution.py:114
  8.6 0.1 fusion.13
  8.7 0.1 select_reduce_fusion.4
  8.9 0.3 fusion.65
  9.2 0.1 add_compare_fusion
  9.3 0.0 copy-done.2
  9.3 0.1 select_reduce_fusion
  9.4 0.1 dynamic-slice_bitcast_fusion
  9.5 0.1 copy.212
  9.6 0.1 copy.211
  9.7 0.0 copy-done.3
  9.7 0.1 copy.236
  9.9 0.9 %reshape.281.prefix_ref = f32[4,192,1]{2,1,0:T(8,128)} reshape(f32[4,24,8]{2,1,0:T(8,128)S(1)} %pad.9.clone) | data formatting | bytes 6144 | tf_op jit(solution)/shard_map/reshape | solution.py:176
  10.8 0.1 broadcast_in_dim.152
  10.9 0.9 %reshape.282.total_ref = f32[4,192,1]{2,1,0:T(8,128)} reshape(f32[4,24,8]{2,1,0:T(8,128)S(1)} %broadcast_in_dim.152) | data formatting | bytes 6144 | tf_op jit(solution)/shard_map/reshape | solution.py:182
  11.8 0.1 select_reduce_fusion.3
  11.9 0.1 broadcast_compare_fusion
  12.0 0.7 compare_convert_fusion.live_ref
  12.7 1.0 %fusion.9.trail_ref = f32[4,24,512]{2,1,0:T(8,128)} fusion(f32[4,24,512]{2,1,0:T(8,128)S(1)} %copy-done.2, pred[4,512]{1,0:T(4,128)(4,1)S(1)} %add_compare_fusion), kind=kOutput, calls=%fused_computation.15 | convolution fusion | flops 302301184 | bytes 395264 | tf_op jit(solution)/shard_map/rhl,lj->rhj/dot_general | solution.py:169
  13.7 10.7 %all-to-all-done = bf16[16,4,5,1536]{3,1,2,0:T(4,128)(2,1)S(1)} async-done(((bf16[16,4,5,1536]{3,1,2,0:T(4,128)(2,1)}), bf16[16,4,5,1536]{3,1,2,0:T(4,128)(2,1)S(1)}, u32[]{:S(2)}, u32[]{:S(2)}) %all-to-all-start) | async-done | bytes 983072 | tf_op jit(solution)/shard_map/all_to_all | solution.py:114
  24.4 0.6 fusion.3
  25.0 0.6 fusion.5
  25.6 0.3 copy.192
  25.9 0.5 reshape.271
  26.4 0.0 copy-start.8
  26.4 0.4 fusion.6
  26.8 0.2 reshape.273
  27.0 0.1 copy.252
  27.2 0.2 broadcast_in_dim.146
  27.4 0.9 %reshape.274 = bf16[128,6,120]{2,1,0:T(8,128)(2,1)} reshape(bf16[16,8,720]{2,1,0:T(8,128)(2,1)S(1)} %broadcast_in_dim.147) | data formatting | bytes 368640 | tf_op jit(solution)/shard_map/reshape | solution.py:136
  28.3 7.6 %all-to-all-start.1 = ((bf16[128,6,120]{2,1,0:T(8,128)(2,1)}), bf16[128,6,120]{2,1,0:T(8,128)(2,1)S(1)}, u32[]{:S(2)}, u32[]{:S(2)}) async-start(bf16[128,6,120]{2,1,0:T(8,128)(2,1)} %reshape.274), calls=%async_computation.1 | async-start | bytes 524288 | tf_op jit(solution)/shard_map/all_to_all | solution.py:137
  35.9 10.5 %all-to-all-done.1 = bf16[128,6,120]{2,1,0:T(8,128)(2,1)S(1)} async-done(((bf16[128,6,120]{2,1,0:T(8,128)(2,1)}), bf16[128,6,120]{2,1,0:T(8,128)(2,1)S(1)}, u32[]{:S(2)}, u32[]{:S(2)}) %all-to-all-start.1) | async-done | bytes 184352 | tf_op jit(solution)/shard_map/all_to_all | solution.py:137
  46.4 0.2 reshape.275
  46.7 1.9 %fusion.2 = bf16[60,1536]{1,0:T(8,128)(2,1)S(1)} fusion(bf16[1536,60]{1,0:T(8,128)(2,1)S(1)} %reshape.275, s32[1536]{0:T(1024)S(1)} %fusion.51), kind=kOutput, calls=%fused_computation.5 | convolution fusion | flops 285566976 | bytes 374784 | tf_op jit(solution)/shard_map/kx,kj->xj/dot_general | solution.py:149
  48.6 0.1 reshape.278
  48.7 0.1 constant_dynamic-slice_fusion
  48.8 0.1 reshape.285
  49.0 0.7 pad.8.q_ref
  49.6 9.0 %shard_map.109 = f32[8,4,3,8,128]{4,3,2,1,0:T(8,128)} custom-call(bf16[4,8,1536]{2,1,0:T(8,128)(2,1)} %pad.8.q_ref, bf16[4,512,1536]{2,1,0:T(8,128)(2,1)} %k_ref.1, bf16[4,512,1536]{2,1,0:T(8,128)(2,1)} %v_ref.1, f32[4,24,512]{2,1,0:T(8,128)} %fusion.9.trail_ref, f32[4,192,1]{2,1,0:T(8,128)} %reshape.281.prefix_ref, ...), custom_call_target="tpu_custom_call" | custom-call | tf_op jit(solution)/shard_map/pallas_call | solution.py:71
  58.6 3.5 %all-to-all-start.2 = ((f32[8,4,3,8,128]{4,3,2,1,0:T(8,128)}), f32[8,4,3,8,128]{4,3,2,1,0:T(8,128)S(1)}, u32[]{:S(2)}, u32[]{:S(2)}) async-start(f32[8,4,3,8,128]{4,3,2,1,0:T(8,128)} %shard_map.109), calls=%async_computation.2 | async-start | bytes 786432 | tf_op jit(solution)/shard_map/all_to_all | solution.py:186
  62.0 0.1 reshape.284
  62.1 0.1 reshape.283
  62.2 0.1 fusion.27
  62.4 0.2 copy.210
  62.5 0.2 select_reduce_fusion.2
  62.7 9.4 %all-to-all-done.2 = f32[8,4,3,8,128]{4,3,2,1,0:T(8,128)S(1)} async-done(((f32[8,4,3,8,128]{4,3,2,1,0:T(8,128)}), f32[8,4,3,8,128]{4,3,2,1,0:T(8,128)S(1)}, u32[]{:S(2)}, u32[]{:S(2)}) %all-to-all-start.2) | async-done | bytes 393248 | tf_op jit(solution)/shard_map/all_to_all | solution.py:186
  72.1 0.2 slice.44
  72.3 0.2 copy.226
  72.5 0.1 select_reduce_fusion.1
  72.6 0.1 copy.199
  72.7 0.2 slice.43
  72.9 0.5 copy.200
  73.3 0.1 fusion.24
  73.4 0.1 copy.202
  73.5 0.2 fusion.68
  73.7 0.4 fusion.71
  74.1 0.9 %copy.227 = f32[8,4,3,5,1]{3,2,1,0,4:T(4,128)S(1)} copy(f32[8,4,3,5,1]{4,3,2,1,0:T(8,128)S(1)} %get-tuple-element.8) | data formatting | bytes 3840 | tf_op jit(solution)/shard_map/mul | solution.py:197
  75.0 0.5 copy.221
  75.5 0.2 fusion.22
  75.7 0.1 fusion.25
  75.8 0.2 fusion.11
  76.0 0.1 select_convert_fusion
  76.1 0.7 convert_element_type.56
  (34 shorter events, 0.3 us)
Async XLA Ops:
  0.0 8.8 %copy-start = (bf16[1536,24]{0,1:T(8,128)(2,1)S(1)}, bf16[1536,24]{0,1:T(8,128)(2,1)}, u32[]{:S(2)}) copy-start(bf16[1536,24]{0,1:T(8,128)(2,1)} %param.14) | copy-start | bytes 221188
  0.0 8.6 %copy-start.1 = (bf16[4,5,1536]{2,0,1:T(4,128)(2,1)S(1)}, bf16[4,5,1536]{2,0,1:T(4,128)(2,1)}, u32[]{:S(2)}) copy-start(bf16[4,5,1536]{2,0,1:T(4,128)(2,1)} %param.11) | copy-start | bytes 184324
  0.0 8.7 %copy-start.5 = (s32[4,8]{1,0:T(4,128)S(1)}, s32[4,8]{1,0:T(4,128)}, u32[]{:S(2)}) copy-start(s32[4,8]{1,0:T(4,128)} %param.20) | copy-start | bytes 388
  0.0 8.9 %copy-start.4 = (f32[1536]{0:T(1024)S(1)}, f32[1536]{0:T(1024)}, u32[]{:S(2)}) copy-start(f32[1536]{0:T(1024)} %param.12) | copy-start | bytes 18436
  0.0 8.9 %copy-start.7 = (f32[24]{0:T(128)S(1)}, f32[24]{0:T(128)}, u32[]{:S(2)}) copy-start(f32[24]{0:T(128)} %param.15) | copy-start | bytes 292
  0.0 9.1 %copy-start.6 = (s32[4]{0:T(128)S(1)}, s32[4]{0:T(128)}, u32[]{:S(2)}) copy-start(s32[4]{0:T(128)} %param.19) | copy-start | bytes 52
  0.0 9.2 %copy-start.2 = (f32[4,24,512]{2,1,0:T(8,128)S(1)}, f32[4,24,512]{2,1,0:T(8,128)}, u32[]{:S(2)}) copy-start(f32[4,24,512]{2,1,0:T(8,128)} %param.18) | copy-start | bytes 589828
  0.0 9.7 %copy-start.3 = (bf16[1536,3,3,4]{0,3,2,1:T(4,128)(2,1)S(1)}, bf16[1536,3,3,4]{0,3,2,1:T(4,128)(2,1)}, u32[]{:S(2)}) copy-start(bf16[1536,3,3,4]{0,3,2,1:T(4,128)(2,1)} %param.13) | copy-start | bytes 331780
  2.1 22.3 %all-to-all-start = ((bf16[16,4,5,1536]{3,1,2,0:T(4,128)(2,1)}), bf16[16,4,5,1536]{3,1,2,0:T(4,128)(2,1)S(1)}, u32[]{:S(2)}, u32[]{:S(2)}) async-start(bf16[16,4,5,1536]{3,1,2,0:T(4,128)(2,1)} %broadcast_in_dim.95), calls=%async_computation | async-start | bytes 1966080 | tf_op jit(solution)/shard_map/all_to_all | solution.py:114
  26.4 9.5 %copy-start.8 = (s32[4]{0:T(128)S(1)}, s32[4]{0:T(128)}, u32[]{:S(2)}) copy-start(s32[4]{0:T(128)} %param.21) | copy-start | bytes 52
  28.3 18.1 %all-to-all-start.1 = ((bf16[128,6,120]{2,1,0:T(8,128)(2,1)}), bf16[128,6,120]{2,1,0:T(8,128)(2,1)S(1)}, u32[]{:S(2)}, u32[]{:S(2)}) async-start(bf16[128,6,120]{2,1,0:T(8,128)(2,1)} %reshape.274), calls=%async_computation.1 | async-start | bytes 524288 | tf_op jit(solution)/shard_map/all_to_all | solution.py:137
  58.6 13.5 %all-to-all-start.2 = ((f32[8,4,3,8,128]{4,3,2,1,0:T(8,128)}), f32[8,4,3,8,128]{4,3,2,1,0:T(8,128)S(1)}, u32[]{:S(2)}, u32[]{:S(2)}) async-start(f32[8,4,3,8,128]{4,3,2,1,0:T(8,128)} %shard_map.109), calls=%async_computation.2 | async-start | bytes 786432 | tf_op jit(solution)/shard_map/all_to_all | solution.py:186
